TPU v7x, 32 devices: a whole 2x2x4 slice. The times are simulated.
32 devices in a mesh: gz: 4 (over z), xy: 8 (over y, x, core).
Axes of the slice: x: 2, y: 2, z: 4, core: 2. Of those that a mesh axis runs over, the one named last changes fastest.
Arguments:
- tile_image: bfloat16 [4, 8, 4, 4, 2, 128], P('gz', 'xy'), may hold values from -6 to 6
- tile_target: bfloat16 [4, 8, 4, 3, 4, 2, 128], P('gz', 'xy'), may hold values from 0 to 1
- owner_counts: int32 [4, 8], P('gz', 'xy'), may hold values from 0 to 4, as said below
- tile_list: int32 [4, 8, 4], P('gz', 'xy'), may hold values from -1 to 15, as said below
- w_in: bfloat16 [27, 32], replicated, may hold values from -1.25 to 1.25
- w_res: bfloat16 [27, 32, 32], replicated, may hold values from -0.21875 to 0.21875
- w_down: bfloat16 [8, 64, 32], replicated, may hold values from -0.375 to 0.375
- w_mid: bfloat16 [27, 64, 64], replicated, may hold values from -0.15625 to 0.15625
- w_up: bfloat16 [8, 32, 64], replicated, may hold values from -0.75 to 0.75
- head_weight: bfloat16 [3, 32], replicated, may hold values from -1 to 1
Outputs:
- err_tiles: bfloat16 [4, 8, 4, 3, 4, 2, 128], P('gz', 'xy')
- grad_in: float32 [27, 32], replicated
- grad_res: float32 [27, 32, 32], replicated
- grad_down: float32 [8, 64, 32], replicated
- grad_mid: float32 [27, 64, 64], replicated
- grad_up: float32 [8, 32, 64], replicated
- head_weight_gradient: float32 [3, 32], replicated
Inputs may be any that keep to these rules, and one draw needn't show every extreme that they name: `owner_counts`: in each depth row the counts add up to 16, and some owner of every row holds exactly 4 tiles. `tile_list`: in each depth row the live slots (s < owner_counts) name every position 0 to 15 exactly once; the other slots hold -1.
All inputs are finite; a program needn't handle non-finite values.
Results may differ from a plain program's by a relative error of at most 0.0046.
Values may be sent and summed in bfloat16 or wider, within the bound.
No kernel may reach another device: no remote copies, remote signals or barrier semaphores. Data moves between devices by JAX's collectives and lax.ppermute only.
A program may use at most 64 MiB of HBM per device.

v0:
```python
import jax
import jax.numpy as jnp
from jax import lax
from jax.sharding import PartitionSpec as P

TPD = 2


def with_halo(cells, sides, width):
    for axis, dim in sides:
        count = lax.axis_size(axis)
        ends = count - 1
        head = lax.slice_in_dim(cells, 0, width, axis=dim)
        tail = lax.slice_in_dim(cells, cells.shape[dim] - width, cells.shape[dim], axis=dim)
        cells = jnp.concatenate(
            [
                lax.ppermute(tail, axis, [(i, (i + 1) % count) for i in range(ends)]),
                cells,
                lax.ppermute(head, axis, [((i + 1) % count, i) for i in range(ends)]),
            ],
            axis=dim,
        )
    return cells


def framed(field):
    padded = with_halo(field, (("gz", 1), ("xy", 3)), 1)
    return jnp.pad(padded, ((0, 0), (0, 0), (1, 1), (0, 0)))


def convolve(padded, weights):
    depth = padded.shape[1] - 2
    height = padded.shape[2] - 2
    width = padded.shape[3] - 2
    total = None
    for tap in range(27):
        off_z, off_y, off_x = (tap // 9, tap // 3 % 3, tap % 3)
        window = padded[:, off_z : off_z + depth, off_y : off_y + height, off_x : off_x + width]
        term = jnp.einsum("oc,czyx->ozyx", weights[tap], window, preferred_element_type=jnp.float32)
        total = term if total is None else total + term
    return total


def tap_grads(grad, padded):
    depth, height, width = grad.shape[1:]
    terms = []
    for tap in range(27):
        off_z, off_y, off_x = (tap // 9, tap // 3 % 3, tap % 3)
        window = padded[:, off_z : off_z + depth, off_y : off_y + height, off_x : off_x + width]
        terms.append(jnp.einsum("ozyx,czyx->oc", grad, window, preferred_element_type=jnp.float32))
    return jnp.stack(terms)


def flipped(weights):
    return jnp.transpose(weights[::-1], (0, 2, 1))


def strided(field, tap):
    return field[:, tap // 4 :: 2, tap // 2 % 2 :: 2, tap % 2 :: 2]


def alternate(parts):
    chans, depth, height, width = parts.shape[1:]
    return (
        parts.reshape(2, 2, 2, chans, depth, height, width)
        .transpose(3, 4, 0, 5, 1, 6, 2)
        .reshape(chans, 2 * depth, 2 * height, 2 * width)
    )


def local(
    tile_image, tile_target, owner_counts, tile_list, w_in, w_res, w_down, w_mid, w_up, head_weight
):
    single_float = jnp.float32
    brain_float_half = jnp.bfloat16
    ranks = lax.axis_size("xy")
    layers = lax.axis_size("gz")
    column = lax.axis_index("xy")
    slots = tile_list.shape[2]
    depth, height, width = (tile_image.shape[3], tile_image.shape[4], tile_image.shape[5])
    per_dev = TPD
    total_tiles = ranks * per_dev
    slot_list = tile_list[0, 0]
    live = jnp.arange(slots) < owner_counts[0, 0]
    select = ((slot_list[None, :] == jnp.arange(total_tiles)[:, None]) & live[None, :]).astype(
        brain_float_half
    )
    wanted = column * per_dev + jnp.arange(per_dev)
    piece_img = lax.all_gather(tile_image, "xy", axis=1, tiled=True)
    piece_tgt = lax.all_gather(tile_target, "xy", axis=1, tiled=True)
    piece_cnt = lax.all_gather(owner_counts, "xy", axis=1, tiled=True)
    piece_list = lax.all_gather(tile_list, "xy", axis=1, tiled=True)
    owners = piece_list.shape[1]
    piece_live = jnp.arange(slots)[None, :] < piece_cnt[0][:, None]
    match = ((piece_list[0][:, :, None] == wanted[None, None, :]) & piece_live[:, :, None]).astype(
        brain_float_half
    )
    acc_img = jnp.einsum(
        "kst,kszyx->tzyx", match, piece_img[0], preferred_element_type=single_float
    )
    acc_tgt = jnp.einsum(
        "kst,ksazyx->tazyx", match, piece_tgt[0], preferred_element_type=single_float
    )
    rows_hit = (jnp.arange(ranks)[:, None] == jnp.arange(owners)[None, :]).astype(single_float)
    acc_hit = jnp.dot(rows_hit, jnp.sum(match.astype(single_float), axis=1))
    acc_img, acc_tgt, acc_hit = (acc_img, acc_tgt, acc_hit)
    mine_img = acc_img.astype(brain_float_half)
    mine_tgt = acc_tgt.astype(brain_float_half)
    owner_hit = acc_hit.astype(brain_float_half)
    image = mine_img.transpose(1, 2, 0, 3).reshape(1, depth, height, per_dev * width)
    target = mine_tgt.transpose(1, 2, 3, 0, 4).reshape(3, depth, height, per_dev * width)
    voxel_cells = depth * height * per_dev * width * ranks * layers
    image_pad = framed(image)
    h0 = jax.nn.relu(convolve(image_pad, w_in[:, :, None])).astype(brain_float_half)
    h0_pad = framed(h0)
    h1 = jax.nn.relu(h0.astype(single_float) + convolve(h0_pad, w_res)).astype(brain_float_half)
    down_sum = None
    for tap in range(8):
        term = jnp.einsum(
            "oc,czyx->ozyx", w_down[tap], strided(h1, tap), preferred_element_type=single_float
        )
        down_sum = term if down_sum is None else down_sum + term
    dfield = jax.nn.relu(down_sum).astype(brain_float_half)
    dfield_pad = framed(dfield)
    cfield = jax.nn.relu(dfield.astype(single_float) + convolve(dfield_pad, w_mid)).astype(
        brain_float_half
    )
    upward = alternate(
        jnp.stack(
            [
                jnp.einsum("oc,czyx->ozyx", w_up[tap], cfield, preferred_element_type=single_float)
                for tap in range(8)
            ]
        )
    )
    signal_field = jax.nn.relu(h1.astype(single_float) + upward).astype(brain_float_half)
    logits = jnp.einsum(
        "ac,czyx->azyx", head_weight, signal_field, preferred_element_type=single_float
    )
    affinity_map = jax.nn.sigmoid(logits)
    error_field = affinity_map - target.astype(single_float)
    err_out = error_field.astype(brain_float_half)
    err_local = err_out.reshape(3, depth, height, per_dev, width).transpose(3, 0, 1, 2, 4)
    sending = owner_hit[:, :, None, None, None, None] * err_local[None]
    returned = lax.all_to_all(sending, "xy", split_axis=0, concat_axis=0, tiled=True)
    returned = returned.reshape((total_tiles, 3, depth, height, width))
    err_tiles = jnp.einsum(
        "ps,pazyx->sazyx", select, returned, preferred_element_type=single_float
    ).astype(brain_float_half)[None, None]
    logit_gradient = (error_field * affinity_map * (1.0 - affinity_map) / voxel_cells).astype(
        brain_float_half
    )
    head_weight_gradient = jnp.einsum(
        "mtnq,btnq->mb", logit_gradient, signal_field, preferred_element_type=single_float
    )
    gradient_total = jnp.einsum(
        "jn,jbrq->nbrq", head_weight, logit_gradient, preferred_element_type=single_float
    )
    gsf = jnp.where(signal_field > 0, gradient_total, 0.0).astype(brain_float_half)
    grad_up = jnp.stack(
        [
            jnp.einsum(
                "ozyx,czyx->oc", strided(gsf, tap), cfield, preferred_element_type=single_float
            )
            for tap in range(8)
        ]
    )
    gcoarse = None
    for tap in range(8):
        term = jnp.einsum(
            "oc,ozyx->czyx", w_up[tap], strided(gsf, tap), preferred_element_type=single_float
        )
        gcoarse = term if gcoarse is None else gcoarse + term
    gquad = jnp.where(cfield > 0, gcoarse, 0.0).astype(brain_float_half)
    grad_mid = tap_grads(gquad, dfield_pad)
    gdown = gquad.astype(single_float) + convolve(framed(gquad), flipped(w_mid))
    gdd = jnp.where(dfield > 0, gdown, 0.0).astype(brain_float_half)
    grad_down = jnp.stack(
        [
            jnp.einsum("ozyx,czyx->oc", gdd, strided(h1, tap), preferred_element_type=single_float)
            for tap in range(8)
        ]
    )
    spread = alternate(
        jnp.stack(
            [
                jnp.einsum("oc,ozyx->czyx", w_down[tap], gdd, preferred_element_type=single_float)
                for tap in range(8)
            ]
        )
    )
    gres = jnp.where(h1 > 0, gsf.astype(single_float) + spread, 0.0).astype(brain_float_half)
    grad_res = tap_grads(gres, h0_pad)
    gfirst = gres.astype(single_float) + convolve(framed(gres), flipped(w_res))
    gact = jnp.where(h0 > 0, gfirst, 0.0).astype(brain_float_half)
    grad_in = tap_grads(gact, image_pad)[:, :, 0]
    summed = lax.psum(
        (grad_in, grad_res, grad_down, grad_mid, grad_up, head_weight_gradient), ("gz", "xy")
    )
    return (err_tiles, summed[0], summed[1], summed[2], summed[3], summed[4], summed[5])


def solution(mesh):
    return jax.shard_map(
        local,
        mesh=mesh,
        in_specs=(
            P("gz", "xy", None, None, None, None),
            P("gz", "xy", None, None, None, None, None),
            P("gz", "xy"),
            P("gz", "xy", None),
            P(),
            P(),
            P(),
            P(),
            P(),
            P(),
        ),
        out_specs=(P("gz", "xy", None, None, None, None, None), P(), P(), P(), P(), P(), P()),
        check_vma=False,
    )
```

profile of v0, /device:TPU:0, one launch (start us, length us, event | category | flops | bytes accessed | tf_op | source)
XLA Modules:
  0.0 325.3 jit_solution(603947522372132895)
XLA Ops:
  9.8 9.5 %all-reduce.3 = s32[8]{0:T(128)S(1)} all-reduce(s32[8]{0:T(128)S(1)} %bitcast_dynamic-update-slice_fusion), channel_id=1, replica_groups=mesh['gz'=4,'xy'=8] {'xy'}, use_global_device_ids=true, to_apply=%add.3 | all-reduce | flops 8 | bytes 64
  19.3 8.1 %all_gather.12 = s32[1,8,4]{2,0,1:T(1,128)S(1)} all-gather(s32[1,1,4]{2,0,1:T(1,128)} %bitcast.2102), channel_id=1, replica_groups=mesh['gz'=4,'xy'=8] {'xy'}, dimensions={1}, use_global_device_ids=true | all-gather | bytes 144 | tf_op jit(solution)/shard_map/all_gather | solution.py:92
  28.2 8.9 %all_gather.14 = bf16[1,8,4,4,2,128]{5,3,4,2,0,1:T(4,128)(2,1)S(1)} all-gather(bf16[1,1,4,4,2,128]{5,3,4,2,0,1:T(4,128)(2,1)S(1)} %copy.229), channel_id=1, replica_groups=mesh['gz'=4,'xy'=8] {'xy'}, dimensions={1}, use_global_device_ids=true | all-gather | bytes 73728 | tf_op jit(solution)/shard_map/all_gather | solution.py:89
  37.4 3.5 %collective-permute-start = (bf16[1,1,2,256]{3,2,1,0:T(2,128)(2,1)S(1)}, bf16[1,1,2,256]{3,2,1,0:T(2,128)(2,1)S(1)}, u32[]{:S(2)}, u32[]{:S(2)}) collective-permute-start(bf16[1,1,2,256]{3,2,1,0:T(2,128)(2,1)S(1)} %get-tuple-element.194), channel_id=1, source_target_pairs={{0,8},{8,16},{16,24},{1,9},{9,17},{17,25},{2,10},{10,18},{18,26},{... | collective-permute-start | bytes 3080 | tf_op jit(solution)/shard_map/ppermute | solution.py:17
  50.6 8.6 %all_gather.15 = bf16[1,8,4,3,4,2,128]{6,4,5,3,2,0,1:T(4,128)(2,1)S(1)} all-gather(bf16[1,1,4,3,4,2,128]{6,4,5,3,2,0,1:T(4,128)(2,1)S(1)} %copy.234), channel_id=1, replica_groups=mesh['gz'=4,'xy'=8] {'xy'}, dimensions={1}, use_global_device_ids=true | all-gather | bytes 221184 | tf_op jit(solution)/shard_map/all_gather | solution.py:90
  63.3 2.2 collective-permute-start.2
  66.8 2.2 collective-permute-done.3
  71.3 4.5 %collective-permute-start.4 = (bf16[32,1,2,256]{3,0,2,1:T(8,128)(2,1)S(1)}, bf16[32,1,2,256]{3,0,2,1:T(8,128)(2,1)S(1)}, u32[]{:S(2)}, u32[]{:S(2)}) collective-permute-start(bf16[32,1,2,256]{3,0,2,1:T(8,128)(2,1)S(1)} %get-tuple-element.91), channel_id=1, source_target_pairs={{0,8},{8,16},{16,24},{1,9},{9,17},{17,25},{2,10},{10,18},{18,26},{... | collective-permute-start | bytes 98312 | tf_op jit(solution)/shard_map/ppermute | solution.py:17
  77.5 4.2 %collective-permute-done.5 = bf16[32,1,2,256]{3,0,2,1:T(8,128)(2,1)S(1)} collective-permute-done((bf16[32,1,2,256]{3,0,2,1:T(8,128)(2,1)S(1)}, bf16[32,1,2,256]{3,0,2,1:T(8,128)(2,1)S(1)}, u32[]{:S(2)}, u32[]{:S(2)}) %collective-permute-start.5) | collective-permute-done | bytes 32800 | tf_op jit(solution)/shard_map/ppermute | solution.py:19
  81.8 2.8 collective-permute-start.6
  86.2 2.6 collective-permute-done.7
  105.3 3.5 %collective-permute-start.8 = (bf16[64,1,1,128]{3,0,1,2:T(8,128)(2,1)S(1)}, bf16[64,1,1,128]{3,0,1,2:T(8,128)(2,1)S(1)}, u32[]{:S(2)}, u32[]{:S(2)}) collective-permute-start(bf16[64,1,1,128]{3,0,1,2:T(8,128)(2,1)S(1)} %get-tuple-element.101), channel_id=1, source_target_pairs={{0,8},{8,16},{16,24},{1,9},{9,17},{17,25},{2,10},{10,18},{18,26},{... | collective-permute-start | bytes 49160 | tf_op jit(solution)/shard_map/ppermute | solution.py:17
  110.2 4.2 %collective-permute-done.9 = bf16[64,1,1,128]{3,0,1,2:T(8,128)(2,1)S(1)} collective-permute-done((bf16[64,1,1,128]{3,0,1,2:T(8,128)(2,1)S(1)}, bf16[64,1,1,128]{3,0,1,2:T(8,128)(2,1)S(1)}, u32[]{:S(2)}, u32[]{:S(2)}) %collective-permute-start.9) | collective-permute-done | bytes 16416 | tf_op jit(solution)/shard_map/ppermute | solution.py:19
  114.6 3.7 %collective-permute-start.10 = (bf16[64,4,1,1]{3,0,1,2:T(8,128)(2,1)S(1)}, bf16[64,4,1,1]{3,0,1,2:T(8,128)(2,1)S(1)}, u32[]{:S(2)}, u32[]{:S(2)}) collective-permute-start(bf16[64,4,1,1]{3,0,1,2:T(8,128)(2,1)S(1)} %get-tuple-element.95), channel_id=1, source_target_pairs={{0,1},{1,2},{2,3},{3,4},{4,5},{5,6},{6,7},{8,9},{9,10},{10,11},{11... | collective-permute-start | bytes 1544 | tf_op jit(solution)/shard_map/ppermute | solution.py:17
  119.9 2.4 collective-permute-done.11
  138.8 3.5 %collective-permute-start.12 = (bf16[64,1,1,128]{3,0,1,2:T(8,128)(2,1)S(1)}, bf16[64,1,1,128]{3,0,1,2:T(8,128)(2,1)S(1)}, u32[]{:S(2)}, u32[]{:S(2)}) collective-permute-start(bf16[64,1,1,128]{3,0,1,2:T(8,128)(2,1)S(1)} %get-tuple-element.99), channel_id=1, source_target_pairs={{0,8},{8,16},{16,24},{1,9},{9,17},{17,25},{2,10},{10,18},{18,26},{... | collective-permute-start | bytes 49160 | tf_op jit(solution)/shard_map/ppermute | solution.py:17
  144.4 7.7 %all-to-all-start = ((bf16[8,2,3,4,2,128]{5,1,4,3,2,0:T(2,128)(2,1)}), bf16[8,2,3,4,2,128]{5,1,4,3,2,0:T(2,128)(2,1)S(1)}, u32[]{:S(2)}, u32[]{:S(2)}) async-start(bf16[8,2,3,4,2,128]{5,1,4,3,2,0:T(2,128)(2,1)} %broadcast_multiply_fusion), calls=%async_computation | async-start | bytes 196608 | tf_op jit(solution)/shard_map/all_to_all | solution.py:145
  153.6 3.0 collective-permute-start.14
  167.8 4.3 %collective-permute-start.16 = (bf16[32,1,2,256]{3,0,2,1:T(8,128)(2,1)S(1)}, bf16[32,1,2,256]{3,0,2,1:T(8,128)(2,1)S(1)}, u32[]{:S(2)}, u32[]{:S(2)}) collective-permute-start(bf16[32,1,2,256]{3,0,2,1:T(8,128)(2,1)S(1)} %get-tuple-element.81), channel_id=1, source_target_pairs={{0,8},{8,16},{16,24},{1,9},{9,17},{17,25},{2,10},{10,18},{18,26},{... | collective-permute-start | bytes 98312 | tf_op jit(solution)/shard_map/ppermute | solution.py:17
  175.1 2.8 collective-permute-done.17
  178.0 2.6 collective-permute-start.18
  182.1 5.0 %collective-permute-done.19 = bf16[32,6,2,1]{3,0,2,1:T(8,128)(2,1)S(1)} collective-permute-done((bf16[32,6,2,1]{3,0,2,1:T(8,128)(2,1)S(1)}, bf16[32,6,2,1]{3,0,2,1:T(8,128)(2,1)S(1)}, u32[]{:S(2)}, u32[]{:S(2)}) %collective-permute-start.19) | collective-permute-done | bytes 800 | tf_op jit(solution)/shard_map/ppermute | solution.py:19
  197.3 44.9 %all-reduce.4 = (f32[27,32]{1,0:T(8,128)}, f32[3,32]{1,0:T(4,128)}) all-reduce(f32[27,32]{1,0:T(8,128)S(1)} %bitcast.2093, f32[3,32]{1,0:T(4,128)S(1)} %copy-done.95), channel_id=1, replica_groups=mesh['gz'=4,'xy'=8] {'gz','xy'}, use_global_device_ids=true, to_apply=%region_1.2 | all-reduce | flops 960 | bytes 7680 | tf_op jit(solution)/shard_map/psum | solution.py:197
  243.1 70.2 %all-reduce.8.cloned.1.call-done = (f32[27,32,32]{2,1,0:T(8,128)}, f32[8,64,32]{1,2,0:T(8,128)}, f32[27,64,64]{2,1,0:T(8,128)}, f32[8,32,64]{2,1,0:T(8,128)}) async-done(((f32[27,32,32]{2,1,0:T(8,128)}, f32[8,64,32]{1,2,0:T(8,128)}, f32[27,64,64]{2,1,0:T(8,128)}, f32[8,32,64]{2,1,0:T(8,128)}), (f32[27,32,32]{2,1,0:T(8,128)}, f32[8,64,32]{1,2,0:T(8,128)}, f32[27,64,64]{2,1,0:T(8,128)}, ...) | async-done | bytes 684048 | tf_op jit(solution)/shard_map/psum | solution.py:197
  (552 shorter events, 93.4 us)
Async XLA Ops:
  7.2 119.9 %copy-start = (bf16[3,32]{1,0:T(4,128)(2,1)S(1)}, bf16[3,32]{1,0:T(4,128)(2,1)}, u32[]{:S(2)}) copy-start(bf16[3,32]{1,0:T(4,128)(2,1)} %param.19) | copy-start | bytes 580
  37.4 25.2 %collective-permute-start = (bf16[1,1,2,256]{3,2,1,0:T(2,128)(2,1)S(1)}, bf16[1,1,2,256]{3,2,1,0:T(2,128)(2,1)S(1)}, u32[]{:S(2)}, u32[]{:S(2)}) collective-permute-start(bf16[1,1,2,256]{3,2,1,0:T(2,128)(2,1)S(1)} %get-tuple-element.194), channel_id=1, source_target_pairs={{0,8},{8,16},{16,24},{1,9},{9,17},{17,25},{2,10},{10,18},{18,26},{... | collective-permute-start | bytes 3080 | tf_op jit(solution)/shard_map/ppermute | solution.py:17
  40.9 21.7 %collective-permute-start.1 = (bf16[1,1,2,256]{3,2,1,0:T(2,128)(2,1)S(1)}, bf16[1,1,2,256]{3,2,1,0:T(2,128)(2,1)S(1)}, u32[]{:S(2)}, u32[]{:S(2)}) collective-permute-start(bf16[1,1,2,256]{3,2,1,0:T(2,128)(2,1)S(1)} %get-tuple-element.193), channel_id=1, source_target_pairs={{8,0},{16,8},{24,16},{9,1},{17,9},{25,17},{10,2},{18,10},{26,18},{... | collective-permute-start | bytes 3080 | tf_op jit(solution)/shard_map/ppermute | solution.py:19
  63.3 3.6 %collective-permute-start.2 = (bf16[1,6,2,1]{3,2,1,0:T(2,128)(2,1)S(1)}, bf16[1,6,2,1]{3,2,1,0:T(2,128)(2,1)S(1)}, u32[]{:S(2)}, u32[]{:S(2)}) collective-permute-start(bf16[1,6,2,1]{3,2,1,0:T(2,128)(2,1)S(1)} %get-tuple-element.184), channel_id=1, source_target_pairs={{0,1},{1,2},{2,3},{3,4},{4,5},{5,6},{6,7},{8,9},{9,10},{10,11},{11... | collective-permute-start | bytes 80 | tf_op jit(solution)/shard_map/ppermute | solution.py:17
  65.5 3.5 %collective-permute-start.3 = (bf16[1,6,2,1]{3,2,1,0:T(2,128)(2,1)S(1)}, bf16[1,6,2,1]{3,2,1,0:T(2,128)(2,1)S(1)}, u32[]{:S(2)}, u32[]{:S(2)}) collective-permute-start(bf16[1,6,2,1]{3,2,1,0:T(2,128)(2,1)S(1)} %get-tuple-element.185), channel_id=1, source_target_pairs={{1,0},{2,1},{3,2},{4,3},{5,4},{6,5},{7,6},{9,8},{10,9},{11,10},{12... | collective-permute-start | bytes 80 | tf_op jit(solution)/shard_map/ppermute | solution.py:19
  71.3 6.1 %collective-permute-start.4 = (bf16[32,1,2,256]{3,0,2,1:T(8,128)(2,1)S(1)}, bf16[32,1,2,256]{3,0,2,1:T(8,128)(2,1)S(1)}, u32[]{:S(2)}, u32[]{:S(2)}) collective-permute-start(bf16[32,1,2,256]{3,0,2,1:T(8,128)(2,1)S(1)} %get-tuple-element.91), channel_id=1, source_target_pairs={{0,8},{8,16},{16,24},{1,9},{9,17},{17,25},{2,10},{10,18},{18,26},{... | collective-permute-start | bytes 98312 | tf_op jit(solution)/shard_map/ppermute | solution.py:17
  75.9 5.8 %collective-permute-start.5 = (bf16[32,1,2,256]{3,0,2,1:T(8,128)(2,1)S(1)}, bf16[32,1,2,256]{3,0,2,1:T(8,128)(2,1)S(1)}, u32[]{:S(2)}, u32[]{:S(2)}) collective-permute-start(bf16[32,1,2,256]{3,0,2,1:T(8,128)(2,1)S(1)} %get-tuple-element.92), channel_id=1, source_target_pairs={{8,0},{16,8},{24,16},{9,1},{17,9},{25,17},{10,2},{18,10},{26,18},{... | collective-permute-start | bytes 98312 | tf_op jit(solution)/shard_map/ppermute | solution.py:19
  81.8 4.4 %collective-permute-start.6 = (bf16[32,6,2,1]{3,0,2,1:T(8,128)(2,1)S(1)}, bf16[32,6,2,1]{3,0,2,1:T(8,128)(2,1)S(1)}, u32[]{:S(2)}, u32[]{:S(2)}) collective-permute-start(bf16[32,6,2,1]{3,0,2,1:T(8,128)(2,1)S(1)} %get-tuple-element.79), channel_id=1, source_target_pairs={{0,1},{1,2},{2,3},{3,4},{4,5},{5,6},{6,7},{8,9},{9,10},{10,11},{11... | collective-permute-start | bytes 2312 | tf_op jit(solution)/shard_map/ppermute | solution.py:17
  84.7 4.2 %collective-permute-start.7 = (bf16[32,6,2,1]{3,0,2,1:T(8,128)(2,1)S(1)}, bf16[32,6,2,1]{3,0,2,1:T(8,128)(2,1)S(1)}, u32[]{:S(2)}, u32[]{:S(2)}) collective-permute-start(bf16[32,6,2,1]{3,0,2,1:T(8,128)(2,1)S(1)} %get-tuple-element.80), channel_id=1, source_target_pairs={{1,0},{2,1},{3,2},{4,3},{5,4},{6,5},{7,6},{9,8},{10,9},{11,10},{12... | collective-permute-start | bytes 2312 | tf_op jit(solution)/shard_map/ppermute | solution.py:19
  105.3 4.9 %collective-permute-start.8 = (bf16[64,1,1,128]{3,0,1,2:T(8,128)(2,1)S(1)}, bf16[64,1,1,128]{3,0,1,2:T(8,128)(2,1)S(1)}, u32[]{:S(2)}, u32[]{:S(2)}) collective-permute-start(bf16[64,1,1,128]{3,0,1,2:T(8,128)(2,1)S(1)} %get-tuple-element.101), channel_id=1, source_target_pairs={{0,8},{8,16},{16,24},{1,9},{9,17},{17,25},{2,10},{10,18},{18,26},{... | collective-permute-start | bytes 49160 | tf_op jit(solution)/shard_map/ppermute | solution.py:17
  108.8 5.6 %collective-permute-start.9 = (bf16[64,1,1,128]{3,0,1,2:T(8,128)(2,1)S(1)}, bf16[64,1,1,128]{3,0,1,2:T(8,128)(2,1)S(1)}, u32[]{:S(2)}, u32[]{:S(2)}) collective-permute-start(bf16[64,1,1,128]{3,0,1,2:T(8,128)(2,1)S(1)} %get-tuple-element.102), channel_id=1, source_target_pairs={{8,0},{16,8},{24,16},{9,1},{17,9},{25,17},{10,2},{18,10},{26,18},{... | collective-permute-start | bytes 49160 | tf_op jit(solution)/shard_map/ppermute | solution.py:19
  114.6 8.0 %collective-permute-start.10 = (bf16[64,4,1,1]{3,0,1,2:T(8,128)(2,1)S(1)}, bf16[64,4,1,1]{3,0,1,2:T(8,128)(2,1)S(1)}, u32[]{:S(2)}, u32[]{:S(2)}) collective-permute-start(bf16[64,4,1,1]{3,0,1,2:T(8,128)(2,1)S(1)} %get-tuple-element.95), channel_id=1, source_target_pairs={{0,1},{1,2},{2,3},{3,4},{4,5},{5,6},{6,7},{8,9},{9,10},{10,11},{11... | collective-permute-start | bytes 1544 | tf_op jit(solution)/shard_map/ppermute | solution.py:17
  118.3 4.0 %collective-permute-start.11 = (bf16[64,4,1,1]{3,0,1,2:T(8,128)(2,1)S(1)}, bf16[64,4,1,1]{3,0,1,2:T(8,128)(2,1)S(1)}, u32[]{:S(2)}, u32[]{:S(2)}) collective-permute-start(bf16[64,4,1,1]{3,0,1,2:T(8,128)(2,1)S(1)} %get-tuple-element.96), channel_id=1, source_target_pairs={{1,0},{2,1},{3,2},{4,3},{5,4},{6,5},{7,6},{9,8},{10,9},{11,10},{12... | collective-permute-start | bytes 1544 | tf_op jit(solution)/shard_map/ppermute | solution.py:19
  138.8 13.4 %collective-permute-start.12 = (bf16[64,1,1,128]{3,0,1,2:T(8,128)(2,1)S(1)}, bf16[64,1,1,128]{3,0,1,2:T(8,128)(2,1)S(1)}, u32[]{:S(2)}, u32[]{:S(2)}) collective-permute-start(bf16[64,1,1,128]{3,0,1,2:T(8,128)(2,1)S(1)} %get-tuple-element.99), channel_id=1, source_target_pairs={{0,8},{8,16},{16,24},{1,9},{9,17},{17,25},{2,10},{10,18},{18,26},{... | collective-permute-start | bytes 49160 | tf_op jit(solution)/shard_map/ppermute | solution.py:17
  142.3 9.9 %collective-permute-start.13 = (bf16[64,1,1,128]{3,0,1,2:T(8,128)(2,1)S(1)}, bf16[64,1,1,128]{3,0,1,2:T(8,128)(2,1)S(1)}, u32[]{:S(2)}, u32[]{:S(2)}) collective-permute-start(bf16[64,1,1,128]{3,0,1,2:T(8,128)(2,1)S(1)} %get-tuple-element.100), channel_id=1, source_target_pairs={{8,0},{16,8},{24,16},{9,1},{17,9},{25,17},{10,2},{18,10},{26,18},{... | collective-permute-start | bytes 49160 | tf_op jit(solution)/shard_map/ppermute | solution.py:19
  144.4 97.8 %all-to-all-start = ((bf16[8,2,3,4,2,128]{5,1,4,3,2,0:T(2,128)(2,1)}), bf16[8,2,3,4,2,128]{5,1,4,3,2,0:T(2,128)(2,1)S(1)}, u32[]{:S(2)}, u32[]{:S(2)}) async-start(bf16[8,2,3,4,2,128]{5,1,4,3,2,0:T(2,128)(2,1)} %broadcast_multiply_fusion), calls=%async_computation | async-start | bytes 196608 | tf_op jit(solution)/shard_map/all_to_all | solution.py:145
  152.1 161.2 %all-reduce.8.cloned.1.call-start = ((), (), s32[]{:S(2)}) async-start(), calls=%async_computation.1 | async-start | bytes 3178496 | tf_op jit(solution)/shard_map/psum | solution.py:197
  152.3 4.5 %collective-permute-start.15 = (bf16[64,4,1,1]{3,0,1,2:T(8,128)(2,1)S(1)}, bf16[64,4,1,1]{3,0,1,2:T(8,128)(2,1)S(1)}, u32[]{:S(2)}, u32[]{:S(2)}) collective-permute-start(bf16[64,4,1,1]{3,0,1,2:T(8,128)(2,1)S(1)} %get-tuple-element.94), channel_id=1, source_target_pairs={{1,0},{2,1},{3,2},{4,3},{5,4},{6,5},{7,6},{9,8},{10,9},{11,10},{12... | collective-permute-start | bytes 1544 | tf_op jit(solution)/shard_map/ppermute | solution.py:19
  153.6 3.9 %collective-permute-start.14 = (bf16[64,4,1,1]{3,0,1,2:T(8,128)(2,1)S(1)}, bf16[64,4,1,1]{3,0,1,2:T(8,128)(2,1)S(1)}, u32[]{:S(2)}, u32[]{:S(2)}) collective-permute-start(bf16[64,4,1,1]{3,0,1,2:T(8,128)(2,1)S(1)} %get-tuple-element.93), channel_id=1, source_target_pairs={{0,1},{1,2},{2,3},{3,4},{4,5},{5,6},{6,7},{8,9},{9,10},{10,11},{11... | collective-permute-start | bytes 1544 | tf_op jit(solution)/shard_map/ppermute | solution.py:17
  167.8 7.3 %collective-permute-start.16 = (bf16[32,1,2,256]{3,0,2,1:T(8,128)(2,1)S(1)}, bf16[32,1,2,256]{3,0,2,1:T(8,128)(2,1)S(1)}, u32[]{:S(2)}, u32[]{:S(2)}) collective-permute-start(bf16[32,1,2,256]{3,0,2,1:T(8,128)(2,1)S(1)} %get-tuple-element.81), channel_id=1, source_target_pairs={{0,8},{8,16},{16,24},{1,9},{9,17},{17,25},{2,10},{10,18},{18,26},{... | collective-permute-start | bytes 98312 | tf_op jit(solution)/shard_map/ppermute | solution.py:17
  172.1 5.8 %collective-permute-start.17 = (bf16[32,1,2,256]{3,0,2,1:T(8,128)(2,1)S(1)}, bf16[32,1,2,256]{3,0,2,1:T(8,128)(2,1)S(1)}, u32[]{:S(2)}, u32[]{:S(2)}) collective-permute-start(bf16[32,1,2,256]{3,0,2,1:T(8,128)(2,1)S(1)} %get-tuple-element.82), channel_id=1, source_target_pairs={{8,0},{16,8},{24,16},{9,1},{17,9},{25,17},{10,2},{18,10},{26,18},{... | collective-permute-start | bytes 98312 | tf_op jit(solution)/shard_map/ppermute | solution.py:19
  178.0 4.1 %collective-permute-start.18 = (bf16[32,6,2,1]{3,0,2,1:T(8,128)(2,1)S(1)}, bf16[32,6,2,1]{3,0,2,1:T(8,128)(2,1)S(1)}, u32[]{:S(2)}, u32[]{:S(2)}) collective-permute-start(bf16[32,6,2,1]{3,0,2,1:T(8,128)(2,1)S(1)} %get-tuple-element.75), channel_id=1, source_target_pairs={{0,1},{1,2},{2,3},{3,4},{4,5},{5,6},{6,7},{8,9},{9,10},{10,11},{11... | collective-permute-start | bytes 2312 | tf_op jit(solution)/shard_map/ppermute | solution.py:17
  180.7 6.5 %collective-permute-start.19 = (bf16[32,6,2,1]{3,0,2,1:T(8,128)(2,1)S(1)}, bf16[32,6,2,1]{3,0,2,1:T(8,128)(2,1)S(1)}, u32[]{:S(2)}, u32[]{:S(2)}) collective-permute-start(bf16[32,6,2,1]{3,0,2,1:T(8,128)(2,1)S(1)} %get-tuple-element.76), channel_id=1, source_target_pairs={{1,0},{2,1},{3,2},{4,3},{5,4},{6,5},{7,6},{9,8},{10,9},{11,10},{12... | collective-permute-start | bytes 2312 | tf_op jit(solution)/shard_map/ppermute | solution.py:19
  195.9 46.4 %copy-start.97 = (pred[4]{0:T(512)(128)(4,1)S(1)}, pred[4]{0:T(512)(128)(4,1)}, u32[]{:S(2)}) copy-start(pred[4]{0:T(512)(128)(4,1)} %iota_compare_fusion.8) | copy-start | bytes 16
  (96 other events, 355.3 us)
Sparse Core Ops, SparseCore 0:
  175.2 138.1 all-reduce.7
where the time goes:
time: 327 us; the launch traced here: 325 us
  waiting for transfers between devices  94.4 us (29%)
  blocking collectives  80 us (24%)
  starting transfers between devices  54.6 us (17%)
  matrix products  41.6 us (13%)
  local copies, waits for them, and re-layouts  30.6 us (9%)
  between operations  16.7 us (5%)
  other arithmetic  7.44 us (2%)
    psum x1, waiting for transfers between devices, local(): lax.psum((grad_in, grad_res, grad_down, grad_mid, grad_up, head_weight_gr...  70.2 us
    psum x1, blocking collectives, local(): lax.psum((grad_in, grad_res, grad_down, grad_mid, grad_up, head_weight_gr...  44.9 us
    ppermute x10, starting transfers between devices, with_halo(): lax.ppermute(tail, axis, [(i, (i + 1) % count) for i in range(ends)])  33.7 us
    ppermute x10, waiting for transfers between devices, with_halo(): lax.ppermute(head, axis, [((i + 1) % count, i) for i in range(ends)])  23.5 us
    dot_general x108, matrix products, convolve(): jnp.einsum('oc,czyx->ozyx', weights[tap], window, preferred_element_type=...  22.8 us
    ppermute x10, starting transfers between devices, with_halo(): lax.ppermute(head, axis, [((i + 1) % count, i) for i in range(ends)])  13.1 us
    unnamed x226, local copies, waits for them, and re-layouts  12 us
    slice x16, local copies, waits for them, and re-layouts, strided(): return field[:, tap // 4::2, tap // 2 % 2::2, tap % 2::2]  11.8 us
  transfers between devices with their start and end apart: 22, of which 10 were waited for; matrix products, arithmetic and copies ran while one was open for 11% of the time, Pallas kernels for 0%

commit v1 on v0

--- a/solution.py
+++ b/solution.py
@@ -4,6 +4,45 @@
 from jax.sharding import PartitionSpec as P
 
 TPD = 2
+
+
+def tree_sum(grads, axes):
+    count = 1
+    for axis in axes:
+        count *= lax.axis_size(axis)
+    if count & (count - 1):
+        return lax.psum(grads, axes)
+    flat = jnp.concatenate([g.reshape(-1) for g in grads])
+    size = flat.shape[0]
+    padded = -(-size // count) * count
+    flat = jnp.pad(flat, (0, padded - size))
+    index = lax.axis_index(axes[0])
+    for axis in axes[1:]:
+        index = index * lax.axis_size(axis) + lax.axis_index(axis)
+    cur = flat
+    step = 1
+    while step < count:
+        half = cur.shape[0] // 2
+        upper = (index // step) % 2 == 1
+        low, high = cur[:half], cur[half:]
+        keep = jnp.where(upper, high, low)
+        send = jnp.where(upper, low, high)
+        pairs = [(i, i ^ step) for i in range(count)]
+        cur = keep + lax.ppermute(send, axes, pairs)
+        step *= 2
+    step = count // 2
+    while step >= 1:
+        pairs = [(i, i ^ step) for i in range(count)]
+        other = lax.ppermute(cur, axes, pairs)
+        upper = (index // step) % 2 == 1
+        cur = jnp.where(upper, jnp.concatenate([other, cur]), jnp.concatenate([cur, other]))
+        step //= 2
+    out = []
+    offset = 0
+    for g in grads:
+        out.append(cur[offset : offset + g.size].reshape(g.shape))
+        offset += g.size
+    return tuple(out)
 
 
 def with_halo(cells, sides, width):
@@ -85,28 +124,13 @@
     select = ((slot_list[None, :] == jnp.arange(total_tiles)[:, None]) & live[None, :]).astype(
         brain_float_half
     )
-    wanted = column * per_dev + jnp.arange(per_dev)
-    piece_img = lax.all_gather(tile_image, "xy", axis=1, tiled=True)
-    piece_tgt = lax.all_gather(tile_target, "xy", axis=1, tiled=True)
-    piece_cnt = lax.all_gather(owner_counts, "xy", axis=1, tiled=True)
-    piece_list = lax.all_gather(tile_list, "xy", axis=1, tiled=True)
-    owners = piece_list.shape[1]
-    piece_live = jnp.arange(slots)[None, :] < piece_cnt[0][:, None]
-    match = ((piece_list[0][:, :, None] == wanted[None, None, :]) & piece_live[:, :, None]).astype(
-        brain_float_half
-    )
-    acc_img = jnp.einsum(
-        "kst,kszyx->tzyx", match, piece_img[0], preferred_element_type=single_float
-    )
-    acc_tgt = jnp.einsum(
-        "kst,ksazyx->tazyx", match, piece_tgt[0], preferred_element_type=single_float
-    )
-    rows_hit = (jnp.arange(ranks)[:, None] == jnp.arange(owners)[None, :]).astype(single_float)
-    acc_hit = jnp.dot(rows_hit, jnp.sum(match.astype(single_float), axis=1))
-    acc_img, acc_tgt, acc_hit = (acc_img, acc_tgt, acc_hit)
-    mine_img = acc_img.astype(brain_float_half)
-    mine_tgt = acc_tgt.astype(brain_float_half)
-    owner_hit = acc_hit.astype(brain_float_half)
+    payload = jnp.concatenate([tile_image[0, 0][:, None], tile_target[0, 0]], axis=1)
+    outgoing = jnp.einsum("ps,sazyx->pazyx", select, payload, preferred_element_type=single_float)
+    outgoing = outgoing.astype(brain_float_half).reshape((ranks, per_dev) + payload.shape[1:])
+    incoming = lax.all_to_all(outgoing, "xy", 0, 0, tiled=True)
+    mine = jnp.sum(incoming.astype(single_float), axis=0).astype(brain_float_half)
+    mine_img = mine[:, 0]
+    mine_tgt = mine[:, 1:]
     image = mine_img.transpose(1, 2, 0, 3).reshape(1, depth, height, per_dev * width)
     target = mine_tgt.transpose(1, 2, 3, 0, 4).reshape(3, depth, height, per_dev * width)
     voxel_cells = depth * height * per_dev * width * ranks * layers
@@ -141,7 +165,7 @@
     error_field = affinity_map - target.astype(single_float)
     err_out = error_field.astype(brain_float_half)
     err_local = err_out.reshape(3, depth, height, per_dev, width).transpose(3, 0, 1, 2, 4)
-    sending = owner_hit[:, :, None, None, None, None] * err_local[None]
+    sending = jnp.broadcast_to(err_local[None], (ranks,) + err_local.shape)
     returned = lax.all_to_all(sending, "xy", split_axis=0, concat_axis=0, tiled=True)
     returned = returned.reshape((total_tiles, 3, depth, height, width))
     err_tiles = jnp.einsum(
@@ -194,7 +218,7 @@
     gfirst = gres.astype(single_float) + convolve(framed(gres), flipped(w_res))
     gact = jnp.where(h0 > 0, gfirst, 0.0).astype(brain_float_half)
     grad_in = tap_grads(gact, image_pad)[:, :, 0]
-    summed = lax.psum(
+    summed = tree_sum(
         (grad_in, grad_res, grad_down, grad_mid, grad_up, head_weight_gradient), ("gz", "xy")
     )
     return (err_tiles, summed[0], summed[1], summed[2], summed[3], summed[4], summed[5])

time: 327 us -> 227 us (0.69)
  blocking collectives: 80 us -> 7.93 us
  waiting for transfers between devices: 94.4 us -> 69.9 us
  between operations: 16.7 us -> 3.67 us
  starting transfers between devices: 54.6 us -> 60.5 us
  local copies, waits for them, and re-layouts: 30.6 us -> 34.4 us
    psum x1 -> x0, waiting for transfers between devices: 70.2 us -> none  [local(): lax.psum((grad_in, grad_res, grad_down, grad_mid, grad_up, head_weight_gr...]
    psum x1 -> x0, blocking collectives: 44.9 us -> none  [local(): lax.psum((grad_in, grad_res, grad_down, grad_mid, grad_up, head_weight_gr...]
    ppermute x0 -> x10, waiting for transfers between devices: none -> 36.4 us  [the longest x5 19.6 us: tree_sum(): cur = keep + lax.ppermute(send, axes, pairs)]
    all_gather x3 -> x0, blocking collectives: 25.6 us -> none  [the longest x1 8.9 us: local(): piece_img = lax.all_gather(tile_image, 'xy', axis=1, tiled=True)]
    ppermute x0 -> x10, starting transfers between devices: none -> 12.2 us  [the longest x5 10.1 us: tree_sum(): cur = keep + lax.ppermute(send, axes, pairs)]
    unnamed x1 -> x0, blocking collectives: 9.51 us -> none
    ppermute x10, waiting for transfers between devices: 23.5 us -> 32.8 us  [with_halo(): lax.ppermute(head, axis, [((i + 1) % count, i) for i in range(ends)])]
    all_to_all x0 -> x1, blocking collectives: none -> 7.93 us  [local(): lax.all_to_all(sending, 'xy', split_axis=0, concat_axis=0, tiled=True)]
  transfers between devices with their start and end apart: 22 -> 31, of which waited for: 10 -> 20; matrix products, arithmetic and copies ran while one was open for 11% -> 6% of each run, Pallas kernels for 0% -> 0%
where the time goes in v1:
time: 227 us; the launch traced here: 226 us
  waiting for transfers between devices  69.9 us (31%)
  starting transfers between devices  60.5 us (27%)
  matrix products  41.2 us (18%)
  local copies, waits for them, and re-layouts  34.4 us (15%)
  other arithmetic  8.65 us (4%)
  blocking collectives  7.93 us (3%)
  between operations  3.67 us (2%)
    ppermute x10, waiting for transfers between devices, with_halo(): lax.ppermute(head, axis, [((i + 1) % count, i) for i in range(ends)])  32.8 us
    ppermute x10, starting transfers between devices, with_halo(): lax.ppermute(tail, axis, [(i, (i + 1) % count) for i in range(ends)])  29.8 us
    dot_general x108, matrix products, convolve(): jnp.einsum('oc,czyx->ozyx', weights[tap], window, preferred_element_type=...  22.7 us
    ppermute x5, waiting for transfers between devices, tree_sum(): cur = keep + lax.ppermute(send, axes, pairs)  19.6 us
    ppermute x5, waiting for transfers between devices, tree_sum(): other = lax.ppermute(cur, axes, pairs)  16.8 us
    ppermute x10, starting transfers between devices, with_halo(): lax.ppermute(head, axis, [((i + 1) % count, i) for i in range(ends)])  13.3 us
    slice x16, local copies, waits for them, and re-layouts, strided(): return field[:, tap // 4::2, tap // 2 % 2::2, tap % 2::2]  11.8 us
    ppermute x5, starting transfers between devices, tree_sum(): cur = keep + lax.ppermute(send, axes, pairs)  10.1 us
  transfers between devices with their start and end apart: 31, of which 20 were waited for; matrix products, arithmetic and copies ran while one was open for 6% of the time, Pallas kernels for 0%

profile of v1, /device:TPU:0, one launch (start us, length us, event | category | flops | bytes accessed | tf_op | source)
XLA Modules:
  0.0 226.2 jit_solution(8501721368479876451)
XLA Ops:
  4.6 5.2 %all-to-all-start = ((bf16[8,2,4,4,2,128]{5,1,4,3,2,0:T(2,128)(2,1)}), bf16[8,2,4,4,2,128]{5,1,4,3,2,0:T(2,128)(2,1)S(1)}, u32[]{:S(2)}, u32[]{:S(2)}) async-start(bf16[8,2,4,4,2,128]{5,1,4,3,2,0:T(2,128)(2,1)} %copy.229), calls=%async_computation | async-start | bytes 262144 | tf_op jit(solution)/shard_map/all_to_all | solution.py:130
  18.2 3.5 %collective-permute-start = (bf16[1,1,2,256]{3,2,1,0:T(2,128)(2,1)S(1)}, bf16[1,1,2,256]{3,2,1,0:T(2,128)(2,1)S(1)}, u32[]{:S(2)}, u32[]{:S(2)}) collective-permute-start(bf16[1,1,2,256]{3,2,1,0:T(2,128)(2,1)S(1)} %get-tuple-element.190), channel_id=1, source_target_pairs={{0,8},{8,16},{16,24},{1,9},{9,17},{17,25},{2,10},{10,18},{18,26},{... | collective-permute-start | bytes 3080 | tf_op jit(solution)/shard_map/ppermute | solution.py:56
  24.3 3.5 %collective-permute-done.1 = bf16[1,1,2,256]{3,2,1,0:T(2,128)(2,1)S(1)} collective-permute-done((bf16[1,1,2,256]{3,2,1,0:T(2,128)(2,1)S(1)}, bf16[1,1,2,256]{3,2,1,0:T(2,128)(2,1)S(1)}, u32[]{:S(2)}, u32[]{:S(2)}) %collective-permute-start.1) | collective-permute-done | bytes 1056 | tf_op jit(solution)/shard_map/ppermute | solution.py:58
  31.1 4.0 %collective-permute-done.3 = bf16[1,6,2,1]{3,2,1,0:T(2,128)(2,1)S(1)} collective-permute-done((bf16[1,6,2,1]{3,2,1,0:T(2,128)(2,1)S(1)}, bf16[1,6,2,1]{3,2,1,0:T(2,128)(2,1)S(1)}, u32[]{:S(2)}, u32[]{:S(2)}) %collective-permute-start.3) | collective-permute-done | bytes 56 | tf_op jit(solution)/shard_map/ppermute | solution.py:58
  37.4 3.5 %collective-permute-start.4 = (bf16[32,1,2,256]{3,0,2,1:T(8,128)(2,1)S(1)}, bf16[32,1,2,256]{3,0,2,1:T(8,128)(2,1)S(1)}, u32[]{:S(2)}, u32[]{:S(2)}) collective-permute-start(bf16[32,1,2,256]{3,0,2,1:T(8,128)(2,1)S(1)} %get-tuple-element.87), channel_id=1, source_target_pairs={{0,8},{8,16},{16,24},{1,9},{9,17},{17,25},{2,10},{10,18},{18,26},{... | collective-permute-start | bytes 98312 | tf_op jit(solution)/shard_map/ppermute | solution.py:56
  42.5 4.2 %collective-permute-done.5 = bf16[32,1,2,256]{3,0,2,1:T(8,128)(2,1)S(1)} collective-permute-done((bf16[32,1,2,256]{3,0,2,1:T(8,128)(2,1)S(1)}, bf16[32,1,2,256]{3,0,2,1:T(8,128)(2,1)S(1)}, u32[]{:S(2)}, u32[]{:S(2)}) %collective-permute-start.5) | collective-permute-done | bytes 32800 | tf_op jit(solution)/shard_map/ppermute | solution.py:58
  70.3 3.5 %collective-permute-start.8 = (bf16[64,1,1,128]{3,0,1,2:T(8,128)(2,1)S(1)}, bf16[64,1,1,128]{3,0,1,2:T(8,128)(2,1)S(1)}, u32[]{:S(2)}, u32[]{:S(2)}) collective-permute-start(bf16[64,1,1,128]{3,0,1,2:T(8,128)(2,1)S(1)} %get-tuple-element.97), channel_id=1, source_target_pairs={{0,8},{8,16},{16,24},{1,9},{9,17},{17,25},{2,10},{10,18},{18,26},{... | collective-permute-start | bytes 49160 | tf_op jit(solution)/shard_map/ppermute | solution.py:56
  75.3 4.2 %collective-permute-done.9 = bf16[64,1,1,128]{3,0,1,2:T(8,128)(2,1)S(1)} collective-permute-done((bf16[64,1,1,128]{3,0,1,2:T(8,128)(2,1)S(1)}, bf16[64,1,1,128]{3,0,1,2:T(8,128)(2,1)S(1)}, u32[]{:S(2)}, u32[]{:S(2)}) %collective-permute-start.9) | collective-permute-done | bytes 16416 | tf_op jit(solution)/shard_map/ppermute | solution.py:58
  79.6 3.7 %collective-permute-start.10 = (bf16[64,4,1,1]{3,0,1,2:T(8,128)(2,1)S(1)}, bf16[64,4,1,1]{3,0,1,2:T(8,128)(2,1)S(1)}, u32[]{:S(2)}, u32[]{:S(2)}) collective-permute-start(bf16[64,4,1,1]{3,0,1,2:T(8,128)(2,1)S(1)} %get-tuple-element.91), channel_id=1, source_target_pairs={{0,1},{1,2},{2,3},{3,4},{4,5},{5,6},{6,7},{8,9},{9,10},{10,11},{11... | collective-permute-start | bytes 1544 | tf_op jit(solution)/shard_map/ppermute | solution.py:56
  107.6 4.0 %collective-permute-done.13 = bf16[64,1,1,128]{3,0,1,2:T(8,128)(2,1)S(1)} collective-permute-done((bf16[64,1,1,128]{3,0,1,2:T(8,128)(2,1)S(1)}, bf16[64,1,1,128]{3,0,1,2:T(8,128)(2,1)S(1)}, u32[]{:S(2)}, u32[]{:S(2)}) %collective-permute-start.13) | collective-permute-done | bytes 16416 | tf_op jit(solution)/shard_map/ppermute | solution.py:58
  112.9 4.6 %collective-permute-start.14 = (bf16[64,4,1,1]{3,0,1,2:T(8,128)(2,1)S(1)}, bf16[64,4,1,1]{3,0,1,2:T(8,128)(2,1)S(1)}, u32[]{:S(2)}, u32[]{:S(2)}) collective-permute-start(bf16[64,4,1,1]{3,0,1,2:T(8,128)(2,1)S(1)} %get-tuple-element.89), channel_id=1, source_target_pairs={{0,1},{1,2},{2,3},{3,4},{4,5},{5,6},{6,7},{8,9},{9,10},{10,11},{11... | collective-permute-start | bytes 1544 | tf_op jit(solution)/shard_map/ppermute | solution.py:56
  141.3 4.8 %collective-permute-done.19 = bf16[32,6,2,1]{3,0,2,1:T(8,128)(2,1)S(1)} collective-permute-done((bf16[32,6,2,1]{3,0,2,1:T(8,128)(2,1)S(1)}, bf16[32,6,2,1]{3,0,2,1:T(8,128)(2,1)S(1)}, u32[]{:S(2)}, u32[]{:S(2)}) %collective-permute-start.19) | collective-permute-done | bytes 800 | tf_op jit(solution)/shard_map/ppermute | solution.py:58
  156.4 3.3 %concatenate.186 = f32[155488]{0:T(1024)S(1)} concatenate(f32[864]{0:T(1024)S(1)} %reshape_squeeze.3, f32[27648]{0:T(1024)S(1)} %reshape.1047, f32[16384]{0:T(1024)S(1)} %reshape.1048, f32[110592]{0:T(1024)S(1)} %reshape.1034), dimensions={0} | concatenate | bytes 1243904 | tf_op jit(solution)/shard_map/concatenate | solution.py:15
  159.8 3.3 %collective-permute-start.20 = (f32[85984]{0:T(1024)S(1)}, f32[85984]{0:T(1024)S(1)}, u32[]{:S(2)}, u32[]{:S(2)}) collective-permute-start(f32[85984]{0:T(1024)S(1)} %slice_select_fusion), channel_id=1, source_target_pairs={{0,1},{1,0},{2,3},{3,2},{4,5},{5,4},{6,7},{7,6},{8,9},{9,8},{10,11... | collective-permute-start | bytes 1031816 | tf_op jit(solution)/shard_map/ppermute | solution.py:31
  164.5 6.4 %collective-permute-start.21 = (f32[42992]{0:T(1024)S(1)}, f32[42992]{0:T(1024)S(1)}, u32[]{:S(2)}, u32[]{:S(2)}) collective-permute-start(f32[42992]{0:T(1024)S(1)} %slice_select_fusion.1), channel_id=1, source_target_pairs={{0,2},{1,3},{2,0},{3,1},{4,6},{5,7},{6,4},{7,5},{8,10},{9,11},{10,... | collective-permute-start | bytes 515912 | tf_op jit(solution)/shard_map/ppermute | solution.py:31
  170.9 4.9 %collective-permute-done.21 = f32[42992]{0:T(1024)S(1)} collective-permute-done((f32[42992]{0:T(1024)S(1)}, f32[42992]{0:T(1024)S(1)}, u32[]{:S(2)}, u32[]{:S(2)}) %collective-permute-start.21) | collective-permute-done | bytes 172000 | tf_op jit(solution)/shard_map/ppermute | solution.py:31
  176.3 4.3 %collective-permute-done.22 = f32[21496]{0:T(1024)S(1)} collective-permute-done((f32[21496]{0:T(1024)S(1)}, f32[21496]{0:T(1024)S(1)}, u32[]{:S(2)}, u32[]{:S(2)}) %collective-permute-start.22) | collective-permute-done | bytes 86016 | tf_op jit(solution)/shard_map/ppermute | solution.py:31
  180.9 4.0 %collective-permute-done.23 = f32[10748]{0:T(1024)S(1)} collective-permute-done((f32[10748]{0:T(1024)S(1)}, f32[10748]{0:T(1024)S(1)}, u32[]{:S(2)}, u32[]{:S(2)}) %collective-permute-start.23) | collective-permute-done | bytes 43024 | tf_op jit(solution)/shard_map/ppermute | solution.py:31
  185.1 5.1 %collective-permute-done.24 = f32[5374]{0:T(1024)S(1)} collective-permute-done((f32[5374]{0:T(1024)S(1)}, f32[5374]{0:T(1024)S(1)}, u32[]{:S(2)}, u32[]{:S(2)}) %collective-permute-start.24) | collective-permute-done | bytes 21528 | tf_op jit(solution)/shard_map/ppermute | solution.py:31
  190.3 4.7 %collective-permute-done.25 = f32[5374]{0:T(1024)S(1)} collective-permute-done((f32[5374]{0:T(1024)S(1)}, f32[5374]{0:T(1024)S(1)}, u32[]{:S(2)}, u32[]{:S(2)}) %collective-permute-start.25) | collective-permute-done | bytes 21528 | tf_op jit(solution)/shard_map/ppermute | solution.py:36
  195.2 4.0 %collective-permute-done.26 = f32[10748]{0:T(1024)S(1)} collective-permute-done((f32[10748]{0:T(1024)S(1)}, f32[10748]{0:T(1024)S(1)}, u32[]{:S(2)}, u32[]{:S(2)}) %collective-permute-start.26) | collective-permute-done | bytes 43024 | tf_op jit(solution)/shard_map/ppermute | solution.py:36
  199.7 4.2 %collective-permute-done.27 = f32[21496]{0:T(1024)S(1)} collective-permute-done((f32[21496]{0:T(1024)S(1)}, f32[21496]{0:T(1024)S(1)}, u32[]{:S(2)}, u32[]{:S(2)}) %collective-permute-start.27) | collective-permute-done | bytes 86016 | tf_op jit(solution)/shard_map/ppermute | solution.py:36
  205.6 3.8 %collective-permute-done.28 = f32[42992]{0:T(1024)S(1)} collective-permute-done((f32[42992]{0:T(1024)S(1)}, f32[42992]{0:T(1024)S(1)}, u32[]{:S(2)}, u32[]{:S(2)}) %collective-permute-start.28) | collective-permute-done | bytes 172000 | tf_op jit(solution)/shard_map/ppermute | solution.py:36
  209.8 7.9 %all_to_all.10 = bf16[8,2,3,4,2,128]{5,1,4,3,2,0:T(2,128)(2,1)S(1)} all-to-all(bf16[8,2,3,4,2,128]{5,1,4,3,2,0:T(2,128)(2,1)S(1)} %broadcast_in_dim.10), channel_id=1, replica_groups=mesh['gz'=4,'xy'=8] {'xy'}, dimensions={0} | all-to-all | bytes 196608 | tf_op jit(solution)/shard_map/all_to_all | solution.py:169
  (577 shorter events, 117.8 us)
Async XLA Ops:
  4.6 13.5 %all-to-all-start = ((bf16[8,2,4,4,2,128]{5,1,4,3,2,0:T(2,128)(2,1)}), bf16[8,2,4,4,2,128]{5,1,4,3,2,0:T(2,128)(2,1)S(1)}, u32[]{:S(2)}, u32[]{:S(2)}) async-start(bf16[8,2,4,4,2,128]{5,1,4,3,2,0:T(2,128)(2,1)} %copy.229), calls=%async_computation | async-start | bytes 262144 | tf_op jit(solution)/shard_map/all_to_all | solution.py:130
  18.2 6.1 %collective-permute-start = (bf16[1,1,2,256]{3,2,1,0:T(2,128)(2,1)S(1)}, bf16[1,1,2,256]{3,2,1,0:T(2,128)(2,1)S(1)}, u32[]{:S(2)}, u32[]{:S(2)}) collective-permute-start(bf16[1,1,2,256]{3,2,1,0:T(2,128)(2,1)S(1)} %get-tuple-element.190), channel_id=1, source_target_pairs={{0,8},{8,16},{16,24},{1,9},{9,17},{17,25},{2,10},{10,18},{18,26},{... | collective-permute-start | bytes 3080 | tf_op jit(solution)/shard_map/ppermute | solution.py:56
  22.4 5.5 %collective-permute-start.1 = (bf16[1,1,2,256]{3,2,1,0:T(2,128)(2,1)S(1)}, bf16[1,1,2,256]{3,2,1,0:T(2,128)(2,1)S(1)}, u32[]{:S(2)}, u32[]{:S(2)}) collective-permute-start(bf16[1,1,2,256]{3,2,1,0:T(2,128)(2,1)S(1)} %get-tuple-element.189), channel_id=1, source_target_pairs={{8,0},{16,8},{24,16},{9,1},{17,9},{25,17},{10,2},{18,10},{26,18},{... | collective-permute-start | bytes 3080 | tf_op jit(solution)/shard_map/ppermute | solution.py:58
  29.8 5.3 %collective-permute-start.3 = (bf16[1,6,2,1]{3,2,1,0:T(2,128)(2,1)S(1)}, bf16[1,6,2,1]{3,2,1,0:T(2,128)(2,1)S(1)}, u32[]{:S(2)}, u32[]{:S(2)}) collective-permute-start(bf16[1,6,2,1]{3,2,1,0:T(2,128)(2,1)S(1)} %get-tuple-element.181), channel_id=1, source_target_pairs={{1,0},{2,1},{3,2},{4,3},{5,4},{6,5},{7,6},{9,8},{10,9},{11,10},{12... | collective-permute-start | bytes 80 | tf_op jit(solution)/shard_map/ppermute | solution.py:58
  37.4 5.1 %collective-permute-start.4 = (bf16[32,1,2,256]{3,0,2,1:T(8,128)(2,1)S(1)}, bf16[32,1,2,256]{3,0,2,1:T(8,128)(2,1)S(1)}, u32[]{:S(2)}, u32[]{:S(2)}) collective-permute-start(bf16[32,1,2,256]{3,0,2,1:T(8,128)(2,1)S(1)} %get-tuple-element.87), channel_id=1, source_target_pairs={{0,8},{8,16},{16,24},{1,9},{9,17},{17,25},{2,10},{10,18},{18,26},{... | collective-permute-start | bytes 98312 | tf_op jit(solution)/shard_map/ppermute | solution.py:56
  40.9 5.8 %collective-permute-start.5 = (bf16[32,1,2,256]{3,0,2,1:T(8,128)(2,1)S(1)}, bf16[32,1,2,256]{3,0,2,1:T(8,128)(2,1)S(1)}, u32[]{:S(2)}, u32[]{:S(2)}) collective-permute-start(bf16[32,1,2,256]{3,0,2,1:T(8,128)(2,1)S(1)} %get-tuple-element.88), channel_id=1, source_target_pairs={{8,0},{16,8},{24,16},{9,1},{17,9},{25,17},{10,2},{18,10},{26,18},{... | collective-permute-start | bytes 98312 | tf_op jit(solution)/shard_map/ppermute | solution.py:58
  46.9 4.4 %collective-permute-start.6 = (bf16[32,6,2,1]{3,0,2,1:T(8,128)(2,1)S(1)}, bf16[32,6,2,1]{3,0,2,1:T(8,128)(2,1)S(1)}, u32[]{:S(2)}, u32[]{:S(2)}) collective-permute-start(bf16[32,6,2,1]{3,0,2,1:T(8,128)(2,1)S(1)} %get-tuple-element.75), channel_id=1, source_target_pairs={{0,1},{1,2},{2,3},{3,4},{4,5},{5,6},{6,7},{8,9},{9,10},{10,11},{11... | collective-permute-start | bytes 2312 | tf_op jit(solution)/shard_map/ppermute | solution.py:56
  70.3 4.9 %collective-permute-start.8 = (bf16[64,1,1,128]{3,0,1,2:T(8,128)(2,1)S(1)}, bf16[64,1,1,128]{3,0,1,2:T(8,128)(2,1)S(1)}, u32[]{:S(2)}, u32[]{:S(2)}) collective-permute-start(bf16[64,1,1,128]{3,0,1,2:T(8,128)(2,1)S(1)} %get-tuple-element.97), channel_id=1, source_target_pairs={{0,8},{8,16},{16,24},{1,9},{9,17},{17,25},{2,10},{10,18},{18,26},{... | collective-permute-start | bytes 49160 | tf_op jit(solution)/shard_map/ppermute | solution.py:56
  73.8 5.6 %collective-permute-start.9 = (bf16[64,1,1,128]{3,0,1,2:T(8,128)(2,1)S(1)}, bf16[64,1,1,128]{3,0,1,2:T(8,128)(2,1)S(1)}, u32[]{:S(2)}, u32[]{:S(2)}) collective-permute-start(bf16[64,1,1,128]{3,0,1,2:T(8,128)(2,1)S(1)} %get-tuple-element.98), channel_id=1, source_target_pairs={{8,0},{16,8},{24,16},{9,1},{17,9},{25,17},{10,2},{18,10},{26,18},{... | collective-permute-start | bytes 49160 | tf_op jit(solution)/shard_map/ppermute | solution.py:58
  79.6 8.0 %collective-permute-start.10 = (bf16[64,4,1,1]{3,0,1,2:T(8,128)(2,1)S(1)}, bf16[64,4,1,1]{3,0,1,2:T(8,128)(2,1)S(1)}, u32[]{:S(2)}, u32[]{:S(2)}) collective-permute-start(bf16[64,4,1,1]{3,0,1,2:T(8,128)(2,1)S(1)} %get-tuple-element.91), channel_id=1, source_target_pairs={{0,1},{1,2},{2,3},{3,4},{4,5},{5,6},{6,7},{8,9},{9,10},{10,11},{11... | collective-permute-start | bytes 1544 | tf_op jit(solution)/shard_map/ppermute | solution.py:56
  105.9 5.6 %collective-permute-start.13 = (bf16[64,1,1,128]{3,0,1,2:T(8,128)(2,1)S(1)}, bf16[64,1,1,128]{3,0,1,2:T(8,128)(2,1)S(1)}, u32[]{:S(2)}, u32[]{:S(2)}) collective-permute-start(bf16[64,1,1,128]{3,0,1,2:T(8,128)(2,1)S(1)} %get-tuple-element.96), channel_id=1, source_target_pairs={{8,0},{16,8},{24,16},{9,1},{17,9},{25,17},{10,2},{18,10},{26,18},{... | collective-permute-start | bytes 49160 | tf_op jit(solution)/shard_map/ppermute | solution.py:58
  111.6 6.1 %collective-permute-start.15 = (bf16[64,4,1,1]{3,0,1,2:T(8,128)(2,1)S(1)}, bf16[64,4,1,1]{3,0,1,2:T(8,128)(2,1)S(1)}, u32[]{:S(2)}, u32[]{:S(2)}) collective-permute-start(bf16[64,4,1,1]{3,0,1,2:T(8,128)(2,1)S(1)} %get-tuple-element.90), channel_id=1, source_target_pairs={{1,0},{2,1},{3,2},{4,3},{5,4},{6,5},{7,6},{9,8},{10,9},{11,10},{12... | collective-permute-start | bytes 1544 | tf_op jit(solution)/shard_map/ppermute | solution.py:58
  112.9 5.5 %collective-permute-start.14 = (bf16[64,4,1,1]{3,0,1,2:T(8,128)(2,1)S(1)}, bf16[64,4,1,1]{3,0,1,2:T(8,128)(2,1)S(1)}, u32[]{:S(2)}, u32[]{:S(2)}) collective-permute-start(bf16[64,4,1,1]{3,0,1,2:T(8,128)(2,1)S(1)} %get-tuple-element.89), channel_id=1, source_target_pairs={{0,1},{1,2},{2,3},{3,4},{4,5},{5,6},{6,7},{8,9},{9,10},{10,11},{11... | collective-permute-start | bytes 1544 | tf_op jit(solution)/shard_map/ppermute | solution.py:56
  128.8 4.9 %collective-permute-start.16 = (bf16[32,1,2,256]{3,0,2,1:T(8,128)(2,1)S(1)}, bf16[32,1,2,256]{3,0,2,1:T(8,128)(2,1)S(1)}, u32[]{:S(2)}, u32[]{:S(2)}) collective-permute-start(bf16[32,1,2,256]{3,0,2,1:T(8,128)(2,1)S(1)} %get-tuple-element.77), channel_id=1, source_target_pairs={{0,8},{8,16},{16,24},{1,9},{9,17},{17,25},{2,10},{10,18},{18,26},{... | collective-permute-start | bytes 98312 | tf_op jit(solution)/shard_map/ppermute | solution.py:56
  131.0 5.8 %collective-permute-start.17 = (bf16[32,1,2,256]{3,0,2,1:T(8,128)(2,1)S(1)}, bf16[32,1,2,256]{3,0,2,1:T(8,128)(2,1)S(1)}, u32[]{:S(2)}, u32[]{:S(2)}) collective-permute-start(bf16[32,1,2,256]{3,0,2,1:T(8,128)(2,1)S(1)} %get-tuple-element.78), channel_id=1, source_target_pairs={{8,0},{16,8},{24,16},{9,1},{17,9},{25,17},{10,2},{18,10},{26,18},{... | collective-permute-start | bytes 98312 | tf_op jit(solution)/shard_map/ppermute | solution.py:58
  139.6 6.5 %collective-permute-start.19 = (bf16[32,6,2,1]{3,0,2,1:T(8,128)(2,1)S(1)}, bf16[32,6,2,1]{3,0,2,1:T(8,128)(2,1)S(1)}, u32[]{:S(2)}, u32[]{:S(2)}) collective-permute-start(bf16[32,6,2,1]{3,0,2,1:T(8,128)(2,1)S(1)} %get-tuple-element.72), channel_id=1, source_target_pairs={{1,0},{2,1},{3,2},{4,3},{5,4},{6,5},{7,6},{9,8},{10,9},{11,10},{12... | collective-permute-start | bytes 2312 | tf_op jit(solution)/shard_map/ppermute | solution.py:58
  159.8 4.6 %collective-permute-start.20 = (f32[85984]{0:T(1024)S(1)}, f32[85984]{0:T(1024)S(1)}, u32[]{:S(2)}, u32[]{:S(2)}) collective-permute-start(f32[85984]{0:T(1024)S(1)} %slice_select_fusion), channel_id=1, source_target_pairs={{0,1},{1,0},{2,3},{3,2},{4,5},{5,4},{6,7},{7,6},{8,9},{9,8},{10,11... | collective-permute-start | bytes 1031816 | tf_op jit(solution)/shard_map/ppermute | solution.py:31
  164.5 11.3 %collective-permute-start.21 = (f32[42992]{0:T(1024)S(1)}, f32[42992]{0:T(1024)S(1)}, u32[]{:S(2)}, u32[]{:S(2)}) collective-permute-start(f32[42992]{0:T(1024)S(1)} %slice_select_fusion.1), channel_id=1, source_target_pairs={{0,2},{1,3},{2,0},{3,1},{4,6},{5,7},{6,4},{7,5},{8,10},{9,11},{10,... | collective-permute-start | bytes 515912 | tf_op jit(solution)/shard_map/ppermute | solution.py:31
  176.0 4.6 %collective-permute-start.22 = (f32[21496]{0:T(1024)S(1)}, f32[21496]{0:T(1024)S(1)}, u32[]{:S(2)}, u32[]{:S(2)}) collective-permute-start(f32[21496]{0:T(1024)S(1)} %slice_select_fusion.2), channel_id=1, source_target_pairs={{0,4},{1,5},{2,6},{3,7},{4,0},{5,1},{6,2},{7,3},{8,12},{9,13},{10,... | collective-permute-start | bytes 257960 | tf_op jit(solution)/shard_map/ppermute | solution.py:31
  185.1 5.2 %collective-permute-start.24 = (f32[5374]{0:T(1024)S(1)}, f32[5374]{0:T(1024)S(1)}, u32[]{:S(2)}, u32[]{:S(2)}) collective-permute-start(f32[5374]{0:T(1024)S(1)} %slice_select_fusion.4), channel_id=1, source_target_pairs={{0,16},{1,17},{2,18},{3,19},{4,20},{5,21},{6,22},{7,23},{8,24},{9,... | collective-permute-start | bytes 64496 | tf_op jit(solution)/shard_map/ppermute | solution.py:31
  190.3 4.7 %collective-permute-start.25 = (f32[5374]{0:T(1024)S(1)}, f32[5374]{0:T(1024)S(1)}, u32[]{:S(2)}, u32[]{:S(2)}) collective-permute-start(f32[5374]{0:T(1024)S(1)} %select_add_fusion.4), channel_id=1, source_target_pairs={{0,16},{1,17},{2,18},{3,19},{4,20},{5,21},{6,22},{7,23},{8,24},{9,... | collective-permute-start | bytes 64496 | tf_op jit(solution)/shard_map/ppermute | solution.py:36
  199.3 4.6 %collective-permute-start.27 = (f32[21496]{0:T(1024)S(1)}, f32[21496]{0:T(1024)S(1)}, u32[]{:S(2)}, u32[]{:S(2)}) collective-permute-start(f32[21496]{0:T(1024)S(1)} %maximum_select_fusion.4), channel_id=1, source_target_pairs={{0,4},{1,5},{2,6},{3,7},{4,0},{5,1},{6,2},{7,3},{8,12},{9,13},{10,... | collective-permute-start | bytes 257960 | tf_op jit(solution)/shard_map/ppermute | solution.py:36
  204.0 5.5 %collective-permute-start.28 = (f32[42992]{0:T(1024)S(1)}, f32[42992]{0:T(1024)S(1)}, u32[]{:S(2)}, u32[]{:S(2)}) collective-permute-start(f32[42992]{0:T(1024)S(1)} %maximum_select_fusion.3), channel_id=1, source_target_pairs={{0,2},{1,3},{2,0},{3,1},{4,6},{5,7},{6,4},{7,5},{8,10},{9,11},{10,... | collective-permute-start | bytes 515912 | tf_op jit(solution)/shard_map/ppermute | solution.py:36
  209.6 9.8 %collective-permute-start.29 = (f32[85984]{0:T(1024)S(1)}, f32[85984]{0:T(1024)S(1)}, u32[]{:S(2)}, u32[]{:S(2)}) collective-permute-start(f32[85984]{0:T(1024)S(1)} %maximum_select_fusion.2), channel_id=1, source_target_pairs={{0,1},{1,0},{2,3},{3,2},{4,5},{5,4},{6,7},{7,6},{8,9},{9,8},{10,11... | collective-permute-start | bytes 1031816 | tf_op jit(solution)/shard_map/ppermute | solution.py:36
  (96 other events, 505.9 us)

commit v2 on v1

--- a/solution.py
+++ b/solution.py
@@ -45,6 +45,14 @@
     return tuple(out)
 
 
+def inside(shape, first_z, first_x, total_z, total_x):
+    zs = first_z + jnp.arange(shape[1])
+    xs = first_x + jnp.arange(shape[3])
+    keep_z = (zs >= 0) & (zs < total_z)
+    keep_x = (xs >= 0) & (xs < total_x)
+    return (keep_z[:, None] & keep_x[None, :])[None, :, None, :]
+
+
 def with_halo(cells, sides, width):
     for axis, dim in sides:
         count = lax.axis_size(axis)
@@ -134,18 +142,43 @@
     image = mine_img.transpose(1, 2, 0, 3).reshape(1, depth, height, per_dev * width)
     target = mine_tgt.transpose(1, 2, 3, 0, 4).reshape(3, depth, height, per_dev * width)
     voxel_cells = depth * height * per_dev * width * ranks * layers
-    image_pad = framed(image)
-    h0 = jax.nn.relu(convolve(image_pad, w_in[:, :, None])).astype(brain_float_half)
-    h0_pad = framed(h0)
-    h1 = jax.nn.relu(h0.astype(single_float) + convolve(h0_pad, w_res)).astype(brain_float_half)
+    block_z = lax.axis_index("gz") * depth
+    block_x = column * per_dev * width
+    image_wide = with_halo(image, (("gz", 1), ("xy", 3)), 4)
+    image_wide = jnp.pad(image_wide, ((0, 0), (0, 0), (1, 1), (0, 0)))
+    image_pad = image_wide[:, 3:-3, :, 3:-3]
+    h0_wide = jax.nn.relu(convolve(image_wide, w_in[:, :, None]))
+    h0_wide = jnp.where(
+        inside(h0_wide.shape, block_z - 3, block_x - 3, depth * layers, per_dev * width * ranks),
+        h0_wide,
+        0.0,
+    ).astype(brain_float_half)
+    h0_wide = jnp.pad(h0_wide, ((0, 0), (0, 0), (1, 1), (0, 0)))
+    h0 = h0_wide[:, 3:-3, 1:-1, 3:-3]
+    h0_pad = h0_wide[:, 2:-2, :, 2:-2]
+    h1_wide = jax.nn.relu(
+        h0_wide[:, 1:-1, 1:-1, 1:-1].astype(single_float) + convolve(h0_wide, w_res)
+    ).astype(brain_float_half)
+    h1 = h1_wide[:, 2:-2, :, 2:-2]
     down_sum = None
     for tap in range(8):
         term = jnp.einsum(
-            "oc,czyx->ozyx", w_down[tap], strided(h1, tap), preferred_element_type=single_float
+            "oc,czyx->ozyx", w_down[tap], strided(h1_wide, tap), preferred_element_type=single_float
         )
         down_sum = term if down_sum is None else down_sum + term
-    dfield = jax.nn.relu(down_sum).astype(brain_float_half)
-    dfield_pad = framed(dfield)
+    d_wide = jnp.where(
+        inside(
+            down_sum.shape,
+            block_z // 2 - 1,
+            block_x // 2 - 1,
+            depth * layers // 2,
+            per_dev * width * ranks // 2,
+        ),
+        jax.nn.relu(down_sum),
+        0.0,
+    ).astype(brain_float_half)
+    dfield = d_wide[:, 1:-1, :, 1:-1]
+    dfield_pad = jnp.pad(d_wide, ((0, 0), (0, 0), (1, 1), (0, 0)))
     cfield = jax.nn.relu(dfield.astype(single_float) + convolve(dfield_pad, w_mid)).astype(
         brain_float_half
     )

time: 227 us -> 207 us (0.912)
  waiting for transfers between devices: 69.9 us -> 33.5 us
  local copies, waits for them, and re-layouts: 34.4 us -> 51.9 us
  starting transfers between devices: 60.5 us -> 56.9 us
    ppermute x10 -> x6, waiting for transfers between devices: 32.8 us -> 6.24 us  [with_halo(): lax.ppermute(head, axis, [((i + 1) % count, i) for i in range(ends)])]
    slice x16 -> x24, local copies, waits for them, and re-layouts: 11.8 us -> 27.6 us  [strided(): return field[:, tap // 4::2, tap // 2 % 2::2, tap % 2::2]]
    ppermute x10 -> x6, starting transfers between devices: 29.8 us -> 23.2 us  [with_halo(): lax.ppermute(tail, axis, [(i, (i + 1) % count) for i in range(ends)])]
    ppermute x10 -> x6, starting transfers between devices: 13.3 us -> 7.88 us  [with_halo(): lax.ppermute(head, axis, [((i + 1) % count, i) for i in range(ends)])]
    ppermute x5, starting transfers between devices: 2.14 us -> 7.47 us  [tree_sum(): other = lax.ppermute(cur, axes, pairs)]
    ppermute x5, waiting for transfers between devices: 19.6 us -> 14.3 us  [tree_sum(): cur = keep + lax.ppermute(send, axes, pairs)]
    ppermute x5, waiting for transfers between devices: 16.8 us -> 11.7 us  [tree_sum(): other = lax.ppermute(cur, axes, pairs)]
    ppermute x5, starting transfers between devices: 10.1 us -> 13.2 us  [tree_sum(): cur = keep + lax.ppermute(send, axes, pairs)]
  transfers between devices with their start and end apart: 31 -> 23, of which waited for: 20 -> 13; matrix products, arithmetic and copies ran while one was open for 6% -> 14% of each run, Pallas kernels for 0% -> 0%
where the time goes in v2:
time: 207 us; the launch traced here: 206 us
  starting transfers between devices  56.9 us (27%)
  local copies, waits for them, and re-layouts  51.9 us (25%)
  matrix products  42.5 us (21%)
  waiting for transfers between devices  33.5 us (16%)
  other arithmetic  9.3 us (4%)
  blocking collectives  8.2 us (4%)
  between operations  3.33 us (2%)
    slice x24, local copies, waits for them, and re-layouts, strided(): return field[:, tap // 4::2, tap // 2 % 2::2, tap % 2::2]  27.6 us
    dot_general x108, matrix products, convolve(): jnp.einsum('oc,czyx->ozyx', weights[tap], window, preferred_element_type=...  23.2 us
    ppermute x6, starting transfers between devices, with_halo(): lax.ppermute(tail, axis, [(i, (i + 1) % count) for i in range(ends)])  23.2 us
    ppermute x5, waiting for transfers between devices, tree_sum(): cur = keep + lax.ppermute(send, axes, pairs)  14.3 us
    ppermute x5, starting transfers between devices, tree_sum(): cur = keep + lax.ppermute(send, axes, pairs)  13.2 us
    ppermute x5, waiting for transfers between devices, tree_sum(): other = lax.ppermute(cur, axes, pairs)  11.7 us
    dot_general x64, matrix products, tap_grads(): jnp.einsum('ozyx,czyx->oc', grad, window, preferred_element_type=jnp.floa...  10.2 us
    all_to_all x1, blocking collectives, local(): lax.all_to_all(sending, 'xy', split_axis=0, concat_axis=0, tiled=True)  8.2 us
  transfers between devices with their start and end apart: 23, of which 13 were waited for; matrix products, arithmetic and copies ran while one was open for 14% of the time, Pallas kernels for 0%

profile of v2, /device:TPU:0, one launch (start us, length us, event | category | flops | bytes accessed | tf_op | source)
XLA Modules:
  0.0 205.7 jit_solution(4714969115424500933)
XLA Ops:
  4.6 5.2 %all-to-all-start = ((bf16[8,2,4,4,2,128]{5,1,4,3,2,0:T(2,128)(2,1)}), bf16[8,2,4,4,2,128]{5,1,4,3,2,0:T(2,128)(2,1)S(1)}, u32[]{:S(2)}, u32[]{:S(2)}) async-start(bf16[8,2,4,4,2,128]{5,1,4,3,2,0:T(2,128)(2,1)} %copy.229), calls=%async_computation | async-start | bytes 262144 | tf_op jit(solution)/shard_map/all_to_all | solution.py:138
  16.8 4.5 %collective-permute-start = (bf16[1,4,2,256]{3,2,1,0:T(2,128)(2,1)S(1)}, bf16[1,4,2,256]{3,2,1,0:T(2,128)(2,1)S(1)}, u32[]{:S(2)}, u32[]{:S(2)}) collective-permute-start(bf16[1,4,2,256]{3,2,1,0:T(2,128)(2,1)S(1)} %reshape.1091), channel_id=1, source_target_pairs={{0,8},{8,16},{16,24},{1,9},{9,17},{17,25},{2,10},{10,18},{18,26},{... | collective-permute-start | bytes 12296 | tf_op jit(solution)/shard_map/ppermute | solution.py:64
  27.2 2.8 %collective-permute-done.3 = bf16[1,12,2,4]{3,2,1,0:T(2,128)(2,1)S(1)} collective-permute-done((bf16[1,12,2,4]{3,2,1,0:T(2,128)(2,1)S(1)}, bf16[1,12,2,4]{3,2,1,0:T(2,128)(2,1)S(1)}, u32[]{:S(2)}, u32[]{:S(2)}) %collective-permute-start.3) | collective-permute-done | bytes 224 | tf_op jit(solution)/shard_map/ppermute | solution.py:66
  31.8 2.1 fusion.177
  72.8 2.0 pad_slice_fusion
  74.8 4.2 %collective-permute-start.4 = (bf16[64,1,1,128]{3,0,1,2:T(8,128)(2,1)}, bf16[64,1,1,128]{3,0,1,2:T(8,128)(2,1)S(1)}, u32[]{:S(2)}, u32[]{:S(2)}) collective-permute-start(bf16[64,1,1,128]{3,0,1,2:T(8,128)(2,1)} %get-tuple-element.74), channel_id=1, source_target_pairs={{0,8},{8,16},{16,24},{1,9},{9,17},{17,25},{2,10},{10,18},{18,26},{... | collective-permute-start | bytes 49160 | tf_op jit(solution)/shard_map/ppermute | solution.py:64
  94.3 4.0 %collective-permute-start.6 = (bf16[64,4,1,1]{3,0,1,2:T(8,128)(2,1)S(1)}, bf16[64,4,1,1]{3,0,1,2:T(8,128)(2,1)S(1)}, u32[]{:S(2)}, u32[]{:S(2)}) collective-permute-start(bf16[64,4,1,1]{3,0,1,2:T(8,128)(2,1)S(1)} %get-tuple-element.70), channel_id=1, source_target_pairs={{0,1},{1,2},{2,3},{3,4},{4,5},{5,6},{6,7},{8,9},{9,10},{10,11},{11... | collective-permute-start | bytes 1544 | tf_op jit(solution)/shard_map/ppermute | solution.py:64
  106.9 4.5 %collective-permute-start.8 = (bf16[32,1,2,256]{3,0,2,1:T(8,128)(2,1)S(1)}, bf16[32,1,2,256]{3,0,2,1:T(8,128)(2,1)S(1)}, u32[]{:S(2)}, u32[]{:S(2)}) collective-permute-start(bf16[32,1,2,256]{3,0,2,1:T(8,128)(2,1)S(1)} %get-tuple-element.68), channel_id=1, source_target_pairs={{0,8},{8,16},{16,24},{1,9},{9,17},{17,25},{2,10},{10,18},{18,26},{... | collective-permute-start | bytes 98312 | tf_op jit(solution)/shard_map/ppermute | solution.py:64
  119.4 4.7 %collective-permute-start.10 = (bf16[32,6,2,1]{3,0,2,1:T(8,128)(2,1)S(1)}, bf16[32,6,2,1]{3,0,2,1:T(8,128)(2,1)S(1)}, u32[]{:S(2)}, u32[]{:S(2)}) collective-permute-start(bf16[32,6,2,1]{3,0,2,1:T(8,128)(2,1)S(1)} %get-tuple-element.66), channel_id=1, source_target_pairs={{0,1},{1,2},{2,3},{3,4},{4,5},{5,6},{6,7},{8,9},{9,10},{10,11},{11... | collective-permute-start | bytes 2312 | tf_op jit(solution)/shard_map/ppermute | solution.py:64
  137.6 3.3 %concatenate.133 = f32[155488]{0:T(1024)S(1)} concatenate(f32[864]{0:T(1024)S(1)} %reshape_squeeze.3, f32[27648]{0:T(1024)S(1)} %reshape.1218, f32[16384]{0:T(1024)S(1)} %reshape.1227, f32[110592]{0:T(1024)S(1)} %reshape.1177), dimensions={0} | concatenate | bytes 1243904 | tf_op jit(solution)/shard_map/concatenate | solution.py:15
  141.0 4.3 %collective-permute-start.12 = (f32[85984]{0:T(1024)S(1)}, f32[85984]{0:T(1024)S(1)}, u32[]{:S(2)}, u32[]{:S(2)}) collective-permute-start(f32[85984]{0:T(1024)S(1)} %slice_select_fusion), channel_id=1, source_target_pairs={{0,1},{1,0},{2,3},{3,2},{4,5},{5,4},{6,7},{7,6},{8,9},{9,8},{10,11... | collective-permute-start | bytes 1031816 | tf_op jit(solution)/shard_map/ppermute | solution.py:31
  146.7 2.8 %collective-permute-start.13 = (f32[42992]{0:T(1024)S(1)}, f32[42992]{0:T(1024)S(1)}, u32[]{:S(2)}, u32[]{:S(2)}) collective-permute-start(f32[42992]{0:T(1024)S(1)} %slice_select_fusion.1), channel_id=1, source_target_pairs={{0,2},{1,3},{2,0},{3,1},{4,6},{5,7},{6,4},{7,5},{8,10},{9,11},{10,... | collective-permute-start | bytes 515912 | tf_op jit(solution)/shard_map/ppermute | solution.py:31
  149.6 4.9 %collective-permute-done.13 = f32[42992]{0:T(1024)S(1)} collective-permute-done((f32[42992]{0:T(1024)S(1)}, f32[42992]{0:T(1024)S(1)}, u32[]{:S(2)}, u32[]{:S(2)}) %collective-permute-start.13) | collective-permute-done | bytes 172000 | tf_op jit(solution)/shard_map/ppermute | solution.py:31
  155.0 4.3 %collective-permute-done.14 = f32[21496]{0:T(1024)S(1)} collective-permute-done((f32[21496]{0:T(1024)S(1)}, f32[21496]{0:T(1024)S(1)}, u32[]{:S(2)}, u32[]{:S(2)}) %collective-permute-start.14) | collective-permute-done | bytes 86016 | tf_op jit(solution)/shard_map/ppermute | solution.py:31
  159.5 2.7 %collective-permute-start.15 = (f32[10748]{0:T(1024)S(1)}, f32[10748]{0:T(1024)S(1)}, u32[]{:S(2)}, u32[]{:S(2)}) collective-permute-start(f32[10748]{0:T(1024)S(1)} %slice_select_fusion.3), channel_id=1, source_target_pairs={{0,8},{1,9},{2,10},{3,11},{4,12},{5,13},{6,14},{7,15},{8,0},{9,1},... | collective-permute-start | bytes 128984 | tf_op jit(solution)/shard_map/ppermute | solution.py:31
  162.2 2.0 collective-permute-done.15
  164.4 3.0 %collective-permute-start.16 = (f32[5374]{0:T(1024)S(1)}, f32[5374]{0:T(1024)S(1)}, u32[]{:S(2)}, u32[]{:S(2)}) collective-permute-start(f32[5374]{0:T(1024)S(1)} %slice_select_fusion.4), channel_id=1, source_target_pairs={{0,16},{1,17},{2,18},{3,19},{4,20},{5,21},{6,22},{7,23},{8,24},{9,... | collective-permute-start | bytes 64496 | tf_op jit(solution)/shard_map/ppermute | solution.py:31
  169.3 3.0 %collective-permute-start.17 = (f32[5374]{0:T(1024)S(1)}, f32[5374]{0:T(1024)S(1)}, u32[]{:S(2)}, u32[]{:S(2)}) collective-permute-start(f32[5374]{0:T(1024)S(1)} %select_add_fusion.4), channel_id=1, source_target_pairs={{0,16},{1,17},{2,18},{3,19},{4,20},{5,21},{6,22},{7,23},{8,24},{9,... | collective-permute-start | bytes 64496 | tf_op jit(solution)/shard_map/ppermute | solution.py:36
  174.2 2.2 %collective-permute-start.18 = (f32[10748]{0:T(1024)S(1)}, f32[10748]{0:T(1024)S(1)}, u32[]{:S(2)}, u32[]{:S(2)}) collective-permute-start(f32[10748]{0:T(1024)S(1)} %maximum_select_fusion.5), channel_id=1, source_target_pairs={{0,8},{1,9},{2,10},{3,11},{4,12},{5,13},{6,14},{7,15},{8,0},{9,1},... | collective-permute-start | bytes 128984 | tf_op jit(solution)/shard_map/ppermute | solution.py:36
  176.4 2.0 collective-permute-done.18
  178.8 4.3 %collective-permute-done.19 = f32[21496]{0:T(1024)S(1)} collective-permute-done((f32[21496]{0:T(1024)S(1)}, f32[21496]{0:T(1024)S(1)}, u32[]{:S(2)}, u32[]{:S(2)}) %collective-permute-start.19) | collective-permute-done | bytes 86016 | tf_op jit(solution)/shard_map/ppermute | solution.py:36
  183.2 1.9 collective-permute-start.20
  185.1 3.6 %collective-permute-done.20 = f32[42992]{0:T(1024)S(1)} collective-permute-done((f32[42992]{0:T(1024)S(1)}, f32[42992]{0:T(1024)S(1)}, u32[]{:S(2)}, u32[]{:S(2)}) %collective-permute-start.20) | collective-permute-done | bytes 172000 | tf_op jit(solution)/shard_map/ppermute | solution.py:36
  189.0 8.2 %all_to_all.10 = bf16[8,2,3,4,2,128]{5,1,4,3,2,0:T(2,128)(2,1)S(1)} all-to-all(bf16[8,2,3,4,2,128]{5,1,4,3,2,0:T(2,128)(2,1)S(1)} %broadcast_in_dim.32), channel_id=1, replica_groups=mesh['gz'=4,'xy'=8] {'xy'}, dimensions={0} | all-to-all | bytes 196608 | tf_op jit(solution)/shard_map/all_to_all | solution.py:202
  (539 shorter events, 115.8 us)
Async XLA Ops:
  0.6 60.3 %copy-start = (bf16[3,32]{1,0:T(4,128)(2,1)S(1)}, bf16[3,32]{1,0:T(4,128)(2,1)}, u32[]{:S(2)}) copy-start(bf16[3,32]{1,0:T(4,128)(2,1)} %param.19) | copy-start | bytes 580
  4.6 10.7 %all-to-all-start = ((bf16[8,2,4,4,2,128]{5,1,4,3,2,0:T(2,128)(2,1)}), bf16[8,2,4,4,2,128]{5,1,4,3,2,0:T(2,128)(2,1)S(1)}, u32[]{:S(2)}, u32[]{:S(2)}) async-start(bf16[8,2,4,4,2,128]{5,1,4,3,2,0:T(2,128)(2,1)} %copy.229), calls=%async_computation | async-start | bytes 262144 | tf_op jit(solution)/shard_map/all_to_all | solution.py:138
  15.5 5.9 %collective-permute-start.1 = (bf16[1,4,2,256]{3,2,1,0:T(2,128)(2,1)S(1)}, bf16[1,4,2,256]{3,2,1,0:T(2,128)(2,1)S(1)}, u32[]{:S(2)}, u32[]{:S(2)}) collective-permute-start(bf16[1,4,2,256]{3,2,1,0:T(2,128)(2,1)S(1)} %reshape.1091), channel_id=1, source_target_pairs={{8,0},{16,8},{24,16},{9,1},{17,9},{25,17},{10,2},{18,10},{26,18},{... | collective-permute-start | bytes 12296 | tf_op jit(solution)/shard_map/ppermute | solution.py:66
  16.8 5.9 %collective-permute-start = (bf16[1,4,2,256]{3,2,1,0:T(2,128)(2,1)S(1)}, bf16[1,4,2,256]{3,2,1,0:T(2,128)(2,1)S(1)}, u32[]{:S(2)}, u32[]{:S(2)}) collective-permute-start(bf16[1,4,2,256]{3,2,1,0:T(2,128)(2,1)S(1)} %reshape.1091), channel_id=1, source_target_pairs={{0,8},{8,16},{16,24},{1,9},{9,17},{17,25},{2,10},{10,18},{18,26},{... | collective-permute-start | bytes 12296 | tf_op jit(solution)/shard_map/ppermute | solution.py:64
  23.4 3.8 %collective-permute-start.2 = (bf16[1,12,2,4]{3,2,1,0:T(2,128)(2,1)S(1)}, bf16[1,12,2,4]{3,2,1,0:T(2,128)(2,1)S(1)}, u32[]{:S(2)}, u32[]{:S(2)}) collective-permute-start(bf16[1,12,2,4]{3,2,1,0:T(2,128)(2,1)S(1)} %get-tuple-element.130), channel_id=1, source_target_pairs={{0,1},{1,2},{2,3},{3,4},{4,5},{5,6},{6,7},{8,9},{9,10},{10,11},{11... | collective-permute-start | bytes 584 | tf_op jit(solution)/shard_map/ppermute | solution.py:64
  24.6 5.3 %collective-permute-start.3 = (bf16[1,12,2,4]{3,2,1,0:T(2,128)(2,1)S(1)}, bf16[1,12,2,4]{3,2,1,0:T(2,128)(2,1)S(1)}, u32[]{:S(2)}, u32[]{:S(2)}) collective-permute-start(bf16[1,12,2,4]{3,2,1,0:T(2,128)(2,1)S(1)} %get-tuple-element.131), channel_id=1, source_target_pairs={{1,0},{2,1},{3,2},{4,3},{5,4},{6,5},{7,6},{9,8},{10,9},{11,10},{12... | collective-permute-start | bytes 584 | tf_op jit(solution)/shard_map/ppermute | solution.py:66
  74.8 19.3 %collective-permute-start.4 = (bf16[64,1,1,128]{3,0,1,2:T(8,128)(2,1)}, bf16[64,1,1,128]{3,0,1,2:T(8,128)(2,1)S(1)}, u32[]{:S(2)}, u32[]{:S(2)}) collective-permute-start(bf16[64,1,1,128]{3,0,1,2:T(8,128)(2,1)} %get-tuple-element.74), channel_id=1, source_target_pairs={{0,8},{8,16},{16,24},{1,9},{9,17},{17,25},{2,10},{10,18},{18,26},{... | collective-permute-start | bytes 49160 | tf_op jit(solution)/shard_map/ppermute | solution.py:64
  79.0 15.2 %collective-permute-start.5 = (bf16[64,1,1,128]{3,0,1,2:T(8,128)(2,1)}, bf16[64,1,1,128]{3,0,1,2:T(8,128)(2,1)S(1)}, u32[]{:S(2)}, u32[]{:S(2)}) collective-permute-start(bf16[64,1,1,128]{3,0,1,2:T(8,128)(2,1)} %get-tuple-element.75), channel_id=1, source_target_pairs={{8,0},{16,8},{24,16},{9,1},{17,9},{25,17},{10,2},{18,10},{26,18},{... | collective-permute-start | bytes 49160 | tf_op jit(solution)/shard_map/ppermute | solution.py:66
  94.3 7.4 %collective-permute-start.6 = (bf16[64,4,1,1]{3,0,1,2:T(8,128)(2,1)S(1)}, bf16[64,4,1,1]{3,0,1,2:T(8,128)(2,1)S(1)}, u32[]{:S(2)}, u32[]{:S(2)}) collective-permute-start(bf16[64,4,1,1]{3,0,1,2:T(8,128)(2,1)S(1)} %get-tuple-element.70), channel_id=1, source_target_pairs={{0,1},{1,2},{2,3},{3,4},{4,5},{5,6},{6,7},{8,9},{9,10},{10,11},{11... | collective-permute-start | bytes 1544 | tf_op jit(solution)/shard_map/ppermute | solution.py:64
  98.3 3.1 %collective-permute-start.7 = (bf16[64,4,1,1]{3,0,1,2:T(8,128)(2,1)S(1)}, bf16[64,4,1,1]{3,0,1,2:T(8,128)(2,1)S(1)}, u32[]{:S(2)}, u32[]{:S(2)}) collective-permute-start(bf16[64,4,1,1]{3,0,1,2:T(8,128)(2,1)S(1)} %get-tuple-element.71), channel_id=1, source_target_pairs={{1,0},{2,1},{3,2},{4,3},{5,4},{6,5},{7,6},{9,8},{10,9},{11,10},{12... | collective-permute-start | bytes 1544 | tf_op jit(solution)/shard_map/ppermute | solution.py:66
  106.9 12.3 %collective-permute-start.8 = (bf16[32,1,2,256]{3,0,2,1:T(8,128)(2,1)S(1)}, bf16[32,1,2,256]{3,0,2,1:T(8,128)(2,1)S(1)}, u32[]{:S(2)}, u32[]{:S(2)}) collective-permute-start(bf16[32,1,2,256]{3,0,2,1:T(8,128)(2,1)S(1)} %get-tuple-element.68), channel_id=1, source_target_pairs={{0,8},{8,16},{16,24},{1,9},{9,17},{17,25},{2,10},{10,18},{18,26},{... | collective-permute-start | bytes 98312 | tf_op jit(solution)/shard_map/ppermute | solution.py:64
  111.4 7.8 %collective-permute-start.9 = (bf16[32,1,2,256]{3,0,2,1:T(8,128)(2,1)S(1)}, bf16[32,1,2,256]{3,0,2,1:T(8,128)(2,1)S(1)}, u32[]{:S(2)}, u32[]{:S(2)}) collective-permute-start(bf16[32,1,2,256]{3,0,2,1:T(8,128)(2,1)S(1)} %get-tuple-element.69), channel_id=1, source_target_pairs={{8,0},{16,8},{24,16},{9,1},{17,9},{25,17},{10,2},{18,10},{26,18},{... | collective-permute-start | bytes 98312 | tf_op jit(solution)/shard_map/ppermute | solution.py:66
  119.4 6.2 %collective-permute-start.10 = (bf16[32,6,2,1]{3,0,2,1:T(8,128)(2,1)S(1)}, bf16[32,6,2,1]{3,0,2,1:T(8,128)(2,1)S(1)}, u32[]{:S(2)}, u32[]{:S(2)}) collective-permute-start(bf16[32,6,2,1]{3,0,2,1:T(8,128)(2,1)S(1)} %get-tuple-element.66), channel_id=1, source_target_pairs={{0,1},{1,2},{2,3},{3,4},{4,5},{5,6},{6,7},{8,9},{9,10},{10,11},{11... | collective-permute-start | bytes 2312 | tf_op jit(solution)/shard_map/ppermute | solution.py:64
  124.1 3.2 %collective-permute-start.11 = (bf16[32,6,2,1]{3,0,2,1:T(8,128)(2,1)S(1)}, bf16[32,6,2,1]{3,0,2,1:T(8,128)(2,1)S(1)}, u32[]{:S(2)}, u32[]{:S(2)}) collective-permute-start(bf16[32,6,2,1]{3,0,2,1:T(8,128)(2,1)S(1)} %get-tuple-element.67), channel_id=1, source_target_pairs={{1,0},{2,1},{3,2},{4,3},{5,4},{6,5},{7,6},{9,8},{10,9},{11,10},{12... | collective-permute-start | bytes 2312 | tf_op jit(solution)/shard_map/ppermute | solution.py:66
  141.0 5.6 %collective-permute-start.12 = (f32[85984]{0:T(1024)S(1)}, f32[85984]{0:T(1024)S(1)}, u32[]{:S(2)}, u32[]{:S(2)}) collective-permute-start(f32[85984]{0:T(1024)S(1)} %slice_select_fusion), channel_id=1, source_target_pairs={{0,1},{1,0},{2,3},{3,2},{4,5},{5,4},{6,7},{7,6},{8,9},{9,8},{10,11... | collective-permute-start | bytes 1031816 | tf_op jit(solution)/shard_map/ppermute | solution.py:31
  146.7 7.7 %collective-permute-start.13 = (f32[42992]{0:T(1024)S(1)}, f32[42992]{0:T(1024)S(1)}, u32[]{:S(2)}, u32[]{:S(2)}) collective-permute-start(f32[42992]{0:T(1024)S(1)} %slice_select_fusion.1), channel_id=1, source_target_pairs={{0,2},{1,3},{2,0},{3,1},{4,6},{5,7},{6,4},{7,5},{8,10},{9,11},{10,... | collective-permute-start | bytes 515912 | tf_op jit(solution)/shard_map/ppermute | solution.py:31
  154.7 4.6 %collective-permute-start.14 = (f32[21496]{0:T(1024)S(1)}, f32[21496]{0:T(1024)S(1)}, u32[]{:S(2)}, u32[]{:S(2)}) collective-permute-start(f32[21496]{0:T(1024)S(1)} %slice_select_fusion.2), channel_id=1, source_target_pairs={{0,4},{1,5},{2,6},{3,7},{4,0},{5,1},{6,2},{7,3},{8,12},{9,13},{10,... | collective-permute-start | bytes 257960 | tf_op jit(solution)/shard_map/ppermute | solution.py:31
  159.5 4.7 %collective-permute-start.15 = (f32[10748]{0:T(1024)S(1)}, f32[10748]{0:T(1024)S(1)}, u32[]{:S(2)}, u32[]{:S(2)}) collective-permute-start(f32[10748]{0:T(1024)S(1)} %slice_select_fusion.3), channel_id=1, source_target_pairs={{0,8},{1,9},{2,10},{3,11},{4,12},{5,13},{6,14},{7,15},{8,0},{9,1},... | collective-permute-start | bytes 128984 | tf_op jit(solution)/shard_map/ppermute | solution.py:31
  164.4 4.9 %collective-permute-start.16 = (f32[5374]{0:T(1024)S(1)}, f32[5374]{0:T(1024)S(1)}, u32[]{:S(2)}, u32[]{:S(2)}) collective-permute-start(f32[5374]{0:T(1024)S(1)} %slice_select_fusion.4), channel_id=1, source_target_pairs={{0,16},{1,17},{2,18},{3,19},{4,20},{5,21},{6,22},{7,23},{8,24},{9,... | collective-permute-start | bytes 64496 | tf_op jit(solution)/shard_map/ppermute | solution.py:31
  169.3 4.8 %collective-permute-start.17 = (f32[5374]{0:T(1024)S(1)}, f32[5374]{0:T(1024)S(1)}, u32[]{:S(2)}, u32[]{:S(2)}) collective-permute-start(f32[5374]{0:T(1024)S(1)} %select_add_fusion.4), channel_id=1, source_target_pairs={{0,16},{1,17},{2,18},{3,19},{4,20},{5,21},{6,22},{7,23},{8,24},{9,... | collective-permute-start | bytes 64496 | tf_op jit(solution)/shard_map/ppermute | solution.py:36
  174.2 4.2 %collective-permute-start.18 = (f32[10748]{0:T(1024)S(1)}, f32[10748]{0:T(1024)S(1)}, u32[]{:S(2)}, u32[]{:S(2)}) collective-permute-start(f32[10748]{0:T(1024)S(1)} %maximum_select_fusion.5), channel_id=1, source_target_pairs={{0,8},{1,9},{2,10},{3,11},{4,12},{5,13},{6,14},{7,15},{8,0},{9,1},... | collective-permute-start | bytes 128984 | tf_op jit(solution)/shard_map/ppermute | solution.py:36
  178.5 4.6 %collective-permute-start.19 = (f32[21496]{0:T(1024)S(1)}, f32[21496]{0:T(1024)S(1)}, u32[]{:S(2)}, u32[]{:S(2)}) collective-permute-start(f32[21496]{0:T(1024)S(1)} %maximum_select_fusion.4), channel_id=1, source_target_pairs={{0,4},{1,5},{2,6},{3,7},{4,0},{5,1},{6,2},{7,3},{8,12},{9,13},{10,... | collective-permute-start | bytes 257960 | tf_op jit(solution)/shard_map/ppermute | solution.py:36
  183.2 5.5 %collective-permute-start.20 = (f32[42992]{0:T(1024)S(1)}, f32[42992]{0:T(1024)S(1)}, u32[]{:S(2)}, u32[]{:S(2)}) collective-permute-start(f32[42992]{0:T(1024)S(1)} %maximum_select_fusion.3), channel_id=1, source_target_pairs={{0,2},{1,3},{2,0},{3,1},{4,6},{5,7},{6,4},{7,5},{8,10},{9,11},{10,... | collective-permute-start | bytes 515912 | tf_op jit(solution)/shard_map/ppermute | solution.py:36
  188.9 10.1 %collective-permute-start.21 = (f32[85984]{0:T(1024)S(1)}, f32[85984]{0:T(1024)S(1)}, u32[]{:S(2)}, u32[]{:S(2)}) collective-permute-start(f32[85984]{0:T(1024)S(1)} %maximum_select_fusion.2), channel_id=1, source_target_pairs={{0,1},{1,0},{2,3},{3,2},{4,5},{5,4},{6,7},{7,6},{8,9},{9,8},{10,11... | collective-permute-start | bytes 1031816 | tf_op jit(solution)/shard_map/ppermute | solution.py:36
  (76 other events, 339.6 us)

commit v3 on v2

--- a/solution.py
+++ b/solution.py
@@ -106,6 +106,16 @@
     return field[:, tap // 4 :: 2, tap // 2 % 2 :: 2, tap % 2 :: 2]
 
 
+def parity(field):
+    chans, depth, height, width = field.shape
+    return field.reshape(chans, depth // 2, 2, height // 2, 2, width // 2, 2)
+
+
+def unparity(cube):
+    shape = cube.shape
+    return cube.reshape(shape[0], shape[1] * 2, shape[3] * 2, shape[5] * 2)
+
+
 def alternate(parts):
     chans, depth, height, width = parts.shape[1:]
     return (
@@ -160,12 +170,11 @@
         h0_wide[:, 1:-1, 1:-1, 1:-1].astype(single_float) + convolve(h0_wide, w_res)
     ).astype(brain_float_half)
     h1 = h1_wide[:, 2:-2, :, 2:-2]
-    down_sum = None
-    for tap in range(8):
-        term = jnp.einsum(
-            "oc,czyx->ozyx", w_down[tap], strided(h1_wide, tap), preferred_element_type=single_float
-        )
-        down_sum = term if down_sum is None else down_sum + term
+    down_cube = w_down.reshape((2, 2, 2) + w_down.shape[1:])
+    up_cube = w_up.reshape((2, 2, 2) + w_up.shape[1:])
+    down_sum = jnp.einsum(
+        "abeoc,czaybxe->ozyx", down_cube, parity(h1_wide), preferred_element_type=single_float
+    )
     d_wide = jnp.where(
         inside(
             down_sum.shape,
@@ -182,13 +191,8 @@
     cfield = jax.nn.relu(dfield.astype(single_float) + convolve(dfield_pad, w_mid)).astype(
         brain_float_half
     )
-    upward = alternate(
-        jnp.stack(
-            [
-                jnp.einsum("oc,czyx->ozyx", w_up[tap], cfield, preferred_element_type=single_float)
-                for tap in range(8)
-            ]
-        )
+    upward = unparity(
+        jnp.einsum("abeoc,czyx->ozaybxe", up_cube, cfield, preferred_element_type=single_float)
     )
     signal_field = jax.nn.relu(h1.astype(single_float) + upward).astype(brain_float_half)
     logits = jnp.einsum(
@@ -214,37 +218,20 @@
         "jn,jbrq->nbrq", head_weight, logit_gradient, preferred_element_type=single_float
     )
     gsf = jnp.where(signal_field > 0, gradient_total, 0.0).astype(brain_float_half)
-    grad_up = jnp.stack(
-        [
-            jnp.einsum(
-                "ozyx,czyx->oc", strided(gsf, tap), cfield, preferred_element_type=single_float
-            )
-            for tap in range(8)
-        ]
-    )
-    gcoarse = None
-    for tap in range(8):
-        term = jnp.einsum(
-            "oc,ozyx->czyx", w_up[tap], strided(gsf, tap), preferred_element_type=single_float
-        )
-        gcoarse = term if gcoarse is None else gcoarse + term
+    gs_cube = parity(gsf)
+    grad_up = jnp.einsum(
+        "ozaybxe,czyx->abeoc", gs_cube, cfield, preferred_element_type=single_float
+    ).reshape(w_up.shape)
+    gcoarse = jnp.einsum("abeoc,ozaybxe->czyx", up_cube, gs_cube, preferred_element_type=single_float)
     gquad = jnp.where(cfield > 0, gcoarse, 0.0).astype(brain_float_half)
     grad_mid = tap_grads(gquad, dfield_pad)
     gdown = gquad.astype(single_float) + convolve(framed(gquad), flipped(w_mid))
     gdd = jnp.where(dfield > 0, gdown, 0.0).astype(brain_float_half)
-    grad_down = jnp.stack(
-        [
-            jnp.einsum("ozyx,czyx->oc", gdd, strided(h1, tap), preferred_element_type=single_float)
-            for tap in range(8)
-        ]
-    )
-    spread = alternate(
-        jnp.stack(
-            [
-                jnp.einsum("oc,ozyx->czyx", w_down[tap], gdd, preferred_element_type=single_float)
-                for tap in range(8)
-            ]
-        )
+    grad_down = jnp.einsum(
+        "ozyx,czaybxe->abeoc", gdd, parity(h1), preferred_element_type=single_float
+    ).reshape(w_down.shape)
+    spread = unparity(
+        jnp.einsum("abeoc,ozyx->czaybxe", down_cube, gdd, preferred_element_type=single_float)
     )
     gres = jnp.where(h1 > 0, gsf.astype(single_float) + spread, 0.0).astype(brain_float_half)
     grad_res = tap_grads(gres, h0_pad)

time: 207 us -> 198 us (0.957)
  local copies, waits for them, and re-layouts: 51.9 us -> 39.2 us
  matrix products: 42.5 us -> 45.9 us
    slice x24 -> x0, local copies, waits for them, and re-layouts: 27.6 us -> none  [strided(): return field[:, tap // 4::2, tap // 2 % 2::2, tap % 2::2]]
    unnamed x179 -> x177, local copies, waits for them, and re-layouts: 6.06 us -> 16 us
    dot_general x64, matrix products: 10.2 us -> 17.3 us  [tap_grads(): jnp.einsum('ozyx,czyx->oc', grad, window, preferred_element_type=jnp.floa...]
    dot_general x48 -> x6, matrix products: 7.42 us -> 2.98 us  [the longest x1 1.76 us: local(): jnp.einsum('abeoc,czaybxe->ozyx', down_cube, parity(h1_wide), preferred_e...]
  transfers between devices with their start and end apart: 23 -> 23, of which waited for: 13 -> 14; matrix products, arithmetic and copies ran while one was open for 14% -> 10% of each run, Pallas kernels for 0% -> 0%
where the time goes in v3:
time: 198 us; the launch traced here: 197 us
  starting transfers between devices  56.7 us (29%)
  matrix products  45.9 us (23%)
  local copies, waits for them, and re-layouts  39.2 us (20%)
  waiting for transfers between devices  35.4 us (18%)
  other arithmetic  8.67 us (4%)
  blocking collectives  8.22 us (4%)
  between operations  3.02 us (2%)
    dot_general x108, matrix products, convolve(): jnp.einsum('oc,czyx->ozyx', weights[tap], window, preferred_element_type=...  23.9 us
    ppermute x6, starting transfers between devices, with_halo(): lax.ppermute(tail, axis, [(i, (i + 1) % count) for i in range(ends)])  21.7 us
    dot_general x64, matrix products, tap_grads(): jnp.einsum('ozyx,czyx->oc', grad, window, preferred_element_type=jnp.floa...  17.3 us
    unnamed x177, local copies, waits for them, and re-layouts  16 us
    ppermute x5, starting transfers between devices, tree_sum(): cur = keep + lax.ppermute(send, axes, pairs)  14.5 us
    ppermute x5, waiting for transfers between devices, tree_sum(): cur = keep + lax.ppermute(send, axes, pairs)  14.3 us
    ppermute x5, waiting for transfers between devices, tree_sum(): other = lax.ppermute(cur, axes, pairs)  11.7 us
    all_to_all x1, blocking collectives, local(): lax.all_to_all(sending, 'xy', split_axis=0, concat_axis=0, tiled=True)  8.22 us
  transfers between devices with their start and end apart: 23, of which 14 were waited for; matrix products, arithmetic and copies ran while one was open for 10% of the time, Pallas kernels for 0%

profile of v3, /device:TPU:0, one launch (start us, length us, event | category | flops | bytes accessed | tf_op | source)
XLA Modules:
  0.0 197.1 jit_solution(260297877933372332)
XLA Ops:
  4.6 5.2 %all-to-all-start = ((bf16[8,2,4,4,2,128]{5,1,4,3,2,0:T(2,128)(2,1)}), bf16[8,2,4,4,2,128]{5,1,4,3,2,0:T(2,128)(2,1)S(1)}, u32[]{:S(2)}, u32[]{:S(2)}) async-start(bf16[8,2,4,4,2,128]{5,1,4,3,2,0:T(2,128)(2,1)} %copy.247), calls=%async_computation | async-start | bytes 262144 | tf_op jit(solution)/shard_map/all_to_all | solution.py:148
  18.1 4.5 %collective-permute-start = (bf16[1,4,2,256]{3,2,1,0:T(2,128)(2,1)S(1)}, bf16[1,4,2,256]{3,2,1,0:T(2,128)(2,1)S(1)}, u32[]{:S(2)}, u32[]{:S(2)}) collective-permute-start(bf16[1,4,2,256]{3,2,1,0:T(2,128)(2,1)S(1)} %reshape.936), channel_id=1, source_target_pairs={{0,8},{8,16},{16,24},{1,9},{9,17},{17,25},{2,10},{10,18},{18,26},{... | collective-permute-start | bytes 12296 | tf_op jit(solution)/shard_map/ppermute | solution.py:64
  28.5 2.8 %collective-permute-done.3 = bf16[1,12,2,4]{3,2,1,0:T(2,128)(2,1)S(1)} collective-permute-done((bf16[1,12,2,4]{3,2,1,0:T(2,128)(2,1)S(1)}, bf16[1,12,2,4]{3,2,1,0:T(2,128)(2,1)S(1)}, u32[]{:S(2)}, u32[]{:S(2)}) %collective-permute-start.3) | collective-permute-done | bytes 224 | tf_op jit(solution)/shard_map/ppermute | solution.py:66
  32.5 2.0 %fusion.144 = bf16[32,10,2,262]{3,0,2,1:T(8,128)(2,1)S(1)} fusion(f32[32]{0:T(128)S(1)} %get-tuple-element.157, f32[10,2,262]{2,1,0:T(2,128)S(1)} %get-tuple-element.117, f32[32]{0:T(128)S(1)} %get-tuple-element.158, f32[10,2,262]{2,1,0:T(2,128)S(1)} %get-tuple-element.116, f32[32]{0:T(128)S(1)} %get-tuple-element.133, ...), kind=kLoop, calls=%fused_computation.351 | loop fusion | flops 9390080 | bytes 907356 | tf_op jit(solution)/shard_map/convert_element_type | solution.py:165
  52.6 2.0 %pad_slice_fusion = (bf16[32,4,2,256]{3,0,2,1:T(8,128)(2,1)}, bf16[32,4,2,256]{3,0,2,1:T(8,128)(2,1)}, bf16[32,4,2,256]{3,0,2,1:T(8,128)(2,1)}, bf16[32,4,2,256]...) fusion(bf16[32,10,2,262]{3,0,2,1:T(8,128)(2,1)S(1)} %fusion.144), kind=kLoop, calls=%fused_computation | loop fusion | bytes 3112960 | tf_op jit(solution)/shard_map/slice | solution.py:96
  74.9 4.2 %collective-permute-start.4 = (bf16[64,1,1,128]{3,0,1,2:T(8,128)(2,1)S(1)}, bf16[64,1,1,128]{3,0,1,2:T(8,128)(2,1)S(1)}, u32[]{:S(2)}, u32[]{:S(2)}) collective-permute-start(bf16[64,1,1,128]{3,0,1,2:T(8,128)(2,1)S(1)} %get-tuple-element.74), channel_id=1, source_target_pairs={{0,8},{8,16},{16,24},{1,9},{9,17},{17,25},{2,10},{10,18},{18,26},{... | collective-permute-start | bytes 49160 | tf_op jit(solution)/shard_map/ppermute | solution.py:64
  86.2 3.7 %collective-permute-start.6 = (bf16[64,4,1,1]{3,0,1,2:T(8,128)(2,1)S(1)}, bf16[64,4,1,1]{3,0,1,2:T(8,128)(2,1)S(1)}, u32[]{:S(2)}, u32[]{:S(2)}) collective-permute-start(bf16[64,4,1,1]{3,0,1,2:T(8,128)(2,1)S(1)} %get-tuple-element.70), channel_id=1, source_target_pairs={{0,1},{1,2},{2,3},{3,4},{4,5},{5,6},{6,7},{8,9},{9,10},{10,11},{11... | collective-permute-start | bytes 1544 | tf_op jit(solution)/shard_map/ppermute | solution.py:64
  95.9 4.3 %collective-permute-start.8 = (bf16[32,1,2,256]{3,0,2,1:T(8,128)(2,1)S(1)}, bf16[32,1,2,256]{3,0,2,1:T(8,128)(2,1)S(1)}, u32[]{:S(2)}, u32[]{:S(2)}) collective-permute-start(bf16[32,1,2,256]{3,0,2,1:T(8,128)(2,1)S(1)} %get-tuple-element.68), channel_id=1, source_target_pairs={{0,8},{8,16},{16,24},{1,9},{9,17},{17,25},{2,10},{10,18},{18,26},{... | collective-permute-start | bytes 98312 | tf_op jit(solution)/shard_map/ppermute | solution.py:64
  108.1 3.8 %collective-permute-start.10 = (bf16[32,6,2,1]{3,0,2,1:T(8,128)(2,1)S(1)}, bf16[32,6,2,1]{3,0,2,1:T(8,128)(2,1)S(1)}, u32[]{:S(2)}, u32[]{:S(2)}) collective-permute-start(bf16[32,6,2,1]{3,0,2,1:T(8,128)(2,1)S(1)} %get-tuple-element.66), channel_id=1, source_target_pairs={{0,1},{1,2},{2,3},{3,4},{4,5},{5,6},{6,7},{8,9},{9,10},{10,11},{11... | collective-permute-start | bytes 2312 | tf_op jit(solution)/shard_map/ppermute | solution.py:64
  113.4 3.8 %collective-permute-done.11 = bf16[32,6,2,1]{3,0,2,1:T(8,128)(2,1)S(1)} collective-permute-done((bf16[32,6,2,1]{3,0,2,1:T(8,128)(2,1)S(1)}, bf16[32,6,2,1]{3,0,2,1:T(8,128)(2,1)S(1)}, u32[]{:S(2)}, u32[]{:S(2)}) %collective-permute-start.11) | collective-permute-done | bytes 800 | tf_op jit(solution)/shard_map/ppermute | solution.py:66
  127.5 3.5 %concatenate.133 = f32[155488]{0:T(1024)S(1)} concatenate(f32[864]{0:T(1024)S(1)} %reshape_squeeze.3, f32[27648]{0:T(1024)S(1)} %reshape.1048, f32[16384]{0:T(1024)S(1)} %reshape_reshape.7, f32[110592]{0:T(1024)S(1)} %reshape.1009), dimensions={0} | concatenate | bytes 1243904 | tf_op jit(solution)/shard_map/concatenate | solution.py:15
  131.2 4.3 %collective-permute-start.12 = (f32[85984]{0:T(1024)S(1)}, f32[85984]{0:T(1024)S(1)}, u32[]{:S(2)}, u32[]{:S(2)}) collective-permute-start(f32[85984]{0:T(1024)S(1)} %slice_select_fusion), channel_id=1, source_target_pairs={{0,1},{1,0},{2,3},{3,2},{4,5},{5,4},{6,7},{7,6},{8,9},{9,8},{10,11... | collective-permute-start | bytes 1031816 | tf_op jit(solution)/shard_map/ppermute | solution.py:31
  136.9 4.1 %collective-permute-start.13 = (f32[42992]{0:T(1024)S(1)}, f32[42992]{0:T(1024)S(1)}, u32[]{:S(2)}, u32[]{:S(2)}) collective-permute-start(f32[42992]{0:T(1024)S(1)} %slice_select_fusion.1), channel_id=1, source_target_pairs={{0,2},{1,3},{2,0},{3,1},{4,6},{5,7},{6,4},{7,5},{8,10},{9,11},{10,... | collective-permute-start | bytes 515912 | tf_op jit(solution)/shard_map/ppermute | solution.py:31
  141.0 4.9 %collective-permute-done.13 = f32[42992]{0:T(1024)S(1)} collective-permute-done((f32[42992]{0:T(1024)S(1)}, f32[42992]{0:T(1024)S(1)}, u32[]{:S(2)}, u32[]{:S(2)}) %collective-permute-start.13) | collective-permute-done | bytes 172000 | tf_op jit(solution)/shard_map/ppermute | solution.py:31
  146.5 4.3 %collective-permute-done.14 = f32[21496]{0:T(1024)S(1)} collective-permute-done((f32[21496]{0:T(1024)S(1)}, f32[21496]{0:T(1024)S(1)}, u32[]{:S(2)}, u32[]{:S(2)}) %collective-permute-start.14) | collective-permute-done | bytes 86016 | tf_op jit(solution)/shard_map/ppermute | solution.py:31
  150.9 2.7 %collective-permute-start.15 = (f32[10748]{0:T(1024)S(1)}, f32[10748]{0:T(1024)S(1)}, u32[]{:S(2)}, u32[]{:S(2)}) collective-permute-start(f32[10748]{0:T(1024)S(1)} %slice_select_fusion.3), channel_id=1, source_target_pairs={{0,8},{1,9},{2,10},{3,11},{4,12},{5,13},{6,14},{7,15},{8,0},{9,1},... | collective-permute-start | bytes 128984 | tf_op jit(solution)/shard_map/ppermute | solution.py:31
  153.6 2.0 %collective-permute-done.15 = f32[10748]{0:T(1024)S(1)} collective-permute-done((f32[10748]{0:T(1024)S(1)}, f32[10748]{0:T(1024)S(1)}, u32[]{:S(2)}, u32[]{:S(2)}) %collective-permute-start.15) | collective-permute-done | bytes 43024 | tf_op jit(solution)/shard_map/ppermute | solution.py:31
  155.8 3.0 %collective-permute-start.16 = (f32[5374]{0:T(1024)S(1)}, f32[5374]{0:T(1024)S(1)}, u32[]{:S(2)}, u32[]{:S(2)}) collective-permute-start(f32[5374]{0:T(1024)S(1)} %slice_select_fusion.4), channel_id=1, source_target_pairs={{0,16},{1,17},{2,18},{3,19},{4,20},{5,21},{6,22},{7,23},{8,24},{9,... | collective-permute-start | bytes 64496 | tf_op jit(solution)/shard_map/ppermute | solution.py:31
  160.8 3.0 %collective-permute-start.17 = (f32[5374]{0:T(1024)S(1)}, f32[5374]{0:T(1024)S(1)}, u32[]{:S(2)}, u32[]{:S(2)}) collective-permute-start(f32[5374]{0:T(1024)S(1)} %select_add_fusion.4), channel_id=1, source_target_pairs={{0,16},{1,17},{2,18},{3,19},{4,20},{5,21},{6,22},{7,23},{8,24},{9,... | collective-permute-start | bytes 64496 | tf_op jit(solution)/shard_map/ppermute | solution.py:36
  165.7 2.2 %collective-permute-start.18 = (f32[10748]{0:T(1024)S(1)}, f32[10748]{0:T(1024)S(1)}, u32[]{:S(2)}, u32[]{:S(2)}) collective-permute-start(f32[10748]{0:T(1024)S(1)} %maximum_select_fusion.5), channel_id=1, source_target_pairs={{0,8},{1,9},{2,10},{3,11},{4,12},{5,13},{6,14},{7,15},{8,0},{9,1},... | collective-permute-start | bytes 128984 | tf_op jit(solution)/shard_map/ppermute | solution.py:36
  167.9 2.0 %collective-permute-done.18 = f32[10748]{0:T(1024)S(1)} collective-permute-done((f32[10748]{0:T(1024)S(1)}, f32[10748]{0:T(1024)S(1)}, u32[]{:S(2)}, u32[]{:S(2)}) %collective-permute-start.18) | collective-permute-done | bytes 43024 | tf_op jit(solution)/shard_map/ppermute | solution.py:36
  170.3 4.3 %collective-permute-done.19 = f32[21496]{0:T(1024)S(1)} collective-permute-done((f32[21496]{0:T(1024)S(1)}, f32[21496]{0:T(1024)S(1)}, u32[]{:S(2)}, u32[]{:S(2)}) %collective-permute-start.19) | collective-permute-done | bytes 86016 | tf_op jit(solution)/shard_map/ppermute | solution.py:36
  176.6 3.5 %collective-permute-done.20 = f32[42992]{0:T(1024)S(1)} collective-permute-done((f32[42992]{0:T(1024)S(1)}, f32[42992]{0:T(1024)S(1)}, u32[]{:S(2)}, u32[]{:S(2)}) %collective-permute-start.20) | collective-permute-done | bytes 172000 | tf_op jit(solution)/shard_map/ppermute | solution.py:36
  180.5 8.2 %all_to_all.10 = bf16[8,2,3,4,2,128]{5,1,4,3,2,0:T(2,128)(2,1)S(1)} all-to-all(bf16[8,2,3,4,2,128]{5,1,4,3,2,0:T(2,128)(2,1)S(1)} %broadcast_in_dim.32), channel_id=1, replica_groups=mesh['gz'=4,'xy'=8] {'xy'}, dimensions={0} | all-to-all | bytes 196608 | tf_op jit(solution)/shard_map/all_to_all | solution.py:206
  (474 shorter events, 105.6 us)
Async XLA Ops:
  0.6 43.3 %copy-start = (bf16[8,64,32]{1,2,0:T(8,128)(2,1)S(1)}, bf16[8,64,32]{1,2,0:T(8,128)(2,1)}, u32[]{:S(2)}) copy-start(bf16[8,64,32]{1,2,0:T(8,128)(2,1)} %param.16) | copy-start | bytes 98308
  4.6 12.1 %all-to-all-start = ((bf16[8,2,4,4,2,128]{5,1,4,3,2,0:T(2,128)(2,1)}), bf16[8,2,4,4,2,128]{5,1,4,3,2,0:T(2,128)(2,1)S(1)}, u32[]{:S(2)}, u32[]{:S(2)}) async-start(bf16[8,2,4,4,2,128]{5,1,4,3,2,0:T(2,128)(2,1)} %copy.247), calls=%async_computation | async-start | bytes 262144 | tf_op jit(solution)/shard_map/all_to_all | solution.py:148
  16.8 5.9 %collective-permute-start.1 = (bf16[1,4,2,256]{3,2,1,0:T(2,128)(2,1)S(1)}, bf16[1,4,2,256]{3,2,1,0:T(2,128)(2,1)S(1)}, u32[]{:S(2)}, u32[]{:S(2)}) collective-permute-start(bf16[1,4,2,256]{3,2,1,0:T(2,128)(2,1)S(1)} %reshape.936), channel_id=1, source_target_pairs={{8,0},{16,8},{24,16},{9,1},{17,9},{25,17},{10,2},{18,10},{26,18},{... | collective-permute-start | bytes 12296 | tf_op jit(solution)/shard_map/ppermute | solution.py:66
  18.1 5.9 %collective-permute-start = (bf16[1,4,2,256]{3,2,1,0:T(2,128)(2,1)S(1)}, bf16[1,4,2,256]{3,2,1,0:T(2,128)(2,1)S(1)}, u32[]{:S(2)}, u32[]{:S(2)}) collective-permute-start(bf16[1,4,2,256]{3,2,1,0:T(2,128)(2,1)S(1)} %reshape.936), channel_id=1, source_target_pairs={{0,8},{8,16},{16,24},{1,9},{9,17},{17,25},{2,10},{10,18},{18,26},{... | collective-permute-start | bytes 12296 | tf_op jit(solution)/shard_map/ppermute | solution.py:64
  24.7 3.8 %collective-permute-start.2 = (bf16[1,12,2,4]{3,2,1,0:T(2,128)(2,1)S(1)}, bf16[1,12,2,4]{3,2,1,0:T(2,128)(2,1)S(1)}, u32[]{:S(2)}, u32[]{:S(2)}) collective-permute-start(bf16[1,12,2,4]{3,2,1,0:T(2,128)(2,1)S(1)} %get-tuple-element.130), channel_id=1, source_target_pairs={{0,1},{1,2},{2,3},{3,4},{4,5},{5,6},{6,7},{8,9},{9,10},{10,11},{11... | collective-permute-start | bytes 584 | tf_op jit(solution)/shard_map/ppermute | solution.py:64
  26.0 5.3 %collective-permute-start.3 = (bf16[1,12,2,4]{3,2,1,0:T(2,128)(2,1)S(1)}, bf16[1,12,2,4]{3,2,1,0:T(2,128)(2,1)S(1)}, u32[]{:S(2)}, u32[]{:S(2)}) collective-permute-start(bf16[1,12,2,4]{3,2,1,0:T(2,128)(2,1)S(1)} %get-tuple-element.131), channel_id=1, source_target_pairs={{1,0},{2,1},{3,2},{4,3},{5,4},{6,5},{7,6},{9,8},{10,9},{11,10},{12... | collective-permute-start | bytes 584 | tf_op jit(solution)/shard_map/ppermute | solution.py:66
  74.9 8.8 %collective-permute-start.4 = (bf16[64,1,1,128]{3,0,1,2:T(8,128)(2,1)S(1)}, bf16[64,1,1,128]{3,0,1,2:T(8,128)(2,1)S(1)}, u32[]{:S(2)}, u32[]{:S(2)}) collective-permute-start(bf16[64,1,1,128]{3,0,1,2:T(8,128)(2,1)S(1)} %get-tuple-element.74), channel_id=1, source_target_pairs={{0,8},{8,16},{16,24},{1,9},{9,17},{17,25},{2,10},{10,18},{18,26},{... | collective-permute-start | bytes 49160 | tf_op jit(solution)/shard_map/ppermute | solution.py:64
  79.1 5.6 %collective-permute-start.5 = (bf16[64,1,1,128]{3,0,1,2:T(8,128)(2,1)S(1)}, bf16[64,1,1,128]{3,0,1,2:T(8,128)(2,1)S(1)}, u32[]{:S(2)}, u32[]{:S(2)}) collective-permute-start(bf16[64,1,1,128]{3,0,1,2:T(8,128)(2,1)S(1)} %get-tuple-element.75), channel_id=1, source_target_pairs={{8,0},{16,8},{24,16},{9,1},{17,9},{25,17},{10,2},{18,10},{26,18},{... | collective-permute-start | bytes 49160 | tf_op jit(solution)/shard_map/ppermute | solution.py:66
  84.9 5.1 %collective-permute-start.7 = (bf16[64,4,1,1]{3,0,1,2:T(8,128)(2,1)S(1)}, bf16[64,4,1,1]{3,0,1,2:T(8,128)(2,1)S(1)}, u32[]{:S(2)}, u32[]{:S(2)}) collective-permute-start(bf16[64,4,1,1]{3,0,1,2:T(8,128)(2,1)S(1)} %get-tuple-element.71), channel_id=1, source_target_pairs={{1,0},{2,1},{3,2},{4,3},{5,4},{6,5},{7,6},{9,8},{10,9},{11,10},{12... | collective-permute-start | bytes 1544 | tf_op jit(solution)/shard_map/ppermute | solution.py:66
  86.2 4.5 %collective-permute-start.6 = (bf16[64,4,1,1]{3,0,1,2:T(8,128)(2,1)S(1)}, bf16[64,4,1,1]{3,0,1,2:T(8,128)(2,1)S(1)}, u32[]{:S(2)}, u32[]{:S(2)}) collective-permute-start(bf16[64,4,1,1]{3,0,1,2:T(8,128)(2,1)S(1)} %get-tuple-element.70), channel_id=1, source_target_pairs={{0,1},{1,2},{2,3},{3,4},{4,5},{5,6},{6,7},{8,9},{9,10},{10,11},{11... | collective-permute-start | bytes 1544 | tf_op jit(solution)/shard_map/ppermute | solution.py:64
  95.9 12.0 %collective-permute-start.8 = (bf16[32,1,2,256]{3,0,2,1:T(8,128)(2,1)S(1)}, bf16[32,1,2,256]{3,0,2,1:T(8,128)(2,1)S(1)}, u32[]{:S(2)}, u32[]{:S(2)}) collective-permute-start(bf16[32,1,2,256]{3,0,2,1:T(8,128)(2,1)S(1)} %get-tuple-element.68), channel_id=1, source_target_pairs={{0,8},{8,16},{16,24},{1,9},{9,17},{17,25},{2,10},{10,18},{18,26},{... | collective-permute-start | bytes 98312 | tf_op jit(solution)/shard_map/ppermute | solution.py:64
  100.2 7.7 %collective-permute-start.9 = (bf16[32,1,2,256]{3,0,2,1:T(8,128)(2,1)S(1)}, bf16[32,1,2,256]{3,0,2,1:T(8,128)(2,1)S(1)}, u32[]{:S(2)}, u32[]{:S(2)}) collective-permute-start(bf16[32,1,2,256]{3,0,2,1:T(8,128)(2,1)S(1)} %get-tuple-element.69), channel_id=1, source_target_pairs={{8,0},{16,8},{24,16},{9,1},{17,9},{25,17},{10,2},{18,10},{26,18},{... | collective-permute-start | bytes 98312 | tf_op jit(solution)/shard_map/ppermute | solution.py:66
  108.1 5.3 %collective-permute-start.10 = (bf16[32,6,2,1]{3,0,2,1:T(8,128)(2,1)S(1)}, bf16[32,6,2,1]{3,0,2,1:T(8,128)(2,1)S(1)}, u32[]{:S(2)}, u32[]{:S(2)}) collective-permute-start(bf16[32,6,2,1]{3,0,2,1:T(8,128)(2,1)S(1)} %get-tuple-element.66), channel_id=1, source_target_pairs={{0,1},{1,2},{2,3},{3,4},{4,5},{5,6},{6,7},{8,9},{9,10},{10,11},{11... | collective-permute-start | bytes 2312 | tf_op jit(solution)/shard_map/ppermute | solution.py:64
  111.9 5.3 %collective-permute-start.11 = (bf16[32,6,2,1]{3,0,2,1:T(8,128)(2,1)S(1)}, bf16[32,6,2,1]{3,0,2,1:T(8,128)(2,1)S(1)}, u32[]{:S(2)}, u32[]{:S(2)}) collective-permute-start(bf16[32,6,2,1]{3,0,2,1:T(8,128)(2,1)S(1)} %get-tuple-element.67), channel_id=1, source_target_pairs={{1,0},{2,1},{3,2},{4,3},{5,4},{6,5},{7,6},{9,8},{10,9},{11,10},{12... | collective-permute-start | bytes 2312 | tf_op jit(solution)/shard_map/ppermute | solution.py:66
  131.2 5.6 %collective-permute-start.12 = (f32[85984]{0:T(1024)S(1)}, f32[85984]{0:T(1024)S(1)}, u32[]{:S(2)}, u32[]{:S(2)}) collective-permute-start(f32[85984]{0:T(1024)S(1)} %slice_select_fusion), channel_id=1, source_target_pairs={{0,1},{1,0},{2,3},{3,2},{4,5},{5,4},{6,7},{7,6},{8,9},{9,8},{10,11... | collective-permute-start | bytes 1031816 | tf_op jit(solution)/shard_map/ppermute | solution.py:31
  136.9 9.1 %collective-permute-start.13 = (f32[42992]{0:T(1024)S(1)}, f32[42992]{0:T(1024)S(1)}, u32[]{:S(2)}, u32[]{:S(2)}) collective-permute-start(f32[42992]{0:T(1024)S(1)} %slice_select_fusion.1), channel_id=1, source_target_pairs={{0,2},{1,3},{2,0},{3,1},{4,6},{5,7},{6,4},{7,5},{8,10},{9,11},{10,... | collective-permute-start | bytes 515912 | tf_op jit(solution)/shard_map/ppermute | solution.py:31
  146.2 4.6 %collective-permute-start.14 = (f32[21496]{0:T(1024)S(1)}, f32[21496]{0:T(1024)S(1)}, u32[]{:S(2)}, u32[]{:S(2)}) collective-permute-start(f32[21496]{0:T(1024)S(1)} %slice_select_fusion.2), channel_id=1, source_target_pairs={{0,4},{1,5},{2,6},{3,7},{4,0},{5,1},{6,2},{7,3},{8,12},{9,13},{10,... | collective-permute-start | bytes 257960 | tf_op jit(solution)/shard_map/ppermute | solution.py:31
  150.9 4.7 %collective-permute-start.15 = (f32[10748]{0:T(1024)S(1)}, f32[10748]{0:T(1024)S(1)}, u32[]{:S(2)}, u32[]{:S(2)}) collective-permute-start(f32[10748]{0:T(1024)S(1)} %slice_select_fusion.3), channel_id=1, source_target_pairs={{0,8},{1,9},{2,10},{3,11},{4,12},{5,13},{6,14},{7,15},{8,0},{9,1},... | collective-permute-start | bytes 128984 | tf_op jit(solution)/shard_map/ppermute | solution.py:31
  155.8 4.9 %collective-permute-start.16 = (f32[5374]{0:T(1024)S(1)}, f32[5374]{0:T(1024)S(1)}, u32[]{:S(2)}, u32[]{:S(2)}) collective-permute-start(f32[5374]{0:T(1024)S(1)} %slice_select_fusion.4), channel_id=1, source_target_pairs={{0,16},{1,17},{2,18},{3,19},{4,20},{5,21},{6,22},{7,23},{8,24},{9,... | collective-permute-start | bytes 64496 | tf_op jit(solution)/shard_map/ppermute | solution.py:31
  160.8 4.8 %collective-permute-start.17 = (f32[5374]{0:T(1024)S(1)}, f32[5374]{0:T(1024)S(1)}, u32[]{:S(2)}, u32[]{:S(2)}) collective-permute-start(f32[5374]{0:T(1024)S(1)} %select_add_fusion.4), channel_id=1, source_target_pairs={{0,16},{1,17},{2,18},{3,19},{4,20},{5,21},{6,22},{7,23},{8,24},{9,... | collective-permute-start | bytes 64496 | tf_op jit(solution)/shard_map/ppermute | solution.py:36
  165.7 4.2 %collective-permute-start.18 = (f32[10748]{0:T(1024)S(1)}, f32[10748]{0:T(1024)S(1)}, u32[]{:S(2)}, u32[]{:S(2)}) collective-permute-start(f32[10748]{0:T(1024)S(1)} %maximum_select_fusion.5), channel_id=1, source_target_pairs={{0,8},{1,9},{2,10},{3,11},{4,12},{5,13},{6,14},{7,15},{8,0},{9,1},... | collective-permute-start | bytes 128984 | tf_op jit(solution)/shard_map/ppermute | solution.py:36
  170.0 4.6 %collective-permute-start.19 = (f32[21496]{0:T(1024)S(1)}, f32[21496]{0:T(1024)S(1)}, u32[]{:S(2)}, u32[]{:S(2)}) collective-permute-start(f32[21496]{0:T(1024)S(1)} %maximum_select_fusion.4), channel_id=1, source_target_pairs={{0,4},{1,5},{2,6},{3,7},{4,0},{5,1},{6,2},{7,3},{8,12},{9,13},{10,... | collective-permute-start | bytes 257960 | tf_op jit(solution)/shard_map/ppermute | solution.py:36
  174.7 5.5 %collective-permute-start.20 = (f32[42992]{0:T(1024)S(1)}, f32[42992]{0:T(1024)S(1)}, u32[]{:S(2)}, u32[]{:S(2)}) collective-permute-start(f32[42992]{0:T(1024)S(1)} %maximum_select_fusion.3), channel_id=1, source_target_pairs={{0,2},{1,3},{2,0},{3,1},{4,6},{5,7},{6,4},{7,5},{8,10},{9,11},{10,... | collective-permute-start | bytes 515912 | tf_op jit(solution)/shard_map/ppermute | solution.py:36
  180.3 10.1 %collective-permute-start.21 = (f32[85984]{0:T(1024)S(1)}, f32[85984]{0:T(1024)S(1)}, u32[]{:S(2)}, u32[]{:S(2)}) collective-permute-start(f32[85984]{0:T(1024)S(1)} %maximum_select_fusion.2), channel_id=1, source_target_pairs={{0,1},{1,0},{2,3},{3,2},{4,5},{5,4},{6,7},{7,6},{8,9},{9,8},{10,11... | collective-permute-start | bytes 1031816 | tf_op jit(solution)/shard_map/ppermute | solution.py:36
  (75 other events, 321.6 us)

commit v4 on v3

--- a/solution.py
+++ b/solution.py
@@ -75,27 +75,29 @@
     return jnp.pad(padded, ((0, 0), (0, 0), (1, 1), (0, 0)))
 
 
-def convolve(padded, weights):
+def windows(padded):
     depth = padded.shape[1] - 2
     height = padded.shape[2] - 2
     width = padded.shape[3] - 2
-    total = None
+    cols = []
     for tap in range(27):
         off_z, off_y, off_x = (tap // 9, tap // 3 % 3, tap % 3)
-        window = padded[:, off_z : off_z + depth, off_y : off_y + height, off_x : off_x + width]
-        term = jnp.einsum("oc,czyx->ozyx", weights[tap], window, preferred_element_type=jnp.float32)
-        total = term if total is None else total + term
-    return total
+        cols.append(
+            padded[:, off_z : off_z + depth, off_y : off_y + height, off_x : off_x + width]
+        )
+    return jnp.stack(cols)
+
+
+def convolve(padded, weights):
+    return jnp.einsum(
+        "toc,tczyx->ozyx", weights, windows(padded), preferred_element_type=jnp.float32
+    )
 
 
 def tap_grads(grad, padded):
-    depth, height, width = grad.shape[1:]
-    terms = []
-    for tap in range(27):
-        off_z, off_y, off_x = (tap // 9, tap // 3 % 3, tap % 3)
-        window = padded[:, off_z : off_z + depth, off_y : off_y + height, off_x : off_x + width]
-        terms.append(jnp.einsum("ozyx,czyx->oc", grad, window, preferred_element_type=jnp.float32))
-    return jnp.stack(terms)
+    return jnp.einsum(
+        "ozyx,tczyx->toc", grad, windows(padded), preferred_element_type=jnp.float32
+    )
 
 
 def flipped(weights):
@@ -238,10 +240,9 @@
     gfirst = gres.astype(single_float) + convolve(framed(gres), flipped(w_res))
     gact = jnp.where(h0 > 0, gfirst, 0.0).astype(brain_float_half)
     grad_in = tap_grads(gact, image_pad)[:, :, 0]
-    summed = tree_sum(
-        (grad_in, grad_res, grad_down, grad_mid, grad_up, head_weight_gradient), ("gz", "xy")
-    )
-    return (err_tiles, summed[0], summed[1], summed[2], summed[3], summed[4], summed[5])
+    early = tree_sum((grad_down, grad_mid, grad_up, head_weight_gradient), ("gz", "xy"))
+    late = tree_sum((grad_in, grad_res), ("gz", "xy"))
+    return (err_tiles, late[0], late[1], early[0], early[1], early[2], early[3])
 
 
 def solution(mesh):

time: 198 us -> 152 us (0.77)
  matrix products: 45.9 us -> 12.8 us
  starting transfers between devices: 56.7 us -> 73.7 us
  waiting for transfers between devices: 35.4 us -> 22.1 us
  blocking collectives: 8.22 us -> 0 us
  local copies, waits for them, and re-layouts: 39.2 us -> 32.2 us
    dot_general x172 -> x8, matrix products: 41.2 us -> 7.21 us  [the longest x3 3.63 us: tap_grads(): jnp.einsum('ozyx,tczyx->toc', grad, windows(padded), preferred_element_ty...]
    all_to_all x1 -> x0, blocking collectives: 8.22 us -> none  [local(): lax.all_to_all(sending, 'xy', split_axis=0, concat_axis=0, tiled=True)]
    ppermute x5 -> x10, waiting for transfers between devices: 14.3 us -> 7.31 us  [tree_sum(): cur = keep + lax.ppermute(send, axes, pairs)]
    ppermute x5 -> x10, waiting for transfers between devices: 11.7 us -> 4.87 us  [tree_sum(): other = lax.ppermute(cur, axes, pairs)]
    all_to_all x0 -> x1, starting transfers between devices: none -> 6.78 us  [local(): lax.all_to_all(sending, 'xy', split_axis=0, concat_axis=0, tiled=True)]
    ppermute x5 -> x10, starting transfers between devices: 7.47 us -> 14.2 us  [tree_sum(): other = lax.ppermute(cur, axes, pairs)]
    ppermute x5 -> x10, starting transfers between devices: 14.5 us -> 20.6 us  [tree_sum(): cur = keep + lax.ppermute(send, axes, pairs)]
    concatenate x4 -> x0, local copies, waits for them, and re-layouts: 4.29 us -> none  [the longest x1 3.55 us: tree_sum(): flat = jnp.concatenate([g.reshape(-1) for g in grads])]
  transfers between devices with their start and end apart: 23 -> 34, of which waited for: 14 -> 13; matrix products, arithmetic and copies ran while one was open for 10% -> 18% of each run, Pallas kernels for 0% -> 0%
where the time goes in v4:
time: 152 us; the launch traced here: 151 us
  starting transfers between devices  73.7 us (48%)
  local copies, waits for them, and re-layouts  32.2 us (21%)
  waiting for transfers between devices  22.1 us (15%)
  matrix products  12.8 us (8%)
  other arithmetic  7.44 us (5%)
  between operations  3.18 us (2%)
    ppermute x10, starting transfers between devices, tree_sum(): cur = keep + lax.ppermute(send, axes, pairs)  20.6 us
    ppermute x6, starting transfers between devices, with_halo(): lax.ppermute(tail, axis, [(i, (i + 1) % count) for i in range(ends)])  19.1 us
    unnamed x212, local copies, waits for them, and re-layouts  15.1 us
    ppermute x10, starting transfers between devices, tree_sum(): other = lax.ppermute(cur, axes, pairs)  14.2 us
    ppermute x6, waiting for transfers between devices, with_halo(): lax.ppermute(head, axis, [((i + 1) % count, i) for i in range(ends)])  9.85 us
    ppermute x6, starting transfers between devices, with_halo(): lax.ppermute(head, axis, [((i + 1) % count, i) for i in range(ends)])  7.92 us
    ppermute x10, waiting for transfers between devices, tree_sum(): cur = keep + lax.ppermute(send, axes, pairs)  7.31 us
    all_to_all x1, starting transfers between devices, local(): lax.all_to_all(sending, 'xy', split_axis=0, concat_axis=0, tiled=True)  6.78 us
  transfers between devices with their start and end apart: 34, of which 13 were waited for; matrix products, arithmetic and copies ran while one was open for 18% of the time, Pallas kernels for 0%

profile of v4, /device:TPU:0, one launch (start us, length us, event | category | flops | bytes accessed | tf_op | source)
XLA Modules:
  0.0 151.4 jit_solution(4762429263020967329)
XLA Ops:
  4.6 5.2 %all-to-all-start = ((bf16[8,2,4,4,2,128]{5,1,4,3,2,0:T(2,128)(2,1)}), bf16[8,2,4,4,2,128]{5,1,4,3,2,0:T(2,128)(2,1)S(1)}, u32[]{:S(2)}, u32[]{:S(2)}) async-start(bf16[8,2,4,4,2,128]{5,1,4,3,2,0:T(2,128)(2,1)} %copy.2326), calls=%async_computation | async-start | bytes 262144 | tf_op jit(solution)/shard_map/all_to_all | solution.py:150
  16.0 3.5 %collective-permute-start = (bf16[1,4,2,256]{3,1,2,0:T(4,128)(2,1)S(1)}, bf16[1,4,2,256]{3,1,2,0:T(4,128)(2,1)S(1)}, u32[]{:S(2)}, u32[]{:S(2)}) collective-permute-start(bf16[1,4,2,256]{3,1,2,0:T(4,128)(2,1)S(1)} %copy.2496), channel_id=1, source_target_pairs={{0,8},{8,16},{16,24},{1,9},{9,17},{17,25},{2,10},{10,18},{18,26},{... | collective-permute-start | bytes 12296 | tf_op jit(solution)/shard_map/ppermute | solution.py:64
  20.9 4.2 %collective-permute-done.1 = bf16[1,4,2,256]{3,1,2,0:T(4,128)(2,1)S(1)} collective-permute-done((bf16[1,4,2,256]{3,1,2,0:T(4,128)(2,1)S(1)}, bf16[1,4,2,256]{3,1,2,0:T(4,128)(2,1)S(1)}, u32[]{:S(2)}, u32[]{:S(2)}) %collective-permute-start.1) | collective-permute-done | bytes 4128 | tf_op jit(solution)/shard_map/ppermute | solution.py:66
  27.8 4.0 %collective-permute-done.3 = bf16[1,12,2,4]{3,1,2,0:T(8,128)(2,1)S(1)} collective-permute-done((bf16[1,12,2,4]{3,1,2,0:T(8,128)(2,1)S(1)}, bf16[1,12,2,4]{3,1,2,0:T(8,128)(2,1)S(1)}, u32[]{:S(2)}, u32[]{:S(2)}) %collective-permute-start.3) | collective-permute-done | bytes 224 | tf_op jit(solution)/shard_map/ppermute | solution.py:66
  47.3 3.5 %collective-permute-start.4 = (bf16[64,1,1,128]{3,0,1,2:T(8,128)(2,1)S(1)}, bf16[64,1,1,128]{3,0,1,2:T(8,128)(2,1)S(1)}, u32[]{:S(2)}, u32[]{:S(2)}) collective-permute-start(bf16[64,1,1,128]{3,0,1,2:T(8,128)(2,1)S(1)} %get-tuple-element.257), channel_id=1, source_target_pairs={{0,8},{8,16},{16,24},{1,9},{9,17},{17,25},{2,10},{10,18},{18,26},{... | collective-permute-start | bytes 49160 | tf_op jit(solution)/shard_map/ppermute | solution.py:64
  57.0 4.0 %collective-permute-start.6 = (bf16[64,4,1,1]{3,0,1,2:T(8,128)(2,1)S(1)}, bf16[64,4,1,1]{3,0,1,2:T(8,128)(2,1)S(1)}, u32[]{:S(2)}, u32[]{:S(2)}) collective-permute-start(bf16[64,4,1,1]{3,0,1,2:T(8,128)(2,1)S(1)} %get-tuple-element.254), channel_id=1, source_target_pairs={{0,1},{1,2},{2,3},{3,4},{4,5},{5,6},{6,7},{8,9},{9,10},{10,11},{11... | collective-permute-start | bytes 1544 | tf_op jit(solution)/shard_map/ppermute | solution.py:64
  67.5 4.4 %collective-permute-start.8 = (bf16[32,1,2,256]{3,0,2,1:T(8,128)(2,1)S(1)}, bf16[32,1,2,256]{3,0,2,1:T(8,128)(2,1)S(1)}, u32[]{:S(2)}, u32[]{:S(2)}) collective-permute-start(bf16[32,1,2,256]{3,0,2,1:T(8,128)(2,1)S(1)} %get-tuple-element.251), channel_id=1, source_target_pairs={{0,8},{8,16},{16,24},{1,9},{9,17},{17,25},{2,10},{10,18},{18,26},{... | collective-permute-start | bytes 98312 | tf_op jit(solution)/shard_map/ppermute | solution.py:64
  77.3 6.8 %all-to-all-start.1 = ((bf16[8,2,3,4,2,128]{5,1,4,3,2,0:T(2,128)(2,1)}), bf16[8,2,3,4,2,128]{5,1,4,3,2,0:T(2,128)(2,1)S(1)}, u32[]{:S(2)}, u32[]{:S(2)}) async-start(bf16[8,2,3,4,2,128]{5,1,4,3,2,0:T(2,128)(2,1)} %broadcast_in_dim.32), calls=%async_computation.1 | async-start | bytes 196608 | tf_op jit(solution)/shard_map/all_to_all | solution.py:208
  84.2 2.4 %collective-permute-start.10 = (bf16[32,6,2,1]{3,0,2,1:T(8,128)(2,1)S(1)}, bf16[32,6,2,1]{3,0,2,1:T(8,128)(2,1)S(1)}, u32[]{:S(2)}, u32[]{:S(2)}) collective-permute-start(bf16[32,6,2,1]{3,0,2,1:T(8,128)(2,1)S(1)} %get-tuple-element.249), channel_id=1, source_target_pairs={{0,1},{1,2},{2,3},{3,4},{4,5},{5,6},{6,7},{8,9},{9,10},{10,11},{11... | collective-permute-start | bytes 2312 | tf_op jit(solution)/shard_map/ppermute | solution.py:64
  87.9 3.0 %convolution_bitcast_fusion.1 = f32[27,32,32]{1,2,0:T(8,128)S(1)} fusion(bf16[27,32,4,2,256]{4,1,3,0,2:T(8,128)(2,1)} %copy-done.14, bf16[32,4,2,256]{3,0,2,1:T(8,128)(2,1)S(1)} %select_convert_fusion), kind=kOutput, calls=%fused_computation.48 | convolution fusion | flops 113246208 | bytes 3780608 | tf_op jit(solution)/shard_map/ozyx,tczyx->toc/dot_general | solution.py:98
  94.9 2.9 %collective-permute-start.12 = (f32[14256]{0:T(1024)S(1)}, f32[14256]{0:T(1024)S(1)}, u32[]{:S(2)}, u32[]{:S(2)}) collective-permute-start(f32[14256]{0:T(1024)S(1)} %slice_select_fusion.2), channel_id=1, source_target_pairs={{0,1},{1,0},{2,3},{3,2},{4,5},{5,4},{6,7},{7,6},{8,9},{9,8},{10,11... | collective-permute-start | bytes 171080 | tf_op jit(solution)/shard_map/ppermute | solution.py:31
  98.9 2.4 %collective-permute-start.13 = (f32[7128]{0:T(1024)S(1)}, f32[7128]{0:T(1024)S(1)}, u32[]{:S(2)}, u32[]{:S(2)}) collective-permute-start(f32[7128]{0:T(1024)S(1)} %slice_select_fusion.4), channel_id=1, source_target_pairs={{0,2},{1,3},{2,0},{3,1},{4,6},{5,7},{6,4},{7,5},{8,10},{9,11},{10,... | collective-permute-start | bytes 85544 | tf_op jit(solution)/shard_map/ppermute | solution.py:31
  107.4 2.1 %collective-permute-start.23 = (f32[35864]{0:T(1024)S(1)}, f32[35864]{0:T(1024)S(1)}, u32[]{:S(2)}, u32[]{:S(2)}) collective-permute-start(f32[35864]{0:T(1024)S(1)} %slice_select_fusion), channel_id=1, source_target_pairs={{0,2},{1,3},{2,0},{3,1},{4,6},{5,7},{6,4},{7,5},{8,10},{9,11},{10,... | collective-permute-start | bytes 430376 | tf_op jit(solution)/shard_map/ppermute | solution.py:31
  109.6 2.4 %collective-permute-start.15 = (f32[1782]{0:T(1024)S(1)}, f32[1782]{0:T(1024)S(1)}, u32[]{:S(2)}, u32[]{:S(2)}) collective-permute-start(f32[1782]{0:T(1024)S(1)} %slice_select_fusion.7), channel_id=1, source_target_pairs={{0,8},{1,9},{2,10},{3,11},{4,12},{5,13},{6,14},{7,15},{8,0},{9,1},... | collective-permute-start | bytes 21392 | tf_op jit(solution)/shard_map/ppermute | solution.py:31
  112.8 2.0 %collective-permute-start.24 = (f32[17932]{0:T(1024)S(1)}, f32[17932]{0:T(1024)S(1)}, u32[]{:S(2)}, u32[]{:S(2)}) collective-permute-start(f32[17932]{0:T(1024)S(1)} %slice_select_fusion.1), channel_id=1, source_target_pairs={{0,4},{1,5},{2,6},{3,7},{4,0},{5,1},{6,2},{7,3},{8,12},{9,13},{10,... | collective-permute-start | bytes 215192 | tf_op jit(solution)/shard_map/ppermute | solution.py:31
  114.9 2.3 %collective-permute-done.24 = f32[17932]{0:T(1024)S(1)} collective-permute-done((f32[17932]{0:T(1024)S(1)}, f32[17932]{0:T(1024)S(1)}, u32[]{:S(2)}, u32[]{:S(2)}) %collective-permute-start.24) | collective-permute-done | bytes 71760 | tf_op jit(solution)/shard_map/ppermute | solution.py:31
  117.4 2.4 %collective-permute-start.25 = (f32[8966]{0:T(1024)S(1)}, f32[8966]{0:T(1024)S(1)}, u32[]{:S(2)}, u32[]{:S(2)}) collective-permute-start(f32[8966]{0:T(1024)S(1)} %slice_select_fusion.3), channel_id=1, source_target_pairs={{0,8},{1,9},{2,10},{3,11},{4,12},{5,13},{6,14},{7,15},{8,0},{9,1},... | collective-permute-start | bytes 107600 | tf_op jit(solution)/shard_map/ppermute | solution.py:31
  121.9 3.1 %collective-permute-start.26 = (f32[4483]{0:T(1024)S(1)}, f32[4483]{0:T(1024)S(1)}, u32[]{:S(2)}, u32[]{:S(2)}) collective-permute-start(f32[4483]{0:T(1024)S(1)} %slice_select_fusion.5), channel_id=1, source_target_pairs={{0,16},{1,17},{2,18},{3,19},{4,20},{5,21},{6,22},{7,23},{8,24},{9,... | collective-permute-start | bytes 53804 | tf_op jit(solution)/shard_map/ppermute | solution.py:31
  126.8 2.9 %collective-permute-start.27 = (f32[4483]{0:T(1024)S(1)}, f32[4483]{0:T(1024)S(1)}, u32[]{:S(2)}, u32[]{:S(2)}) collective-permute-start(f32[4483]{0:T(1024)S(1)} %select_add_fusion.6), channel_id=1, source_target_pairs={{0,16},{1,17},{2,18},{3,19},{4,20},{5,21},{6,22},{7,23},{8,24},{9,... | collective-permute-start | bytes 53804 | tf_op jit(solution)/shard_map/ppermute | solution.py:36
  131.6 2.0 %collective-permute-start.28 = (f32[8966]{0:T(1024)S(1)}, f32[8966]{0:T(1024)S(1)}, u32[]{:S(2)}, u32[]{:S(2)}) collective-permute-start(f32[8966]{0:T(1024)S(1)} %maximum_select_fusion.6), channel_id=1, source_target_pairs={{0,8},{1,9},{2,10},{3,11},{4,12},{5,13},{6,14},{7,15},{8,0},{9,1},... | collective-permute-start | bytes 107600 | tf_op jit(solution)/shard_map/ppermute | solution.py:36
  133.6 2.0 %collective-permute-start.19 = (f32[3564]{0:T(1024)S(1)}, f32[3564]{0:T(1024)S(1)}, u32[]{:S(2)}, u32[]{:S(2)}) collective-permute-start(f32[3564]{0:T(1024)S(1)} %maximum_select_fusion.8), channel_id=1, source_target_pairs={{0,4},{1,5},{2,6},{3,7},{4,0},{5,1},{6,2},{7,3},{8,12},{9,13},{10,... | collective-permute-start | bytes 42776 | tf_op jit(solution)/shard_map/ppermute | solution.py:36
  135.7 2.1 %collective-permute-start.29 = (f32[17932]{0:T(1024)S(1)}, f32[17932]{0:T(1024)S(1)}, u32[]{:S(2)}, u32[]{:S(2)}) collective-permute-start(f32[17932]{0:T(1024)S(1)} %maximum_select_fusion.4), channel_id=1, source_target_pairs={{0,4},{1,5},{2,6},{3,7},{4,0},{5,1},{6,2},{7,3},{8,12},{9,13},{10,... | collective-permute-start | bytes 215192 | tf_op jit(solution)/shard_map/ppermute | solution.py:36
  140.3 2.3 %collective-permute-start.30 = (f32[35864]{0:T(1024)S(1)}, f32[35864]{0:T(1024)S(1)}, u32[]{:S(2)}, u32[]{:S(2)}) collective-permute-start(f32[35864]{0:T(1024)S(1)} %maximum_select_fusion.2), channel_id=1, source_target_pairs={{0,2},{1,3},{2,0},{3,1},{4,6},{5,7},{6,4},{7,5},{8,10},{9,11},{10,... | collective-permute-start | bytes 430376 | tf_op jit(solution)/shard_map/ppermute | solution.py:36
  142.7 3.0 %collective-permute-done.30 = f32[35864]{0:T(1024)S(1)} collective-permute-done((f32[35864]{0:T(1024)S(1)}, f32[35864]{0:T(1024)S(1)}, u32[]{:S(2)}, u32[]{:S(2)}) %collective-permute-start.30) | collective-permute-done | bytes 143488 | tf_op jit(solution)/shard_map/ppermute | solution.py:36
  (396 shorter events, 73.6 us)
Async XLA Ops:
  4.6 11.3 %all-to-all-start = ((bf16[8,2,4,4,2,128]{5,1,4,3,2,0:T(2,128)(2,1)}), bf16[8,2,4,4,2,128]{5,1,4,3,2,0:T(2,128)(2,1)S(1)}, u32[]{:S(2)}, u32[]{:S(2)}) async-start(bf16[8,2,4,4,2,128]{5,1,4,3,2,0:T(2,128)(2,1)} %copy.2326), calls=%async_computation | async-start | bytes 262144 | tf_op jit(solution)/shard_map/all_to_all | solution.py:150
  16.0 4.8 %collective-permute-start = (bf16[1,4,2,256]{3,1,2,0:T(4,128)(2,1)S(1)}, bf16[1,4,2,256]{3,1,2,0:T(4,128)(2,1)S(1)}, u32[]{:S(2)}, u32[]{:S(2)}) collective-permute-start(bf16[1,4,2,256]{3,1,2,0:T(4,128)(2,1)S(1)} %copy.2496), channel_id=1, source_target_pairs={{0,8},{8,16},{16,24},{1,9},{9,17},{17,25},{2,10},{10,18},{18,26},{... | collective-permute-start | bytes 12296 | tf_op jit(solution)/shard_map/ppermute | solution.py:64
  19.5 5.5 %collective-permute-start.1 = (bf16[1,4,2,256]{3,1,2,0:T(4,128)(2,1)S(1)}, bf16[1,4,2,256]{3,1,2,0:T(4,128)(2,1)S(1)}, u32[]{:S(2)}, u32[]{:S(2)}) collective-permute-start(bf16[1,4,2,256]{3,1,2,0:T(4,128)(2,1)S(1)} %copy.2496), channel_id=1, source_target_pairs={{8,0},{16,8},{24,16},{9,1},{17,9},{25,17},{10,2},{18,10},{26,18},{... | collective-permute-start | bytes 12296 | tf_op jit(solution)/shard_map/ppermute | solution.py:66
  26.4 5.3 %collective-permute-start.3 = (bf16[1,12,2,4]{3,1,2,0:T(8,128)(2,1)S(1)}, bf16[1,12,2,4]{3,1,2,0:T(8,128)(2,1)S(1)}, u32[]{:S(2)}, u32[]{:S(2)}) collective-permute-start(bf16[1,12,2,4]{3,1,2,0:T(8,128)(2,1)S(1)} %get-tuple-element.287), channel_id=1, source_target_pairs={{1,0},{2,1},{3,2},{4,3},{5,4},{6,5},{7,6},{9,8},{10,9},{11,10},{12... | collective-permute-start | bytes 584 | tf_op jit(solution)/shard_map/ppermute | solution.py:66
  47.3 9.5 %collective-permute-start.4 = (bf16[64,1,1,128]{3,0,1,2:T(8,128)(2,1)S(1)}, bf16[64,1,1,128]{3,0,1,2:T(8,128)(2,1)S(1)}, u32[]{:S(2)}, u32[]{:S(2)}) collective-permute-start(bf16[64,1,1,128]{3,0,1,2:T(8,128)(2,1)S(1)} %get-tuple-element.257), channel_id=1, source_target_pairs={{0,8},{8,16},{16,24},{1,9},{9,17},{17,25},{2,10},{10,18},{18,26},{... | collective-permute-start | bytes 49160 | tf_op jit(solution)/shard_map/ppermute | solution.py:64
  50.9 6.0 %collective-permute-start.5 = (bf16[64,1,1,128]{3,0,1,2:T(8,128)(2,1)S(1)}, bf16[64,1,1,128]{3,0,1,2:T(8,128)(2,1)S(1)}, u32[]{:S(2)}, u32[]{:S(2)}) collective-permute-start(bf16[64,1,1,128]{3,0,1,2:T(8,128)(2,1)S(1)} %get-tuple-element.258), channel_id=1, source_target_pairs={{8,0},{16,8},{24,16},{9,1},{17,9},{25,17},{10,2},{18,10},{26,18},{... | collective-permute-start | bytes 49160 | tf_op jit(solution)/shard_map/ppermute | solution.py:66
  57.0 5.4 %collective-permute-start.6 = (bf16[64,4,1,1]{3,0,1,2:T(8,128)(2,1)S(1)}, bf16[64,4,1,1]{3,0,1,2:T(8,128)(2,1)S(1)}, u32[]{:S(2)}, u32[]{:S(2)}) collective-permute-start(bf16[64,4,1,1]{3,0,1,2:T(8,128)(2,1)S(1)} %get-tuple-element.254), channel_id=1, source_target_pairs={{0,1},{1,2},{2,3},{3,4},{4,5},{5,6},{6,7},{8,9},{9,10},{10,11},{11... | collective-permute-start | bytes 1544 | tf_op jit(solution)/shard_map/ppermute | solution.py:64
  67.5 16.6 %collective-permute-start.8 = (bf16[32,1,2,256]{3,0,2,1:T(8,128)(2,1)S(1)}, bf16[32,1,2,256]{3,0,2,1:T(8,128)(2,1)S(1)}, u32[]{:S(2)}, u32[]{:S(2)}) collective-permute-start(bf16[32,1,2,256]{3,0,2,1:T(8,128)(2,1)S(1)} %get-tuple-element.251), channel_id=1, source_target_pairs={{0,8},{8,16},{16,24},{1,9},{9,17},{17,25},{2,10},{10,18},{18,26},{... | collective-permute-start | bytes 98312 | tf_op jit(solution)/shard_map/ppermute | solution.py:64
  71.9 12.2 %collective-permute-start.9 = (bf16[32,1,2,256]{3,0,2,1:T(8,128)(2,1)S(1)}, bf16[32,1,2,256]{3,0,2,1:T(8,128)(2,1)S(1)}, u32[]{:S(2)}, u32[]{:S(2)}) collective-permute-start(bf16[32,1,2,256]{3,0,2,1:T(8,128)(2,1)S(1)} %get-tuple-element.252), channel_id=1, source_target_pairs={{8,0},{16,8},{24,16},{9,1},{17,9},{25,17},{10,2},{18,10},{26,18},{... | collective-permute-start | bytes 98312 | tf_op jit(solution)/shard_map/ppermute | solution.py:66
  77.3 24.3 %all-to-all-start.1 = ((bf16[8,2,3,4,2,128]{5,1,4,3,2,0:T(2,128)(2,1)}), bf16[8,2,3,4,2,128]{5,1,4,3,2,0:T(2,128)(2,1)S(1)}, u32[]{:S(2)}, u32[]{:S(2)}) async-start(bf16[8,2,3,4,2,128]{5,1,4,3,2,0:T(2,128)(2,1)} %broadcast_in_dim.32), calls=%async_computation.1 | async-start | bytes 196608 | tf_op jit(solution)/shard_map/all_to_all | solution.py:208
  84.2 7.1 %collective-permute-start.10 = (bf16[32,6,2,1]{3,0,2,1:T(8,128)(2,1)S(1)}, bf16[32,6,2,1]{3,0,2,1:T(8,128)(2,1)S(1)}, u32[]{:S(2)}, u32[]{:S(2)}) collective-permute-start(bf16[32,6,2,1]{3,0,2,1:T(8,128)(2,1)S(1)} %get-tuple-element.249), channel_id=1, source_target_pairs={{0,1},{1,2},{2,3},{3,4},{4,5},{5,6},{6,7},{8,9},{9,10},{10,11},{11... | collective-permute-start | bytes 2312 | tf_op jit(solution)/shard_map/ppermute | solution.py:64
  86.6 4.7 %collective-permute-start.11 = (bf16[32,6,2,1]{3,0,2,1:T(8,128)(2,1)S(1)}, bf16[32,6,2,1]{3,0,2,1:T(8,128)(2,1)S(1)}, u32[]{:S(2)}, u32[]{:S(2)}) collective-permute-start(bf16[32,6,2,1]{3,0,2,1:T(8,128)(2,1)S(1)} %get-tuple-element.250), channel_id=1, source_target_pairs={{1,0},{2,1},{3,2},{4,3},{5,4},{6,5},{7,6},{9,8},{10,9},{11,10},{12... | collective-permute-start | bytes 2312 | tf_op jit(solution)/shard_map/ppermute | solution.py:66
  101.4 5.7 %collective-permute-start.22 = (f32[71728]{0:T(1024)S(1)}, f32[71728]{0:T(1024)S(1)}, u32[]{:S(2)}, u32[]{:S(2)}) collective-permute-start(f32[71728]{0:T(1024)S(1)} %broadcast_select_fusion), channel_id=1, source_target_pairs={{0,1},{1,0},{2,3},{3,2},{4,5},{5,4},{6,7},{7,6},{8,9},{9,8},{10,11... | collective-permute-start | bytes 860744 | tf_op jit(solution)/shard_map/ppermute | solution.py:31
  107.4 5.2 %collective-permute-start.23 = (f32[35864]{0:T(1024)S(1)}, f32[35864]{0:T(1024)S(1)}, u32[]{:S(2)}, u32[]{:S(2)}) collective-permute-start(f32[35864]{0:T(1024)S(1)} %slice_select_fusion), channel_id=1, source_target_pairs={{0,2},{1,3},{2,0},{3,1},{4,6},{5,7},{6,4},{7,5},{8,10},{9,11},{10,... | collective-permute-start | bytes 430376 | tf_op jit(solution)/shard_map/ppermute | solution.py:31
  109.6 5.3 %collective-permute-start.15 = (f32[1782]{0:T(1024)S(1)}, f32[1782]{0:T(1024)S(1)}, u32[]{:S(2)}, u32[]{:S(2)}) collective-permute-start(f32[1782]{0:T(1024)S(1)} %slice_select_fusion.7), channel_id=1, source_target_pairs={{0,8},{1,9},{2,10},{3,11},{4,12},{5,13},{6,14},{7,15},{8,0},{9,1},... | collective-permute-start | bytes 21392 | tf_op jit(solution)/shard_map/ppermute | solution.py:31
  112.8 4.4 %collective-permute-start.24 = (f32[17932]{0:T(1024)S(1)}, f32[17932]{0:T(1024)S(1)}, u32[]{:S(2)}, u32[]{:S(2)}) collective-permute-start(f32[17932]{0:T(1024)S(1)} %slice_select_fusion.1), channel_id=1, source_target_pairs={{0,4},{1,5},{2,6},{3,7},{4,0},{5,1},{6,2},{7,3},{8,12},{9,13},{10,... | collective-permute-start | bytes 215192 | tf_op jit(solution)/shard_map/ppermute | solution.py:31
  117.4 4.4 %collective-permute-start.25 = (f32[8966]{0:T(1024)S(1)}, f32[8966]{0:T(1024)S(1)}, u32[]{:S(2)}, u32[]{:S(2)}) collective-permute-start(f32[8966]{0:T(1024)S(1)} %slice_select_fusion.3), channel_id=1, source_target_pairs={{0,8},{1,9},{2,10},{3,11},{4,12},{5,13},{6,14},{7,15},{8,0},{9,1},... | collective-permute-start | bytes 107600 | tf_op jit(solution)/shard_map/ppermute | solution.py:31
  119.9 5.1 %collective-permute-start.16 = (f32[891]{0:T(1024)S(1)}, f32[891]{0:T(1024)S(1)}, u32[]{:S(2)}, u32[]{:S(2)}) collective-permute-start(f32[891]{0:T(1024)S(1)} %slice_select_fusion.8), channel_id=1, source_target_pairs={{0,16},{1,17},{2,18},{3,19},{4,20},{5,21},{6,22},{7,23},{8,24},{9,... | collective-permute-start | bytes 10700 | tf_op jit(solution)/shard_map/ppermute | solution.py:31
  121.9 4.8 %collective-permute-start.26 = (f32[4483]{0:T(1024)S(1)}, f32[4483]{0:T(1024)S(1)}, u32[]{:S(2)}, u32[]{:S(2)}) collective-permute-start(f32[4483]{0:T(1024)S(1)} %slice_select_fusion.5), channel_id=1, source_target_pairs={{0,16},{1,17},{2,18},{3,19},{4,20},{5,21},{6,22},{7,23},{8,24},{9,... | collective-permute-start | bytes 53804 | tf_op jit(solution)/shard_map/ppermute | solution.py:31
  125.1 4.7 %collective-permute-start.17 = (f32[891]{0:T(1024)S(1)}, f32[891]{0:T(1024)S(1)}, u32[]{:S(2)}, u32[]{:S(2)}) collective-permute-start(f32[891]{0:T(1024)S(1)} %select_add_fusion.9), channel_id=1, source_target_pairs={{0,16},{1,17},{2,18},{3,19},{4,20},{5,21},{6,22},{7,23},{8,24},{9,... | collective-permute-start | bytes 10700 | tf_op jit(solution)/shard_map/ppermute | solution.py:36
  126.8 4.7 %collective-permute-start.27 = (f32[4483]{0:T(1024)S(1)}, f32[4483]{0:T(1024)S(1)}, u32[]{:S(2)}, u32[]{:S(2)}) collective-permute-start(f32[4483]{0:T(1024)S(1)} %select_add_fusion.6), channel_id=1, source_target_pairs={{0,16},{1,17},{2,18},{3,19},{4,20},{5,21},{6,22},{7,23},{8,24},{9,... | collective-permute-start | bytes 53804 | tf_op jit(solution)/shard_map/ppermute | solution.py:36
  135.7 4.4 %collective-permute-start.29 = (f32[17932]{0:T(1024)S(1)}, f32[17932]{0:T(1024)S(1)}, u32[]{:S(2)}, u32[]{:S(2)}) collective-permute-start(f32[17932]{0:T(1024)S(1)} %maximum_select_fusion.4), channel_id=1, source_target_pairs={{0,4},{1,5},{2,6},{3,7},{4,0},{5,1},{6,2},{7,3},{8,12},{9,13},{10,... | collective-permute-start | bytes 215192 | tf_op jit(solution)/shard_map/ppermute | solution.py:36
  137.9 4.7 %collective-permute-start.20 = (f32[7128]{0:T(1024)S(1)}, f32[7128]{0:T(1024)S(1)}, u32[]{:S(2)}, u32[]{:S(2)}) collective-permute-start(f32[7128]{0:T(1024)S(1)} %maximum_select_fusion.7), channel_id=1, source_target_pairs={{0,2},{1,3},{2,0},{3,1},{4,6},{5,7},{6,4},{7,5},{8,10},{9,11},{10,... | collective-permute-start | bytes 85544 | tf_op jit(solution)/shard_map/ppermute | solution.py:36
  140.3 5.4 %collective-permute-start.30 = (f32[35864]{0:T(1024)S(1)}, f32[35864]{0:T(1024)S(1)}, u32[]{:S(2)}, u32[]{:S(2)}) collective-permute-start(f32[35864]{0:T(1024)S(1)} %maximum_select_fusion.2), channel_id=1, source_target_pairs={{0,2},{1,3},{2,0},{3,1},{4,6},{5,7},{6,4},{7,5},{8,10},{9,11},{10,... | collective-permute-start | bytes 430376 | tf_op jit(solution)/shard_map/ppermute | solution.py:36
  (32 other events, 224.6 us)

commit v5 on v4

--- a/solution.py
+++ b/solution.py
@@ -146,9 +146,19 @@
     )
     payload = jnp.concatenate([tile_image[0, 0][:, None], tile_target[0, 0]], axis=1)
     outgoing = jnp.einsum("ps,sazyx->pazyx", select, payload, preferred_element_type=single_float)
-    outgoing = outgoing.astype(brain_float_half).reshape((ranks, per_dev) + payload.shape[1:])
+    outgoing = outgoing.astype(brain_float_half).reshape((ranks, per_dev * payload.shape[1]) + payload.shape[2:])
+    first_pos = jnp.arange(ranks) * per_dev
+    beside = jnp.stack([first_pos - 1, first_pos + per_dev], axis=1)
+    near = ((slot_list[None, None, :] == beside[:, :, None]) & live[None, None, :]).astype(
+        brain_float_half
+    )
+    flank = jnp.einsum("dks,szyx->dkzyx", near, tile_image[0, 0], preferred_element_type=single_float)
+    outgoing = jnp.concatenate([outgoing, flank.astype(brain_float_half)], axis=1)
     incoming = lax.all_to_all(outgoing, "xy", 0, 0, tiled=True)
     mine = jnp.sum(incoming.astype(single_float), axis=0).astype(brain_float_half)
+    flank_left = mine[per_dev * payload.shape[1]][None, :, :, width - 4 :]
+    flank_right = mine[per_dev * payload.shape[1] + 1][None, :, :, :4]
+    mine = mine[: per_dev * payload.shape[1]].reshape((per_dev,) + payload.shape[1:])
     mine_img = mine[:, 0]
     mine_tgt = mine[:, 1:]
     image = mine_img.transpose(1, 2, 0, 3).reshape(1, depth, height, per_dev * width)
@@ -156,7 +166,8 @@
     voxel_cells = depth * height * per_dev * width * ranks * layers
     block_z = lax.axis_index("gz") * depth
     block_x = column * per_dev * width
-    image_wide = with_halo(image, (("gz", 1), ("xy", 3)), 4)
+    image_wide = jnp.concatenate([flank_left, image, flank_right], axis=3)
+    image_wide = with_halo(image_wide, (("gz", 1),), 4)
     image_wide = jnp.pad(image_wide, ((0, 0), (0, 0), (1, 1), (0, 0)))
     image_pad = image_wide[:, 3:-3, :, 3:-3]
     h0_wide = jax.nn.relu(convolve(image_wide, w_in[:, :, None]))

time: 152 us -> 148 us (0.974)
  starting transfers between devices: 73.7 us -> 67.7 us
  matrix products: 12.8 us -> 15.3 us
  waiting for transfers between devices: 22.1 us -> 20.3 us
    ppermute x6 -> x5, starting transfers between devices: 19.1 us -> 15.2 us  [with_halo(): lax.ppermute(tail, axis, [(i, (i + 1) % count) for i in range(ends)])]
    ppermute x6 -> x5, waiting for transfers between devices: 9.85 us -> 7.78 us  [with_halo(): lax.ppermute(head, axis, [((i + 1) % count, i) for i in range(ends)])]
    ppermute x6 -> x5, starting transfers between devices: 7.92 us -> 6.63 us  [with_halo(): lax.ppermute(head, axis, [((i + 1) % count, i) for i in range(ends)])]
    unnamed x212 -> x222, local copies, waits for them, and re-layouts: 15.1 us -> 16.2 us
  transfers between devices with their start and end apart: 34 -> 32, of which waited for: 13 -> 13; matrix products, arithmetic and copies ran while one was open for 18% -> 18% of each run, Pallas kernels for 0% -> 0%
where the time goes in v5:
time: 148 us; the launch traced here: 147 us
  starting transfers between devices  67.7 us (46%)
  local copies, waits for them, and re-layouts  33.5 us (23%)
  waiting for transfers between devices  20.3 us (14%)
  matrix products  15.3 us (10%)
  other arithmetic  6.64 us (4%)
  between operations  3.28 us (2%)
    ppermute x10, starting transfers between devices, tree_sum(): cur = keep + lax.ppermute(send, axes, pairs)  20.6 us
    unnamed x222, local copies, waits for them, and re-layouts  16.2 us
    ppermute x5, starting transfers between devices, with_halo(): lax.ppermute(tail, axis, [(i, (i + 1) % count) for i in range(ends)])  15.2 us
    ppermute x10, starting transfers between devices, tree_sum(): other = lax.ppermute(cur, axes, pairs)  14.2 us
    ppermute x5, waiting for transfers between devices, with_halo(): lax.ppermute(head, axis, [((i + 1) % count, i) for i in range(ends)])  7.78 us
    ppermute x10, waiting for transfers between devices, tree_sum(): cur = keep + lax.ppermute(send, axes, pairs)  7.31 us
    ppermute x5, starting transfers between devices, with_halo(): lax.ppermute(head, axis, [((i + 1) % count, i) for i in range(ends)])  6.63 us
    all_to_all x1, starting transfers between devices, local(): lax.all_to_all(sending, 'xy', split_axis=0, concat_axis=0, tiled=True)  5.91 us
  transfers between devices with their start and end apart: 32, of which 13 were waited for; matrix products, arithmetic and copies ran while one was open for 18% of the time, Pallas kernels for 0%

profile of v5, /device:TPU:0, one launch (start us, length us, event | category | flops | bytes accessed | tf_op | source)
XLA Modules:
  0.0 146.7 jit_solution(17597567676018567730)
XLA Ops:
  5.8 5.2 %all-to-all-start = ((bf16[8,10,4,2,128]{4,2,3,1,0:T(4,128)(2,1)}), bf16[8,10,4,2,128]{4,2,3,1,0:T(4,128)(2,1)S(1)}, u32[]{:S(2)}, u32[]{:S(2)}) async-start(bf16[8,10,4,2,128]{4,2,3,1,0:T(4,128)(2,1)} %copy.2729), calls=%async_computation | async-start | bytes 327680 | tf_op jit(solution)/shard_map/all_to_all | solution.py:157
  17.2 3.5 %collective-permute-start = (bf16[1,4,2,264]{3,1,2,0:T(4,128)(2,1)S(1)}, bf16[1,4,2,264]{3,1,2,0:T(4,128)(2,1)S(1)}, u32[]{:S(2)}, u32[]{:S(2)}) collective-permute-start(bf16[1,4,2,264]{3,1,2,0:T(4,128)(2,1)S(1)} %pad_maximum_fusion.20), channel_id=1, source_target_pairs={{0,8},{8,16},{16,24},{1,9},{9,17},{17,25},{2,10},{10,18},{18,26},{... | collective-permute-start | bytes 12680 | tf_op jit(solution)/shard_map/ppermute | solution.py:64
  22.1 4.1 %collective-permute-done.1 = bf16[1,4,2,264]{3,1,2,0:T(4,128)(2,1)S(1)} collective-permute-done((bf16[1,4,2,264]{3,1,2,0:T(4,128)(2,1)S(1)}, bf16[1,4,2,264]{3,1,2,0:T(4,128)(2,1)S(1)}, u32[]{:S(2)}, u32[]{:S(2)}) %collective-permute-start.1) | collective-permute-done | bytes 4256 | tf_op jit(solution)/shard_map/ppermute | solution.py:66
  43.9 3.5 %collective-permute-start.2 = (bf16[64,1,1,128]{3,0,1,2:T(8,128)(2,1)S(1)}, bf16[64,1,1,128]{3,0,1,2:T(8,128)(2,1)S(1)}, u32[]{:S(2)}, u32[]{:S(2)}) collective-permute-start(bf16[64,1,1,128]{3,0,1,2:T(8,128)(2,1)S(1)} %get-tuple-element.264), channel_id=1, source_target_pairs={{0,8},{8,16},{16,24},{1,9},{9,17},{17,25},{2,10},{10,18},{18,26},{... | collective-permute-start | bytes 49160 | tf_op jit(solution)/shard_map/ppermute | solution.py:64
  56.5 3.7 %collective-permute-done.5 = bf16[64,4,1,1]{3,0,1,2:T(8,128)(2,1)S(1)} collective-permute-done((bf16[64,4,1,1]{3,0,1,2:T(8,128)(2,1)S(1)}, bf16[64,4,1,1]{3,0,1,2:T(8,128)(2,1)S(1)}, u32[]{:S(2)}, u32[]{:S(2)}) %collective-permute-start.5) | collective-permute-done | bytes 544 | tf_op jit(solution)/shard_map/ppermute | solution.py:66
  63.5 4.5 %collective-permute-start.6 = (bf16[32,1,2,256]{3,0,2,1:T(8,128)(2,1)S(1)}, bf16[32,1,2,256]{3,0,2,1:T(8,128)(2,1)S(1)}, u32[]{:S(2)}, u32[]{:S(2)}) collective-permute-start(bf16[32,1,2,256]{3,0,2,1:T(8,128)(2,1)S(1)} %get-tuple-element.258), channel_id=1, source_target_pairs={{0,8},{8,16},{16,24},{1,9},{9,17},{17,25},{2,10},{10,18},{18,26},{... | collective-permute-start | bytes 98312 | tf_op jit(solution)/shard_map/ppermute | solution.py:64
  73.4 5.9 %all-to-all-start.1 = ((bf16[8,2,3,4,2,128]{5,1,4,3,2,0:T(2,128)(2,1)}), bf16[8,2,3,4,2,128]{5,1,4,3,2,0:T(2,128)(2,1)S(1)}, u32[]{:S(2)}, u32[]{:S(2)}) async-start(bf16[8,2,3,4,2,128]{5,1,4,3,2,0:T(2,128)(2,1)} %broadcast_in_dim.57), calls=%async_computation.1 | async-start | bytes 196608 | tf_op jit(solution)/shard_map/all_to_all | solution.py:219
  79.5 2.4 %collective-permute-start.8 = (bf16[32,6,2,1]{3,0,2,1:T(8,128)(2,1)S(1)}, bf16[32,6,2,1]{3,0,2,1:T(8,128)(2,1)S(1)}, u32[]{:S(2)}, u32[]{:S(2)}) collective-permute-start(bf16[32,6,2,1]{3,0,2,1:T(8,128)(2,1)S(1)} %get-tuple-element.256), channel_id=1, source_target_pairs={{0,1},{1,2},{2,3},{3,4},{4,5},{5,6},{6,7},{8,9},{9,10},{10,11},{11... | collective-permute-start | bytes 2312 | tf_op jit(solution)/shard_map/ppermute | solution.py:64
  83.2 3.0 %convolution_bitcast_fusion.1 = f32[27,32,32]{1,2,0:T(8,128)S(1)} fusion(bf16[27,32,4,2,256]{4,1,3,0,2:T(8,128)(2,1)} %copy-done.17, bf16[32,4,2,256]{3,0,2,1:T(8,128)(2,1)S(1)} %select_convert_fusion), kind=kOutput, calls=%fused_computation.48 | convolution fusion | flops 113246208 | bytes 3780608 | tf_op jit(solution)/shard_map/ozyx,tczyx->toc/dot_general | solution.py:98
  90.2 2.9 %collective-permute-start.10 = (f32[14256]{0:T(1024)S(1)}, f32[14256]{0:T(1024)S(1)}, u32[]{:S(2)}, u32[]{:S(2)}) collective-permute-start(f32[14256]{0:T(1024)S(1)} %slice_select_fusion.2), channel_id=1, source_target_pairs={{0,1},{1,0},{2,3},{3,2},{4,5},{5,4},{6,7},{7,6},{8,9},{9,8},{10,11... | collective-permute-start | bytes 171080 | tf_op jit(solution)/shard_map/ppermute | solution.py:31
  94.2 2.4 %collective-permute-start.11 = (f32[7128]{0:T(1024)S(1)}, f32[7128]{0:T(1024)S(1)}, u32[]{:S(2)}, u32[]{:S(2)}) collective-permute-start(f32[7128]{0:T(1024)S(1)} %slice_select_fusion.4), channel_id=1, source_target_pairs={{0,2},{1,3},{2,0},{3,1},{4,6},{5,7},{6,4},{7,5},{8,10},{9,11},{10,... | collective-permute-start | bytes 85544 | tf_op jit(solution)/shard_map/ppermute | solution.py:31
  98.6 1.9 %collective-permute-start.12 = (f32[3564]{0:T(1024)S(1)}, f32[3564]{0:T(1024)S(1)}, u32[]{:S(2)}, u32[]{:S(2)}) collective-permute-start(f32[3564]{0:T(1024)S(1)} %slice_select_fusion.6), channel_id=1, source_target_pairs={{0,4},{1,5},{2,6},{3,7},{4,0},{5,1},{6,2},{7,3},{8,12},{9,13},{10,... | collective-permute-start | bytes 42776 | tf_op jit(solution)/shard_map/ppermute | solution.py:31
  102.7 2.1 %collective-permute-start.21 = (f32[35864]{0:T(1024)S(1)}, f32[35864]{0:T(1024)S(1)}, u32[]{:S(2)}, u32[]{:S(2)}) collective-permute-start(f32[35864]{0:T(1024)S(1)} %slice_select_fusion), channel_id=1, source_target_pairs={{0,2},{1,3},{2,0},{3,1},{4,6},{5,7},{6,4},{7,5},{8,10},{9,11},{10,... | collective-permute-start | bytes 430376 | tf_op jit(solution)/shard_map/ppermute | solution.py:31
  104.8 2.4 %collective-permute-start.13 = (f32[1782]{0:T(1024)S(1)}, f32[1782]{0:T(1024)S(1)}, u32[]{:S(2)}, u32[]{:S(2)}) collective-permute-start(f32[1782]{0:T(1024)S(1)} %slice_select_fusion.7), channel_id=1, source_target_pairs={{0,8},{1,9},{2,10},{3,11},{4,12},{5,13},{6,14},{7,15},{8,0},{9,1},... | collective-permute-start | bytes 21392 | tf_op jit(solution)/shard_map/ppermute | solution.py:31
  108.1 2.0 %collective-permute-start.22 = (f32[17932]{0:T(1024)S(1)}, f32[17932]{0:T(1024)S(1)}, u32[]{:S(2)}, u32[]{:S(2)}) collective-permute-start(f32[17932]{0:T(1024)S(1)} %slice_select_fusion.1), channel_id=1, source_target_pairs={{0,4},{1,5},{2,6},{3,7},{4,0},{5,1},{6,2},{7,3},{8,12},{9,13},{10,... | collective-permute-start | bytes 215192 | tf_op jit(solution)/shard_map/ppermute | solution.py:31
  110.2 2.3 %collective-permute-done.22 = f32[17932]{0:T(1024)S(1)} collective-permute-done((f32[17932]{0:T(1024)S(1)}, f32[17932]{0:T(1024)S(1)}, u32[]{:S(2)}, u32[]{:S(2)}) %collective-permute-start.22) | collective-permute-done | bytes 71760 | tf_op jit(solution)/shard_map/ppermute | solution.py:31
  112.7 2.4 %collective-permute-start.23 = (f32[8966]{0:T(1024)S(1)}, f32[8966]{0:T(1024)S(1)}, u32[]{:S(2)}, u32[]{:S(2)}) collective-permute-start(f32[8966]{0:T(1024)S(1)} %slice_select_fusion.3), channel_id=1, source_target_pairs={{0,8},{1,9},{2,10},{3,11},{4,12},{5,13},{6,14},{7,15},{8,0},{9,1},... | collective-permute-start | bytes 107600 | tf_op jit(solution)/shard_map/ppermute | solution.py:31
  117.2 3.0 %collective-permute-start.24 = (f32[4483]{0:T(1024)S(1)}, f32[4483]{0:T(1024)S(1)}, u32[]{:S(2)}, u32[]{:S(2)}) collective-permute-start(f32[4483]{0:T(1024)S(1)} %slice_select_fusion.5), channel_id=1, source_target_pairs={{0,16},{1,17},{2,18},{3,19},{4,20},{5,21},{6,22},{7,23},{8,24},{9,... | collective-permute-start | bytes 53804 | tf_op jit(solution)/shard_map/ppermute | solution.py:31
  122.1 2.9 %collective-permute-start.25 = (f32[4483]{0:T(1024)S(1)}, f32[4483]{0:T(1024)S(1)}, u32[]{:S(2)}, u32[]{:S(2)}) collective-permute-start(f32[4483]{0:T(1024)S(1)} %select_add_fusion.6), channel_id=1, source_target_pairs={{0,16},{1,17},{2,18},{3,19},{4,20},{5,21},{6,22},{7,23},{8,24},{9,... | collective-permute-start | bytes 53804 | tf_op jit(solution)/shard_map/ppermute | solution.py:36
  126.9 2.0 %collective-permute-start.26 = (f32[8966]{0:T(1024)S(1)}, f32[8966]{0:T(1024)S(1)}, u32[]{:S(2)}, u32[]{:S(2)}) collective-permute-start(f32[8966]{0:T(1024)S(1)} %maximum_select_fusion.6), channel_id=1, source_target_pairs={{0,8},{1,9},{2,10},{3,11},{4,12},{5,13},{6,14},{7,15},{8,0},{9,1},... | collective-permute-start | bytes 107600 | tf_op jit(solution)/shard_map/ppermute | solution.py:36
  128.9 2.0 %collective-permute-start.17 = (f32[3564]{0:T(1024)S(1)}, f32[3564]{0:T(1024)S(1)}, u32[]{:S(2)}, u32[]{:S(2)}) collective-permute-start(f32[3564]{0:T(1024)S(1)} %maximum_select_fusion.8), channel_id=1, source_target_pairs={{0,4},{1,5},{2,6},{3,7},{4,0},{5,1},{6,2},{7,3},{8,12},{9,13},{10,... | collective-permute-start | bytes 42776 | tf_op jit(solution)/shard_map/ppermute | solution.py:36
  131.0 2.1 %collective-permute-start.27 = (f32[17932]{0:T(1024)S(1)}, f32[17932]{0:T(1024)S(1)}, u32[]{:S(2)}, u32[]{:S(2)}) collective-permute-start(f32[17932]{0:T(1024)S(1)} %maximum_select_fusion.4), channel_id=1, source_target_pairs={{0,4},{1,5},{2,6},{3,7},{4,0},{5,1},{6,2},{7,3},{8,12},{9,13},{10,... | collective-permute-start | bytes 215192 | tf_op jit(solution)/shard_map/ppermute | solution.py:36
  135.6 2.3 %collective-permute-start.28 = (f32[35864]{0:T(1024)S(1)}, f32[35864]{0:T(1024)S(1)}, u32[]{:S(2)}, u32[]{:S(2)}) collective-permute-start(f32[35864]{0:T(1024)S(1)} %maximum_select_fusion.2), channel_id=1, source_target_pairs={{0,2},{1,3},{2,0},{3,1},{4,6},{5,7},{6,4},{7,5},{8,10},{9,11},{10,... | collective-permute-start | bytes 430376 | tf_op jit(solution)/shard_map/ppermute | solution.py:36
  138.0 3.0 %collective-permute-done.28 = f32[35864]{0:T(1024)S(1)} collective-permute-done((f32[35864]{0:T(1024)S(1)}, f32[35864]{0:T(1024)S(1)}, u32[]{:S(2)}, u32[]{:S(2)}) %collective-permute-start.28) | collective-permute-done | bytes 143488 | tf_op jit(solution)/shard_map/ppermute | solution.py:36
  (413 shorter events, 71.9 us)
Async XLA Ops:
  5.8 11.0 %all-to-all-start = ((bf16[8,10,4,2,128]{4,2,3,1,0:T(4,128)(2,1)}), bf16[8,10,4,2,128]{4,2,3,1,0:T(4,128)(2,1)S(1)}, u32[]{:S(2)}, u32[]{:S(2)}) async-start(bf16[8,10,4,2,128]{4,2,3,1,0:T(4,128)(2,1)} %copy.2729), calls=%async_computation | async-start | bytes 327680 | tf_op jit(solution)/shard_map/all_to_all | solution.py:157
  17.2 4.9 %collective-permute-start = (bf16[1,4,2,264]{3,1,2,0:T(4,128)(2,1)S(1)}, bf16[1,4,2,264]{3,1,2,0:T(4,128)(2,1)S(1)}, u32[]{:S(2)}, u32[]{:S(2)}) collective-permute-start(bf16[1,4,2,264]{3,1,2,0:T(4,128)(2,1)S(1)} %pad_maximum_fusion.20), channel_id=1, source_target_pairs={{0,8},{8,16},{16,24},{1,9},{9,17},{17,25},{2,10},{10,18},{18,26},{... | collective-permute-start | bytes 12680 | tf_op jit(solution)/shard_map/ppermute | solution.py:64
  20.7 5.5 %collective-permute-start.1 = (bf16[1,4,2,264]{3,1,2,0:T(4,128)(2,1)S(1)}, bf16[1,4,2,264]{3,1,2,0:T(4,128)(2,1)S(1)}, u32[]{:S(2)}, u32[]{:S(2)}) collective-permute-start(bf16[1,4,2,264]{3,1,2,0:T(4,128)(2,1)S(1)} %pad_maximum_fusion.20), channel_id=1, source_target_pairs={{8,0},{16,8},{24,16},{9,1},{17,9},{25,17},{10,2},{18,10},{26,18},{... | collective-permute-start | bytes 12680 | tf_op jit(solution)/shard_map/ppermute | solution.py:66
  43.9 9.7 %collective-permute-start.2 = (bf16[64,1,1,128]{3,0,1,2:T(8,128)(2,1)S(1)}, bf16[64,1,1,128]{3,0,1,2:T(8,128)(2,1)S(1)}, u32[]{:S(2)}, u32[]{:S(2)}) collective-permute-start(bf16[64,1,1,128]{3,0,1,2:T(8,128)(2,1)S(1)} %get-tuple-element.264), channel_id=1, source_target_pairs={{0,8},{8,16},{16,24},{1,9},{9,17},{17,25},{2,10},{10,18},{18,26},{... | collective-permute-start | bytes 49160 | tf_op jit(solution)/shard_map/ppermute | solution.py:64
  47.4 6.2 %collective-permute-start.3 = (bf16[64,1,1,128]{3,0,1,2:T(8,128)(2,1)S(1)}, bf16[64,1,1,128]{3,0,1,2:T(8,128)(2,1)S(1)}, u32[]{:S(2)}, u32[]{:S(2)}) collective-permute-start(bf16[64,1,1,128]{3,0,1,2:T(8,128)(2,1)S(1)} %get-tuple-element.265), channel_id=1, source_target_pairs={{8,0},{16,8},{24,16},{9,1},{17,9},{25,17},{10,2},{18,10},{26,18},{... | collective-permute-start | bytes 49160 | tf_op jit(solution)/shard_map/ppermute | solution.py:66
  55.1 5.1 %collective-permute-start.5 = (bf16[64,4,1,1]{3,0,1,2:T(8,128)(2,1)S(1)}, bf16[64,4,1,1]{3,0,1,2:T(8,128)(2,1)S(1)}, u32[]{:S(2)}, u32[]{:S(2)}) collective-permute-start(bf16[64,4,1,1]{3,0,1,2:T(8,128)(2,1)S(1)} %get-tuple-element.260), channel_id=1, source_target_pairs={{1,0},{2,1},{3,2},{4,3},{5,4},{6,5},{7,6},{9,8},{10,9},{11,10},{12... | collective-permute-start | bytes 1544 | tf_op jit(solution)/shard_map/ppermute | solution.py:66
  63.5 15.9 %collective-permute-start.6 = (bf16[32,1,2,256]{3,0,2,1:T(8,128)(2,1)S(1)}, bf16[32,1,2,256]{3,0,2,1:T(8,128)(2,1)S(1)}, u32[]{:S(2)}, u32[]{:S(2)}) collective-permute-start(bf16[32,1,2,256]{3,0,2,1:T(8,128)(2,1)S(1)} %get-tuple-element.258), channel_id=1, source_target_pairs={{0,8},{8,16},{16,24},{1,9},{9,17},{17,25},{2,10},{10,18},{18,26},{... | collective-permute-start | bytes 98312 | tf_op jit(solution)/shard_map/ppermute | solution.py:64
  68.0 11.3 %collective-permute-start.7 = (bf16[32,1,2,256]{3,0,2,1:T(8,128)(2,1)S(1)}, bf16[32,1,2,256]{3,0,2,1:T(8,128)(2,1)S(1)}, u32[]{:S(2)}, u32[]{:S(2)}) collective-permute-start(bf16[32,1,2,256]{3,0,2,1:T(8,128)(2,1)S(1)} %get-tuple-element.259), channel_id=1, source_target_pairs={{8,0},{16,8},{24,16},{9,1},{17,9},{25,17},{10,2},{18,10},{26,18},{... | collective-permute-start | bytes 98312 | tf_op jit(solution)/shard_map/ppermute | solution.py:66
  73.4 23.4 %all-to-all-start.1 = ((bf16[8,2,3,4,2,128]{5,1,4,3,2,0:T(2,128)(2,1)}), bf16[8,2,3,4,2,128]{5,1,4,3,2,0:T(2,128)(2,1)S(1)}, u32[]{:S(2)}, u32[]{:S(2)}) async-start(bf16[8,2,3,4,2,128]{5,1,4,3,2,0:T(2,128)(2,1)} %broadcast_in_dim.57), calls=%async_computation.1 | async-start | bytes 196608 | tf_op jit(solution)/shard_map/all_to_all | solution.py:219
  79.5 7.1 %collective-permute-start.8 = (bf16[32,6,2,1]{3,0,2,1:T(8,128)(2,1)S(1)}, bf16[32,6,2,1]{3,0,2,1:T(8,128)(2,1)S(1)}, u32[]{:S(2)}, u32[]{:S(2)}) collective-permute-start(bf16[32,6,2,1]{3,0,2,1:T(8,128)(2,1)S(1)} %get-tuple-element.256), channel_id=1, source_target_pairs={{0,1},{1,2},{2,3},{3,4},{4,5},{5,6},{6,7},{8,9},{9,10},{10,11},{11... | collective-permute-start | bytes 2312 | tf_op jit(solution)/shard_map/ppermute | solution.py:64
  81.9 4.7 %collective-permute-start.9 = (bf16[32,6,2,1]{3,0,2,1:T(8,128)(2,1)S(1)}, bf16[32,6,2,1]{3,0,2,1:T(8,128)(2,1)S(1)}, u32[]{:S(2)}, u32[]{:S(2)}) collective-permute-start(bf16[32,6,2,1]{3,0,2,1:T(8,128)(2,1)S(1)} %get-tuple-element.257), channel_id=1, source_target_pairs={{1,0},{2,1},{3,2},{4,3},{5,4},{6,5},{7,6},{9,8},{10,9},{11,10},{12... | collective-permute-start | bytes 2312 | tf_op jit(solution)/shard_map/ppermute | solution.py:66
  94.2 4.2 %collective-permute-start.11 = (f32[7128]{0:T(1024)S(1)}, f32[7128]{0:T(1024)S(1)}, u32[]{:S(2)}, u32[]{:S(2)}) collective-permute-start(f32[7128]{0:T(1024)S(1)} %slice_select_fusion.4), channel_id=1, source_target_pairs={{0,2},{1,3},{2,0},{3,1},{4,6},{5,7},{6,4},{7,5},{8,10},{9,11},{10,... | collective-permute-start | bytes 85544 | tf_op jit(solution)/shard_map/ppermute | solution.py:31
  96.7 5.7 %collective-permute-start.20 = (f32[71728]{0:T(1024)S(1)}, f32[71728]{0:T(1024)S(1)}, u32[]{:S(2)}, u32[]{:S(2)}) collective-permute-start(f32[71728]{0:T(1024)S(1)} %broadcast_select_fusion), channel_id=1, source_target_pairs={{0,1},{1,0},{2,3},{3,2},{4,5},{5,4},{6,7},{7,6},{8,9},{9,8},{10,11... | collective-permute-start | bytes 860744 | tf_op jit(solution)/shard_map/ppermute | solution.py:31
  102.7 5.2 %collective-permute-start.21 = (f32[35864]{0:T(1024)S(1)}, f32[35864]{0:T(1024)S(1)}, u32[]{:S(2)}, u32[]{:S(2)}) collective-permute-start(f32[35864]{0:T(1024)S(1)} %slice_select_fusion), channel_id=1, source_target_pairs={{0,2},{1,3},{2,0},{3,1},{4,6},{5,7},{6,4},{7,5},{8,10},{9,11},{10,... | collective-permute-start | bytes 430376 | tf_op jit(solution)/shard_map/ppermute | solution.py:31
  104.8 5.3 %collective-permute-start.13 = (f32[1782]{0:T(1024)S(1)}, f32[1782]{0:T(1024)S(1)}, u32[]{:S(2)}, u32[]{:S(2)}) collective-permute-start(f32[1782]{0:T(1024)S(1)} %slice_select_fusion.7), channel_id=1, source_target_pairs={{0,8},{1,9},{2,10},{3,11},{4,12},{5,13},{6,14},{7,15},{8,0},{9,1},... | collective-permute-start | bytes 21392 | tf_op jit(solution)/shard_map/ppermute | solution.py:31
  108.1 4.4 %collective-permute-start.22 = (f32[17932]{0:T(1024)S(1)}, f32[17932]{0:T(1024)S(1)}, u32[]{:S(2)}, u32[]{:S(2)}) collective-permute-start(f32[17932]{0:T(1024)S(1)} %slice_select_fusion.1), channel_id=1, source_target_pairs={{0,4},{1,5},{2,6},{3,7},{4,0},{5,1},{6,2},{7,3},{8,12},{9,13},{10,... | collective-permute-start | bytes 215192 | tf_op jit(solution)/shard_map/ppermute | solution.py:31
  112.7 4.4 %collective-permute-start.23 = (f32[8966]{0:T(1024)S(1)}, f32[8966]{0:T(1024)S(1)}, u32[]{:S(2)}, u32[]{:S(2)}) collective-permute-start(f32[8966]{0:T(1024)S(1)} %slice_select_fusion.3), channel_id=1, source_target_pairs={{0,8},{1,9},{2,10},{3,11},{4,12},{5,13},{6,14},{7,15},{8,0},{9,1},... | collective-permute-start | bytes 107600 | tf_op jit(solution)/shard_map/ppermute | solution.py:31
  115.2 5.1 %collective-permute-start.14 = (f32[891]{0:T(1024)S(1)}, f32[891]{0:T(1024)S(1)}, u32[]{:S(2)}, u32[]{:S(2)}) collective-permute-start(f32[891]{0:T(1024)S(1)} %slice_select_fusion.8), channel_id=1, source_target_pairs={{0,16},{1,17},{2,18},{3,19},{4,20},{5,21},{6,22},{7,23},{8,24},{9,... | collective-permute-start | bytes 10700 | tf_op jit(solution)/shard_map/ppermute | solution.py:31
  117.2 4.8 %collective-permute-start.24 = (f32[4483]{0:T(1024)S(1)}, f32[4483]{0:T(1024)S(1)}, u32[]{:S(2)}, u32[]{:S(2)}) collective-permute-start(f32[4483]{0:T(1024)S(1)} %slice_select_fusion.5), channel_id=1, source_target_pairs={{0,16},{1,17},{2,18},{3,19},{4,20},{5,21},{6,22},{7,23},{8,24},{9,... | collective-permute-start | bytes 53804 | tf_op jit(solution)/shard_map/ppermute | solution.py:31
  120.4 4.7 %collective-permute-start.15 = (f32[891]{0:T(1024)S(1)}, f32[891]{0:T(1024)S(1)}, u32[]{:S(2)}, u32[]{:S(2)}) collective-permute-start(f32[891]{0:T(1024)S(1)} %select_add_fusion.9), channel_id=1, source_target_pairs={{0,16},{1,17},{2,18},{3,19},{4,20},{5,21},{6,22},{7,23},{8,24},{9,... | collective-permute-start | bytes 10700 | tf_op jit(solution)/shard_map/ppermute | solution.py:36
  122.1 4.7 %collective-permute-start.25 = (f32[4483]{0:T(1024)S(1)}, f32[4483]{0:T(1024)S(1)}, u32[]{:S(2)}, u32[]{:S(2)}) collective-permute-start(f32[4483]{0:T(1024)S(1)} %select_add_fusion.6), channel_id=1, source_target_pairs={{0,16},{1,17},{2,18},{3,19},{4,20},{5,21},{6,22},{7,23},{8,24},{9,... | collective-permute-start | bytes 53804 | tf_op jit(solution)/shard_map/ppermute | solution.py:36
  131.0 4.4 %collective-permute-start.27 = (f32[17932]{0:T(1024)S(1)}, f32[17932]{0:T(1024)S(1)}, u32[]{:S(2)}, u32[]{:S(2)}) collective-permute-start(f32[17932]{0:T(1024)S(1)} %maximum_select_fusion.4), channel_id=1, source_target_pairs={{0,4},{1,5},{2,6},{3,7},{4,0},{5,1},{6,2},{7,3},{8,12},{9,13},{10,... | collective-permute-start | bytes 215192 | tf_op jit(solution)/shard_map/ppermute | solution.py:36
  133.2 4.7 %collective-permute-start.18 = (f32[7128]{0:T(1024)S(1)}, f32[7128]{0:T(1024)S(1)}, u32[]{:S(2)}, u32[]{:S(2)}) collective-permute-start(f32[7128]{0:T(1024)S(1)} %maximum_select_fusion.7), channel_id=1, source_target_pairs={{0,2},{1,3},{2,0},{3,1},{4,6},{5,7},{6,4},{7,5},{8,10},{9,11},{10,... | collective-permute-start | bytes 85544 | tf_op jit(solution)/shard_map/ppermute | solution.py:36
  135.6 5.4 %collective-permute-start.28 = (f32[35864]{0:T(1024)S(1)}, f32[35864]{0:T(1024)S(1)}, u32[]{:S(2)}, u32[]{:S(2)}) collective-permute-start(f32[35864]{0:T(1024)S(1)} %maximum_select_fusion.2), channel_id=1, source_target_pairs={{0,2},{1,3},{2,0},{3,1},{4,6},{5,7},{6,4},{7,5},{8,10},{9,11},{10,... | collective-permute-start | bytes 430376 | tf_op jit(solution)/shard_map/ppermute | solution.py:36
  (32 other events, 221.5 us)

commit v6 on v5

--- a/solution.py
+++ b/solution.py
@@ -179,8 +179,11 @@
     h0_wide = jnp.pad(h0_wide, ((0, 0), (0, 0), (1, 1), (0, 0)))
     h0 = h0_wide[:, 3:-3, 1:-1, 3:-3]
     h0_pad = h0_wide[:, 2:-2, :, 2:-2]
+    h0_cols = windows(h0_wide)
     h1_wide = jax.nn.relu(
-        h0_wide[:, 1:-1, 1:-1, 1:-1].astype(single_float) + convolve(h0_wide, w_res)
+        h0_wide[:, 1:-1, 1:-1, 1:-1].astype(single_float) + jnp.einsum(
+            "toc,tczyx->ozyx", w_res, h0_cols, preferred_element_type=single_float
+        )
     ).astype(brain_float_half)
     h1 = h1_wide[:, 2:-2, :, 2:-2]
     down_cube = w_down.reshape((2, 2, 2) + w_down.shape[1:])
@@ -247,7 +250,12 @@
         jnp.einsum("abeoc,ozyx->czaybxe", down_cube, gdd, preferred_element_type=single_float)
     )
     gres = jnp.where(h1 > 0, gsf.astype(single_float) + spread, 0.0).astype(brain_float_half)
-    grad_res = tap_grads(gres, h0_pad)
+    grad_res = jnp.einsum(
+        "ozyx,tczyx->toc",
+        gres,
+        h0_cols[:, :, 2:-2, :, 2:-2],
+        preferred_element_type=single_float,
+    )
     gfirst = gres.astype(single_float) + convolve(framed(gres), flipped(w_res))
     gact = jnp.where(h0 > 0, gfirst, 0.0).astype(brain_float_half)
     grad_in = tap_grads(gact, image_pad)[:, :, 0]

time: 148 us -> 147 us (level)
  waiting for transfers between devices: 20.3 us -> 28.1 us
  starting transfers between devices: 67.7 us -> 60.1 us
    dot_general x0 -> x2, matrix products: none -> 5.86 us  [the longest x1 3.98 us: local(): jnp.einsum('ozyx,tczyx->toc', gres, h0_cols[:, :, 2:-2, :, 2:-2], preferr...]
    ppermute x10, starting transfers between devices: 14.2 us -> 10.8 us  [tree_sum(): other = lax.ppermute(cur, axes, pairs)]
    ppermute x10, waiting for transfers between devices: 7.31 us -> 10.5 us  [tree_sum(): cur = keep + lax.ppermute(send, axes, pairs)]
    ppermute x10, starting transfers between devices: 20.6 us -> 17.5 us  [tree_sum(): cur = keep + lax.ppermute(send, axes, pairs)]
    ppermute x10, waiting for transfers between devices: 4.87 us -> 7.95 us  [tree_sum(): other = lax.ppermute(cur, axes, pairs)]
    dot_general x3 -> x2, matrix products: 3.63 us -> 0.6 us  [tap_grads(): jnp.einsum('ozyx,tczyx->toc', grad, windows(padded), preferred_element_ty...]
    dot_general x5 -> x4, matrix products: 3.59 us -> 1.71 us  [convolve(): jnp.einsum('toc,tczyx->ozyx', weights, windows(padded), preferred_element...]
    ppermute x5, waiting for transfers between devices: 7.78 us -> 9.57 us  [with_halo(): lax.ppermute(head, axis, [((i + 1) % count, i) for i in range(ends)])]
  transfers between devices with their start and end apart: 32 -> 32, of which waited for: 13 -> 16; matrix products, arithmetic and copies ran while one was open for 18% -> 18% of each run, Pallas kernels for 0% -> 0%
where the time goes in v6:
time: 147 us; the launch traced here: 146 us
  starting transfers between devices  60.1 us (41%)
  local copies, waits for them, and re-layouts  33.1 us (23%)
  waiting for transfers between devices  28.1 us (19%)
  matrix products  14.7 us (10%)
  other arithmetic  6.61 us (4%)
  between operations  3.2 us (2%)
    ppermute x10, starting transfers between devices, tree_sum(): cur = keep + lax.ppermute(send, axes, pairs)  17.5 us
    unnamed x202, local copies, waits for them, and re-layouts  15.2 us
    ppermute x5, starting transfers between devices, with_halo(): lax.ppermute(tail, axis, [(i, (i + 1) % count) for i in range(ends)])  14.1 us
    ppermute x10, starting transfers between devices, tree_sum(): other = lax.ppermute(cur, axes, pairs)  10.8 us
    ppermute x10, waiting for transfers between devices, tree_sum(): cur = keep + lax.ppermute(send, axes, pairs)  10.5 us
    ppermute x5, waiting for transfers between devices, with_halo(): lax.ppermute(head, axis, [((i + 1) % count, i) for i in range(ends)])  9.57 us
    ppermute x10, waiting for transfers between devices, tree_sum(): other = lax.ppermute(cur, axes, pairs)  7.95 us
    ppermute x5, starting transfers between devices, with_halo(): lax.ppermute(head, axis, [((i + 1) % count, i) for i in range(ends)])  6.63 us
  transfers between devices with their start and end apart: 32, of which 16 were waited for; matrix products, arithmetic and copies ran while one was open for 18% of the time, Pallas kernels for 0%

profile of v6, /device:TPU:0, one launch (start us, length us, event | category | flops | bytes accessed | tf_op | source)
XLA Modules:
  0.0 145.7 jit_solution(17775658370004686086)
XLA Ops:
  5.8 5.2 %all-to-all-start = ((bf16[8,10,4,2,128]{4,2,3,1,0:T(4,128)(2,1)}), bf16[8,10,4,2,128]{4,2,3,1,0:T(4,128)(2,1)S(1)}, u32[]{:S(2)}, u32[]{:S(2)}) async-start(bf16[8,10,4,2,128]{4,2,3,1,0:T(4,128)(2,1)} %copy.2653), calls=%async_computation | async-start | bytes 327680 | tf_op jit(solution)/shard_map/all_to_all | solution.py:157
  17.5 3.5 %collective-permute-start = (bf16[1,4,2,264]{3,1,2,0:T(4,128)(2,1)S(1)}, bf16[1,4,2,264]{3,1,2,0:T(4,128)(2,1)S(1)}, u32[]{:S(2)}, u32[]{:S(2)}) collective-permute-start(bf16[1,4,2,264]{3,1,2,0:T(4,128)(2,1)S(1)} %pad_maximum_fusion.20), channel_id=1, source_target_pairs={{0,8},{8,16},{16,24},{1,9},{9,17},{17,25},{2,10},{10,18},{18,26},{... | collective-permute-start | bytes 12680 | tf_op jit(solution)/shard_map/ppermute | solution.py:64
  23.0 3.5 %collective-permute-done.1 = bf16[1,4,2,264]{3,1,2,0:T(4,128)(2,1)S(1)} collective-permute-done((bf16[1,4,2,264]{3,1,2,0:T(4,128)(2,1)S(1)}, bf16[1,4,2,264]{3,1,2,0:T(4,128)(2,1)S(1)}, u32[]{:S(2)}, u32[]{:S(2)}) %collective-permute-start.1) | collective-permute-done | bytes 4256 | tf_op jit(solution)/shard_map/ppermute | solution.py:66
  31.5 1.9 %convolution_bitcast_fusion.1 = f32[8,2,260,32]{2,3,0,1:T(8,128)S(1)} fusion(bf16[27,32,32]{2,1,0:T(8,128)(2,1)S(1)} %copy-done.10, bf16[27,32,8,2,260]{4,1,3,2,0:T(8,128)(2,1)S(1)} %fusion.82), kind=kOutput, calls=%fused_computation.27 | convolution fusion | flops 230031360 | bytes 7776256 | tf_op jit(solution)/shard_map/toc,tczyx->ozyx/dot_general | solution.py:184
  33.4 2.2 %copy-done.16 = bf16[27,32,8,2,260]{4,1,3,2,0:T(8,128)(2,1)} copy-done((bf16[27,32,8,2,260]{4,1,3,2,0:T(8,128)(2,1)}, bf16[27,32,8,2,260]{4,1,3,2,0:T(8,128)(2,1)S(1)}, u32[]{:S(2)}) %copy-start.16) | copy-done | bytes 7188504
  43.6 3.5 %collective-permute-start.2 = (bf16[64,1,1,128]{3,0,1,2:T(8,128)(2,1)S(1)}, bf16[64,1,1,128]{3,0,1,2:T(8,128)(2,1)S(1)}, u32[]{:S(2)}, u32[]{:S(2)}) collective-permute-start(bf16[64,1,1,128]{3,0,1,2:T(8,128)(2,1)S(1)} %get-tuple-element.264), channel_id=1, source_target_pairs={{0,8},{8,16},{16,24},{1,9},{9,17},{17,25},{2,10},{10,18},{18,26},{... | collective-permute-start | bytes 49160 | tf_op jit(solution)/shard_map/ppermute | solution.py:64
  50.4 2.3 %collective-permute-done.3 = bf16[64,1,1,128]{3,0,1,2:T(8,128)(2,1)S(1)} collective-permute-done((bf16[64,1,1,128]{3,0,1,2:T(8,128)(2,1)S(1)}, bf16[64,1,1,128]{3,0,1,2:T(8,128)(2,1)S(1)}, u32[]{:S(2)}, u32[]{:S(2)}) %collective-permute-start.3) | collective-permute-done | bytes 16416 | tf_op jit(solution)/shard_map/ppermute | solution.py:66
  55.8 3.8 %collective-permute-done.5 = bf16[64,4,1,1]{3,0,1,2:T(8,128)(2,1)S(1)} collective-permute-done((bf16[64,4,1,1]{3,0,1,2:T(8,128)(2,1)S(1)}, bf16[64,4,1,1]{3,0,1,2:T(8,128)(2,1)S(1)}, u32[]{:S(2)}, u32[]{:S(2)}) %collective-permute-start.5) | collective-permute-done | bytes 544 | tf_op jit(solution)/shard_map/ppermute | solution.py:66
  62.8 3.5 %collective-permute-start.6 = (bf16[32,1,2,256]{3,0,2,1:T(8,128)(2,1)S(1)}, bf16[32,1,2,256]{3,0,2,1:T(8,128)(2,1)S(1)}, u32[]{:S(2)}, u32[]{:S(2)}) collective-permute-start(bf16[32,1,2,256]{3,0,2,1:T(8,128)(2,1)S(1)} %get-tuple-element.258), channel_id=1, source_target_pairs={{0,8},{8,16},{16,24},{1,9},{9,17},{17,25},{2,10},{10,18},{18,26},{... | collective-permute-start | bytes 98312 | tf_op jit(solution)/shard_map/ppermute | solution.py:64
  71.7 5.9 %all-to-all-start.1 = ((bf16[8,2,3,4,2,128]{5,1,4,3,2,0:T(2,128)(2,1)}), bf16[8,2,3,4,2,128]{5,1,4,3,2,0:T(2,128)(2,1)S(1)}, u32[]{:S(2)}, u32[]{:S(2)}) async-start(bf16[8,2,3,4,2,128]{5,1,4,3,2,0:T(2,128)(2,1)} %broadcast_in_dim.57), calls=%async_computation.1 | async-start | bytes 196608 | tf_op jit(solution)/shard_map/all_to_all | solution.py:222
  77.8 2.4 %collective-permute-start.8 = (bf16[32,6,2,1]{3,0,2,1:T(8,128)(2,1)S(1)}, bf16[32,6,2,1]{3,0,2,1:T(8,128)(2,1)S(1)}, u32[]{:S(2)}, u32[]{:S(2)}) collective-permute-start(bf16[32,6,2,1]{3,0,2,1:T(8,128)(2,1)S(1)} %get-tuple-element.256), channel_id=1, source_target_pairs={{0,1},{1,2},{2,3},{3,4},{4,5},{5,6},{6,7},{8,9},{9,10},{10,11},{11... | collective-permute-start | bytes 2312 | tf_op jit(solution)/shard_map/ppermute | solution.py:64
  81.5 4.0 %fusion.7 = f32[27,32,32]{1,2,0:T(8,128)S(1)} fusion(bf16[27,32,8,2,260]{4,1,3,2,0:T(8,128)(2,1)} %copy-done.16, bf16[32,4,2,256]{3,0,2,1:T(8,128)(2,1)S(1)} %select_convert_fusion), kind=kOutput, calls=%fused_computation.30 | convolution fusion | flops 113246208 | bytes 3780608 | tf_op jit(solution)/shard_map/ozyx,tczyx->toc/dot_general | solution.py:253
  89.4 2.3 %collective-permute-start.10 = (f32[14256]{0:T(1024)S(1)}, f32[14256]{0:T(1024)S(1)}, u32[]{:S(2)}, u32[]{:S(2)}) collective-permute-start(f32[14256]{0:T(1024)S(1)} %slice_select_fusion.2), channel_id=1, source_target_pairs={{0,1},{1,0},{2,3},{3,2},{4,5},{5,4},{6,7},{7,6},{8,9},{9,8},{10,11... | collective-permute-start | bytes 171080 | tf_op jit(solution)/shard_map/ppermute | solution.py:31
  92.8 2.0 %collective-permute-start.11 = (f32[7128]{0:T(1024)S(1)}, f32[7128]{0:T(1024)S(1)}, u32[]{:S(2)}, u32[]{:S(2)}) collective-permute-start(f32[7128]{0:T(1024)S(1)} %slice_select_fusion.4), channel_id=1, source_target_pairs={{0,2},{1,3},{2,0},{3,1},{4,6},{5,7},{6,4},{7,5},{8,10},{9,11},{10,... | collective-permute-start | bytes 85544 | tf_op jit(solution)/shard_map/ppermute | solution.py:31
  96.9 2.9 %collective-permute-start.12 = (f32[3564]{0:T(1024)S(1)}, f32[3564]{0:T(1024)S(1)}, u32[]{:S(2)}, u32[]{:S(2)}) collective-permute-start(f32[3564]{0:T(1024)S(1)} %slice_select_fusion.6), channel_id=1, source_target_pairs={{0,4},{1,5},{2,6},{3,7},{4,0},{5,1},{6,2},{7,3},{8,12},{9,13},{10,... | collective-permute-start | bytes 42776 | tf_op jit(solution)/shard_map/ppermute | solution.py:31
  103.1 2.4 %collective-permute-start.13 = (f32[1782]{0:T(1024)S(1)}, f32[1782]{0:T(1024)S(1)}, u32[]{:S(2)}, u32[]{:S(2)}) collective-permute-start(f32[1782]{0:T(1024)S(1)} %slice_select_fusion.7), channel_id=1, source_target_pairs={{0,8},{1,9},{2,10},{3,11},{4,12},{5,13},{6,14},{7,15},{8,0},{9,1},... | collective-permute-start | bytes 21392 | tf_op jit(solution)/shard_map/ppermute | solution.py:31
  107.2 2.1 %collective-permute-start.22 = (f32[17932]{0:T(1024)S(1)}, f32[17932]{0:T(1024)S(1)}, u32[]{:S(2)}, u32[]{:S(2)}) collective-permute-start(f32[17932]{0:T(1024)S(1)} %slice_select_fusion.1), channel_id=1, source_target_pairs={{0,4},{1,5},{2,6},{3,7},{4,0},{5,1},{6,2},{7,3},{8,12},{9,13},{10,... | collective-permute-start | bytes 215192 | tf_op jit(solution)/shard_map/ppermute | solution.py:31
  109.4 2.3 %collective-permute-done.22 = f32[17932]{0:T(1024)S(1)} collective-permute-done((f32[17932]{0:T(1024)S(1)}, f32[17932]{0:T(1024)S(1)}, u32[]{:S(2)}, u32[]{:S(2)}) %collective-permute-start.22) | collective-permute-done | bytes 71760 | tf_op jit(solution)/shard_map/ppermute | solution.py:31
  111.8 2.4 %collective-permute-start.23 = (f32[8966]{0:T(1024)S(1)}, f32[8966]{0:T(1024)S(1)}, u32[]{:S(2)}, u32[]{:S(2)}) collective-permute-start(f32[8966]{0:T(1024)S(1)} %slice_select_fusion.3), channel_id=1, source_target_pairs={{0,8},{1,9},{2,10},{3,11},{4,12},{5,13},{6,14},{7,15},{8,0},{9,1},... | collective-permute-start | bytes 107600 | tf_op jit(solution)/shard_map/ppermute | solution.py:31
  123.5 2.3 %collective-permute-done.25 = f32[4483]{0:T(1024)S(1)} collective-permute-done((f32[4483]{0:T(1024)S(1)}, f32[4483]{0:T(1024)S(1)}, u32[]{:S(2)}, u32[]{:S(2)}) %collective-permute-start.25) | collective-permute-done | bytes 17964 | tf_op jit(solution)/shard_map/ppermute | solution.py:36
  125.9 2.3 %collective-permute-start.26 = (f32[8966]{0:T(1024)S(1)}, f32[8966]{0:T(1024)S(1)}, u32[]{:S(2)}, u32[]{:S(2)}) collective-permute-start(f32[8966]{0:T(1024)S(1)} %maximum_select_fusion.6), channel_id=1, source_target_pairs={{0,8},{1,9},{2,10},{3,11},{4,12},{5,13},{6,14},{7,15},{8,0},{9,1},... | collective-permute-start | bytes 107600 | tf_op jit(solution)/shard_map/ppermute | solution.py:36
  128.3 1.9 %collective-permute-start.17 = (f32[3564]{0:T(1024)S(1)}, f32[3564]{0:T(1024)S(1)}, u32[]{:S(2)}, u32[]{:S(2)}) collective-permute-start(f32[3564]{0:T(1024)S(1)} %maximum_select_fusion.8), channel_id=1, source_target_pairs={{0,4},{1,5},{2,6},{3,7},{4,0},{5,1},{6,2},{7,3},{8,12},{9,13},{10,... | collective-permute-start | bytes 42776 | tf_op jit(solution)/shard_map/ppermute | solution.py:36
  130.2 1.9 %collective-permute-start.27 = (f32[17932]{0:T(1024)S(1)}, f32[17932]{0:T(1024)S(1)}, u32[]{:S(2)}, u32[]{:S(2)}) collective-permute-start(f32[17932]{0:T(1024)S(1)} %maximum_select_fusion.4), channel_id=1, source_target_pairs={{0,4},{1,5},{2,6},{3,7},{4,0},{5,1},{6,2},{7,3},{8,12},{9,13},{10,... | collective-permute-start | bytes 215192 | tf_op jit(solution)/shard_map/ppermute | solution.py:36
  136.3 3.7 %collective-permute-done.28 = f32[35864]{0:T(1024)S(1)} collective-permute-done((f32[35864]{0:T(1024)S(1)}, f32[35864]{0:T(1024)S(1)}, u32[]{:S(2)}, u32[]{:S(2)}) %collective-permute-start.28) | collective-permute-done | bytes 143488 | tf_op jit(solution)/shard_map/ppermute | solution.py:36
  (392 shorter events, 72.6 us)
Async XLA Ops:
  5.8 11.3 %all-to-all-start = ((bf16[8,10,4,2,128]{4,2,3,1,0:T(4,128)(2,1)}), bf16[8,10,4,2,128]{4,2,3,1,0:T(4,128)(2,1)S(1)}, u32[]{:S(2)}, u32[]{:S(2)}) async-start(bf16[8,10,4,2,128]{4,2,3,1,0:T(4,128)(2,1)} %copy.2653), calls=%async_computation | async-start | bytes 327680 | tf_op jit(solution)/shard_map/all_to_all | solution.py:157
  17.5 5.5 %collective-permute-start = (bf16[1,4,2,264]{3,1,2,0:T(4,128)(2,1)S(1)}, bf16[1,4,2,264]{3,1,2,0:T(4,128)(2,1)S(1)}, u32[]{:S(2)}, u32[]{:S(2)}) collective-permute-start(bf16[1,4,2,264]{3,1,2,0:T(4,128)(2,1)S(1)} %pad_maximum_fusion.20), channel_id=1, source_target_pairs={{0,8},{8,16},{16,24},{1,9},{9,17},{17,25},{2,10},{10,18},{18,26},{... | collective-permute-start | bytes 12680 | tf_op jit(solution)/shard_map/ppermute | solution.py:64
  21.0 5.5 %collective-permute-start.1 = (bf16[1,4,2,264]{3,1,2,0:T(4,128)(2,1)S(1)}, bf16[1,4,2,264]{3,1,2,0:T(4,128)(2,1)S(1)}, u32[]{:S(2)}, u32[]{:S(2)}) collective-permute-start(bf16[1,4,2,264]{3,1,2,0:T(4,128)(2,1)S(1)} %pad_maximum_fusion.20), channel_id=1, source_target_pairs={{8,0},{16,8},{24,16},{9,1},{17,9},{25,17},{10,2},{18,10},{26,18},{... | collective-permute-start | bytes 12680 | tf_op jit(solution)/shard_map/ppermute | solution.py:66
  43.6 6.9 %collective-permute-start.2 = (bf16[64,1,1,128]{3,0,1,2:T(8,128)(2,1)S(1)}, bf16[64,1,1,128]{3,0,1,2:T(8,128)(2,1)S(1)}, u32[]{:S(2)}, u32[]{:S(2)}) collective-permute-start(bf16[64,1,1,128]{3,0,1,2:T(8,128)(2,1)S(1)} %get-tuple-element.264), channel_id=1, source_target_pairs={{0,8},{8,16},{16,24},{1,9},{9,17},{17,25},{2,10},{10,18},{18,26},{... | collective-permute-start | bytes 49160 | tf_op jit(solution)/shard_map/ppermute | solution.py:64
  47.1 5.6 %collective-permute-start.3 = (bf16[64,1,1,128]{3,0,1,2:T(8,128)(2,1)S(1)}, bf16[64,1,1,128]{3,0,1,2:T(8,128)(2,1)S(1)}, u32[]{:S(2)}, u32[]{:S(2)}) collective-permute-start(bf16[64,1,1,128]{3,0,1,2:T(8,128)(2,1)S(1)} %get-tuple-element.265), channel_id=1, source_target_pairs={{8,0},{16,8},{24,16},{9,1},{17,9},{25,17},{10,2},{18,10},{26,18},{... | collective-permute-start | bytes 49160 | tf_op jit(solution)/shard_map/ppermute | solution.py:66
  54.2 5.4 %collective-permute-start.5 = (bf16[64,4,1,1]{3,0,1,2:T(8,128)(2,1)S(1)}, bf16[64,4,1,1]{3,0,1,2:T(8,128)(2,1)S(1)}, u32[]{:S(2)}, u32[]{:S(2)}) collective-permute-start(bf16[64,4,1,1]{3,0,1,2:T(8,128)(2,1)S(1)} %get-tuple-element.260), channel_id=1, source_target_pairs={{1,0},{2,1},{3,2},{4,3},{5,4},{6,5},{7,6},{9,8},{10,9},{11,10},{12... | collective-permute-start | bytes 1544 | tf_op jit(solution)/shard_map/ppermute | solution.py:66
  62.8 14.8 %collective-permute-start.6 = (bf16[32,1,2,256]{3,0,2,1:T(8,128)(2,1)S(1)}, bf16[32,1,2,256]{3,0,2,1:T(8,128)(2,1)S(1)}, u32[]{:S(2)}, u32[]{:S(2)}) collective-permute-start(bf16[32,1,2,256]{3,0,2,1:T(8,128)(2,1)S(1)} %get-tuple-element.258), channel_id=1, source_target_pairs={{0,8},{8,16},{16,24},{1,9},{9,17},{17,25},{2,10},{10,18},{18,26},{... | collective-permute-start | bytes 98312 | tf_op jit(solution)/shard_map/ppermute | solution.py:64
  66.3 11.3 %collective-permute-start.7 = (bf16[32,1,2,256]{3,0,2,1:T(8,128)(2,1)S(1)}, bf16[32,1,2,256]{3,0,2,1:T(8,128)(2,1)S(1)}, u32[]{:S(2)}, u32[]{:S(2)}) collective-permute-start(bf16[32,1,2,256]{3,0,2,1:T(8,128)(2,1)S(1)} %get-tuple-element.259), channel_id=1, source_target_pairs={{8,0},{16,8},{24,16},{9,1},{17,9},{25,17},{10,2},{18,10},{26,18},{... | collective-permute-start | bytes 98312 | tf_op jit(solution)/shard_map/ppermute | solution.py:66
  71.7 23.4 %all-to-all-start.1 = ((bf16[8,2,3,4,2,128]{5,1,4,3,2,0:T(2,128)(2,1)}), bf16[8,2,3,4,2,128]{5,1,4,3,2,0:T(2,128)(2,1)S(1)}, u32[]{:S(2)}, u32[]{:S(2)}) async-start(bf16[8,2,3,4,2,128]{5,1,4,3,2,0:T(2,128)(2,1)} %broadcast_in_dim.57), calls=%async_computation.1 | async-start | bytes 196608 | tf_op jit(solution)/shard_map/all_to_all | solution.py:222
  77.8 8.0 %collective-permute-start.8 = (bf16[32,6,2,1]{3,0,2,1:T(8,128)(2,1)S(1)}, bf16[32,6,2,1]{3,0,2,1:T(8,128)(2,1)S(1)}, u32[]{:S(2)}, u32[]{:S(2)}) collective-permute-start(bf16[32,6,2,1]{3,0,2,1:T(8,128)(2,1)S(1)} %get-tuple-element.256), channel_id=1, source_target_pairs={{0,1},{1,2},{2,3},{3,4},{4,5},{5,6},{6,7},{8,9},{9,10},{10,11},{11... | collective-permute-start | bytes 2312 | tf_op jit(solution)/shard_map/ppermute | solution.py:64
  80.2 5.6 %collective-permute-start.9 = (bf16[32,6,2,1]{3,0,2,1:T(8,128)(2,1)S(1)}, bf16[32,6,2,1]{3,0,2,1:T(8,128)(2,1)S(1)}, u32[]{:S(2)}, u32[]{:S(2)}) collective-permute-start(bf16[32,6,2,1]{3,0,2,1:T(8,128)(2,1)S(1)} %get-tuple-element.257), channel_id=1, source_target_pairs={{1,0},{2,1},{3,2},{4,3},{5,4},{6,5},{7,6},{9,8},{10,9},{11,10},{12... | collective-permute-start | bytes 2312 | tf_op jit(solution)/shard_map/ppermute | solution.py:66
  95.0 6.5 %collective-permute-start.20 = (f32[71728]{0:T(1024)S(1)}, f32[71728]{0:T(1024)S(1)}, u32[]{:S(2)}, u32[]{:S(2)}) collective-permute-start(f32[71728]{0:T(1024)S(1)} %broadcast_select_fusion), channel_id=1, source_target_pairs={{0,1},{1,0},{2,3},{3,2},{4,5},{5,4},{6,7},{7,6},{8,9},{9,8},{10,11... | collective-permute-start | bytes 860744 | tf_op jit(solution)/shard_map/ppermute | solution.py:31
  96.9 4.6 %collective-permute-start.12 = (f32[3564]{0:T(1024)S(1)}, f32[3564]{0:T(1024)S(1)}, u32[]{:S(2)}, u32[]{:S(2)}) collective-permute-start(f32[3564]{0:T(1024)S(1)} %slice_select_fusion.6), channel_id=1, source_target_pairs={{0,4},{1,5},{2,6},{3,7},{4,0},{5,1},{6,2},{7,3},{8,12},{9,13},{10,... | collective-permute-start | bytes 42776 | tf_op jit(solution)/shard_map/ppermute | solution.py:31
  101.8 5.2 %collective-permute-start.21 = (f32[35864]{0:T(1024)S(1)}, f32[35864]{0:T(1024)S(1)}, u32[]{:S(2)}, u32[]{:S(2)}) collective-permute-start(f32[35864]{0:T(1024)S(1)} %slice_select_fusion), channel_id=1, source_target_pairs={{0,2},{1,3},{2,0},{3,1},{4,6},{5,7},{6,4},{7,5},{8,10},{9,11},{10,... | collective-permute-start | bytes 430376 | tf_op jit(solution)/shard_map/ppermute | solution.py:31
  103.1 6.2 %collective-permute-start.13 = (f32[1782]{0:T(1024)S(1)}, f32[1782]{0:T(1024)S(1)}, u32[]{:S(2)}, u32[]{:S(2)}) collective-permute-start(f32[1782]{0:T(1024)S(1)} %slice_select_fusion.7), channel_id=1, source_target_pairs={{0,8},{1,9},{2,10},{3,11},{4,12},{5,13},{6,14},{7,15},{8,0},{9,1},... | collective-permute-start | bytes 21392 | tf_op jit(solution)/shard_map/ppermute | solution.py:31
  107.2 4.4 %collective-permute-start.22 = (f32[17932]{0:T(1024)S(1)}, f32[17932]{0:T(1024)S(1)}, u32[]{:S(2)}, u32[]{:S(2)}) collective-permute-start(f32[17932]{0:T(1024)S(1)} %slice_select_fusion.1), channel_id=1, source_target_pairs={{0,4},{1,5},{2,6},{3,7},{4,0},{5,1},{6,2},{7,3},{8,12},{9,13},{10,... | collective-permute-start | bytes 215192 | tf_op jit(solution)/shard_map/ppermute | solution.py:31
  111.8 4.4 %collective-permute-start.23 = (f32[8966]{0:T(1024)S(1)}, f32[8966]{0:T(1024)S(1)}, u32[]{:S(2)}, u32[]{:S(2)}) collective-permute-start(f32[8966]{0:T(1024)S(1)} %slice_select_fusion.3), channel_id=1, source_target_pairs={{0,8},{1,9},{2,10},{3,11},{4,12},{5,13},{6,14},{7,15},{8,0},{9,1},... | collective-permute-start | bytes 107600 | tf_op jit(solution)/shard_map/ppermute | solution.py:31
  114.3 4.5 %collective-permute-start.14 = (f32[891]{0:T(1024)S(1)}, f32[891]{0:T(1024)S(1)}, u32[]{:S(2)}, u32[]{:S(2)}) collective-permute-start(f32[891]{0:T(1024)S(1)} %slice_select_fusion.8), channel_id=1, source_target_pairs={{0,16},{1,17},{2,18},{3,19},{4,20},{5,21},{6,22},{7,23},{8,24},{9,... | collective-permute-start | bytes 10700 | tf_op jit(solution)/shard_map/ppermute | solution.py:31
  116.3 4.7 %collective-permute-start.24 = (f32[4483]{0:T(1024)S(1)}, f32[4483]{0:T(1024)S(1)}, u32[]{:S(2)}, u32[]{:S(2)}) collective-permute-start(f32[4483]{0:T(1024)S(1)} %slice_select_fusion.5), channel_id=1, source_target_pairs={{0,16},{1,17},{2,18},{3,19},{4,20},{5,21},{6,22},{7,23},{8,24},{9,... | collective-permute-start | bytes 53804 | tf_op jit(solution)/shard_map/ppermute | solution.py:31
  118.9 4.5 %collective-permute-start.15 = (f32[891]{0:T(1024)S(1)}, f32[891]{0:T(1024)S(1)}, u32[]{:S(2)}, u32[]{:S(2)}) collective-permute-start(f32[891]{0:T(1024)S(1)} %select_add_fusion.9), channel_id=1, source_target_pairs={{0,16},{1,17},{2,18},{3,19},{4,20},{5,21},{6,22},{7,23},{8,24},{9,... | collective-permute-start | bytes 10700 | tf_op jit(solution)/shard_map/ppermute | solution.py:36
  121.1 4.7 %collective-permute-start.25 = (f32[4483]{0:T(1024)S(1)}, f32[4483]{0:T(1024)S(1)}, u32[]{:S(2)}, u32[]{:S(2)}) collective-permute-start(f32[4483]{0:T(1024)S(1)} %select_add_fusion.6), channel_id=1, source_target_pairs={{0,16},{1,17},{2,18},{3,19},{4,20},{5,21},{6,22},{7,23},{8,24},{9,... | collective-permute-start | bytes 53804 | tf_op jit(solution)/shard_map/ppermute | solution.py:36
  123.5 4.7 %collective-permute-start.16 = (f32[1782]{0:T(1024)S(1)}, f32[1782]{0:T(1024)S(1)}, u32[]{:S(2)}, u32[]{:S(2)}) collective-permute-start(f32[1782]{0:T(1024)S(1)} %maximum_select_fusion.9), channel_id=1, source_target_pairs={{0,8},{1,9},{2,10},{3,11},{4,12},{5,13},{6,14},{7,15},{8,0},{9,1},... | collective-permute-start | bytes 21392 | tf_op jit(solution)/shard_map/ppermute | solution.py:36
  130.2 4.4 %collective-permute-start.27 = (f32[17932]{0:T(1024)S(1)}, f32[17932]{0:T(1024)S(1)}, u32[]{:S(2)}, u32[]{:S(2)}) collective-permute-start(f32[17932]{0:T(1024)S(1)} %maximum_select_fusion.4), channel_id=1, source_target_pairs={{0,4},{1,5},{2,6},{3,7},{4,0},{5,1},{6,2},{7,3},{8,12},{9,13},{10,... | collective-permute-start | bytes 215192 | tf_op jit(solution)/shard_map/ppermute | solution.py:36
  134.8 5.2 %collective-permute-start.28 = (f32[35864]{0:T(1024)S(1)}, f32[35864]{0:T(1024)S(1)}, u32[]{:S(2)}, u32[]{:S(2)}) collective-permute-start(f32[35864]{0:T(1024)S(1)} %maximum_select_fusion.2), channel_id=1, source_target_pairs={{0,2},{1,3},{2,0},{3,1},{4,6},{5,7},{6,4},{7,5},{8,10},{9,11},{10,... | collective-permute-start | bytes 430376 | tf_op jit(solution)/shard_map/ppermute | solution.py:36
  (35 other events, 247.9 us)
